TPU v7x, 256 devices: a whole 4x4x8 slice. The times are simulated.
256 devices in a mesh: req: 2 (over core), seq: 16 (over y, x), tp: 8 (over z).
Axes of the slice: x: 4, y: 4, z: 8, core: 2. Of those that a mesh axis runs over, the one named last changes fastest.
Arguments:
- queries: bfloat16 [4, 512, 3072], P('req', 'seq', 'tp'), may hold values from -48 to 48
- new_kv: bfloat16 [4, 512, 2, 3072], P('req', 'seq', None, 'tp'), may hold values from -4 to 4
- cache_kv: bfloat16 [4, 16384, 2, 3072], P('req', 'seq', None, 'tp'), may hold values from -4 to 4
- cached_len: int32 [4], P('req'), may hold values from 1 to 16384, as said below
- residual_in: bfloat16 [4, 512, 3072], P('req', 'seq', 'tp'), may hold values from -1.5 to 1.5
- norm_gain: float32 [3072], replicated, may hold values from 0.1 to 1.9
- gate_w: bfloat16 [3072, 4096], P(None, 'tp'), may hold values from -0.109375 to 0.109375
- up_w: bfloat16 [3072, 4096], P(None, 'tp'), may hold values from -0.109375 to 0.109375
- down_w: bfloat16 [4096, 3072], P('tp'), may hold values from -0.09375 to 0.09375
- owner: int32 [32, 64, 1], P(('req', 'seq')), may hold values from 0 to 31; in each aligned block of 64 rows (0 to 63, 64 to 127, ..., all dimensions but the last counted through in order) at most 4 rows name the same one
Outputs:
- layer_out: bfloat16 [32, 32, 4, 3072], P(('req', 'seq'), None, None, 'tp')
Inputs may be any that keep to these rules, and one draw needn't show every extreme that they name: `cached_len`: exactly 1 request have 16384 - 16384 // 8 cached positions or more, one of them exactly 16384; every other request has at most 1024. Within one row block no owner is named by more than 4 rows.
All inputs are finite; a program needn't handle non-finite values.
Results may differ from a plain program's by a relative error of at most 0.02.
Values may be sent and summed in bfloat16 or wider, within the bound.
No kernel may reach another device: no remote copies, remote signals or barrier semaphores. Data moves between devices by JAX's collectives and lax.ppermute only.
A program may use at most 256 MiB of HBM per device.

v0:
```python
import jax
import jax.numpy as jnp
from jax import lax
from jax.sharding import PartitionSpec as P

HEAD = 96


masked_floor = -1e30


def block_stats(query_heads, key_heads, value_heads, visible):
    scores = jnp.einsum(
        "qhd,khd->qhk", query_heads, key_heads, preferred_element_type=jnp.float32
    ) * HEAD ** (-0.5)
    visible_heads = visible[:, None, :]
    masked = jnp.where(visible_heads, scores, masked_floor)
    row_peak = jnp.max(masked, axis=-1)
    weights = jnp.where(visible_heads, jnp.exp(masked - row_peak[..., None]), 0.0)
    row_total = jnp.sum(weights, axis=-1)
    weighted = jnp.einsum(
        "qhk,khd->qhd",
        weights.astype(jnp.bfloat16),
        value_heads,
        preferred_element_type=jnp.float32,
    )
    return (row_peak, row_total, weighted.reshape(weighted.shape[0], -1))


def slot_partial(query_slot, cached_slot, fresh_slot, length, seq_index):
    query_count = query_slot.shape[0]
    head_count = query_slot.shape[1] // HEAD
    query_heads = query_slot.reshape(query_count, head_count, HEAD)
    positions = jnp.arange(query_count, dtype=jnp.int32)
    fresh_count = fresh_slot.shape[0]
    fresh_index = seq_index * fresh_count + jnp.arange(fresh_count, dtype=jnp.int32)
    fresh_visible = fresh_index[None, :] <= positions[:, None]
    shard_span = cached_slot.shape[0]
    shard_offset = seq_index * shard_span
    key_total = shard_span + fresh_count
    keys_all = jnp.concatenate([cached_slot[:, 0], fresh_slot[:, 0]], axis=0).reshape(
        key_total, head_count, HEAD
    )
    values_all = jnp.concatenate([cached_slot[:, 1], fresh_slot[:, 1]], axis=0).reshape(
        key_total, head_count, HEAD
    )
    cached_index = shard_offset + jnp.arange(shard_span, dtype=jnp.int32)
    cached_visible = jnp.broadcast_to((cached_index < length)[None, :], (query_count, shard_span))
    visible = jnp.concatenate([cached_visible, fresh_visible], axis=1)
    return block_stats(query_heads, keys_all, values_all, visible)


def normalize(features, norm_gain):
    values = features.astype(jnp.float32)
    mean_square = jnp.mean(values * values, axis=-1, keepdims=True)
    return (values * lax.rsqrt(mean_square + 1e-05) * norm_gain).astype(jnp.bfloat16)


def per_device(
    queries, new_kv, cache_kv, cached_len, residual_in, norm_gain, gate_w, up_w, down_w, owner
):
    slot_count, token_count, width_local = queries.shape
    seq_index = lax.axis_index("seq")
    all_queries = lax.all_gather(queries, "seq", axis=1, tiled=True)
    partials = [
        slot_partial(
            all_queries[slot_number],
            cache_kv[slot_number],
            new_kv[slot_number],
            cached_len[slot_number],
            seq_index,
        )
        for slot_number in range(slot_count)
    ]
    row_peak = jnp.stack([partial_item[0] for partial_item in partials])
    row_total = jnp.stack([partial_item[1] for partial_item in partials])
    weighted = jnp.stack([partial_item[2] for partial_item in partials])
    pieces = (
        lax.all_to_all(row_peak[None], "seq", split_axis=2, concat_axis=0, tiled=True),
        lax.all_to_all(row_total[None], "seq", split_axis=2, concat_axis=0, tiled=True),
        lax.all_to_all(weighted[None], "seq", split_axis=2, concat_axis=0, tiled=True),
    )
    source_peak, source_total, source_sum = pieces
    joint_peak = jnp.max(source_peak, axis=0)
    source_scale = jnp.exp(source_peak - joint_peak[None])
    own_total = jnp.sum(source_total * source_scale, axis=0)
    grouped = source_sum.reshape(source_sum.shape[:-1] + (source_peak.shape[-1], HEAD))
    own_sum = jnp.sum(grouped * source_scale[..., None], axis=0).reshape(source_sum.shape[1:])
    head_count = width_local // HEAD
    attention = (
        own_sum.reshape(slot_count, token_count, head_count, HEAD) / own_total[..., None]
    ).reshape(slot_count, token_count, width_local)
    stream = (residual_in.astype(jnp.float32) + attention).astype(jnp.bfloat16)
    stream_rows = stream.reshape(slot_count * token_count, width_local)
    owner_ids = owner.reshape(-1)
    owner_count = lax.axis_size(("req", "seq"))
    row_count = owner_ids.shape[0]
    slot_cap = max(2, 2 * row_count // owner_count)
    matches = (owner_ids[:, None] == jnp.arange(owner_count, dtype=jnp.int32)[None, :]).astype(
        jnp.int32
    )
    ranking = jnp.sum(jnp.cumsum(matches, axis=0) * matches, axis=1) - 1
    outgoing = (
        jnp.zeros((owner_count * slot_cap, width_local), jnp.bfloat16)
        .at[owner_ids * slot_cap + ranking]
        .set(stream_rows)
    )
    incoming = lax.all_to_all(
        outgoing.reshape(owner_count, slot_cap, width_local),
        ("req", "seq"),
        split_axis=0,
        concat_axis=0,
        tiled=True,
    )
    arrived = incoming.reshape(owner_count * slot_cap, width_local)
    full_rows = lax.all_gather(arrived, "tp", axis=1, tiled=True)
    normed = normalize(full_rows, norm_gain)
    gate_out = jnp.dot(normed, gate_w, preferred_element_type=jnp.float32)
    up_out = jnp.dot(normed, up_w, preferred_element_type=jnp.float32)
    hidden = (jax.nn.silu(gate_out) * up_out).astype(jnp.bfloat16)
    partial_sum = jnp.dot(hidden, down_w, preferred_element_type=jnp.float32)
    unit_share = lax.psum_scatter(
        partial_sum.astype(jnp.bfloat16), "tp", scatter_dimension=1, tiled=True
    ).astype(jnp.float32)
    result = (arrived.astype(jnp.float32) + unit_share).astype(jnp.bfloat16)
    return result.reshape(1, owner_count, slot_cap, width_local)


def solution(mesh):
    return jax.shard_map(
        per_device,
        mesh=mesh,
        in_specs=(
            P("req", "seq", "tp"),
            P("req", "seq", None, "tp"),
            P("req", "seq", None, "tp"),
            P("req"),
            P("req", "seq", "tp"),
            P(),
            P(None, "tp"),
            P(None, "tp"),
            P("tp", None),
            P(("req", "seq"), None, None),
        ),
        out_specs=P(("req", "seq"), None, None, "tp"),
        check_vma=False,
    )
```

profile of v0, /device:TPU:2, one launch (start us, length us, event | category | flops | bytes accessed | tf_op | source)
XLA Modules:
  0.0 262.6 jit_solution(4247062035156930165)
XLA Ops:
  6.5 1.4 fusion.65
  8.0 1.3 fusion.45
  10.5 0.9 slice_bitcast_fusion.3
  13.7 24.4 %all_gather.6 = bf16[2,512,384]{2,1,0:T(8,128)(2,1)S(1)} all-gather(bf16[2,32,384]{2,1,0:T(8,128)(2,1)} %param.10), channel_id=1, replica_groups=mesh['req'=2,'seq'=16,'tp'=8] {'seq'}, dimensions={1}, use_global_device_ids=true | all-gather | bytes 835584 | tf_op jit(solution)/shard_map/all_gather | solution.py:64
  38.9 1.9 copy.57
  40.8 0.9 copy.62
  41.8 3.9 %slice_bitcast_fusion.1 = (bf16[1024,2,384]{2,1,0:T(2,128)(2,1)S(1)}, bf16[1024,2,384]{2,1,0:T(2,128)(2,1)S(1)}) fusion(bf16[2,1024,2,384]{3,2,1,0:T(2,128)(2,1)} %param.12), kind=kLoop, calls=%fused_computation.26 | loop fusion | bytes 6291456 | tf_op jit(solution)/shard_map/squeeze | solution.py:68
  45.6 6.3 %fusion.60 = (bf16[1024,1,384]{2,1,0:T(2,128)(2,1)}, bf16[1024,1,384]{2,1,0:T(2,128)(2,1)}, bf16[1024,1,384]{2,1,0:T(2,128)(2,1)}, bf16[1024,1,384]{2,1,0:T(2,128)(2,1)}) fusion(bf16[1024,2,384]{2,1,0:T(2,128)(2,1)S(1)} %get-tuple-element.7, bf16[1024,2,384]{2,1,0:T(2,128)(2,1)S(1)} %get-tuple-element.8), kind=kLoop, calls=%fused_computation.86 | loop fusion | bytes 6291456 | tf_op jit(solution)/shard_map/slice | solution.py:44
  51.9 4.7 %copy.55 = bf16[1024,1,384]{0,2,1:T(8,128)(2,1)} copy(bf16[1024,1,384]{2,1,0:T(2,128)(2,1)} %get-tuple-element.10) | data formatting | bytes 1572864 | tf_op jit(solution)/shard_map/slice | solution.py:41
  56.6 4.7 %copy.60 = bf16[1024,1,384]{0,2,1:T(8,128)(2,1)} copy(bf16[1024,1,384]{2,1,0:T(2,128)(2,1)} %get-tuple-element.33) | data formatting | bytes 1572864 | tf_op jit(solution)/shard_map/slice | solution.py:41
  61.3 1.8 pad_add_fusion.1
  63.2 6.7 %fusion.1 = (f32[512,4]{0,1:T(4,128)S(1)}, f32[4,1056,512]{2,1,0:T(8,128)}) fusion(pred[512,1056]{0,1:T(8,128)(4,1)S(1)} %get-tuple-element.22, bf16[512,4,96]{0,2,1:T(8,128)(2,1)S(1)} %bitcast.116, bf16[32,4,96]{0,2,1:T(8,128)(2,1)} %bitcast.118, bf16[1024,4,96]{0,2,1:T(8,128)(2,1)} %bitcast.114), kind=kOutput, calls=%fused_computation.6 | convolution fusion | flops 423344128 | bytes 10403840 | tf_op jit(solution)/shard_map/qhd,khd->qhk/dot_general | solution.py:13
  69.9 5.2 %fusion = (f32[512,4]{0,1:T(4,128)S(1)}, f32[4,1056,512]{2,1,0:T(8,128)}) fusion(pred[512,1056]{0,1:T(8,128)(4,1)S(1)} %get-tuple-element.21, bf16[512,4,96]{0,2,1:T(8,128)(2,1)S(1)} %bitcast.115, bf16[32,4,96]{0,2,1:T(8,128)(2,1)S(1)} %bitcast.117, bf16[1024,4,96]{0,2,1:T(8,128)(2,1)S(1)} %bitcast.112), kind=kOutput, calls=%fused_computation.5 | convolution fusion | flops 423344128 | bytes 10403840 | tf_op jit(solution)/shard_map/qhd,khd->qhk/dot_general | solution.py:13
  75.1 1.0 copy.66
  76.1 1.9 bitcast_bitcast_fusion.1
  78.0 2.4 reshape.128
  80.3 5.7 %all-to-all-start.1 = ((f32[16,1,256]{2,1,0:T(1,128)}), f32[16,1,256]{2,1,0:T(1,128)S(1)}, u32[]{:S(2)}, u32[]{:S(2)}) async-start(f32[16,1,256]{2,1,0:T(1,128)} %reshape.128), calls=%async_computation.1 | async-start | bytes 32768 | tf_op jit(solution)/shard_map/all_to_all | solution.py:79
  86.9 4.7 %copy.53 = bf16[1024,1,384]{0,2,1:T(8,128)(2,1)} copy(bf16[1024,1,384]{2,1,0:T(2,128)(2,1)} %get-tuple-element.9) | data formatting | bytes 1572864 | tf_op jit(solution)/shard_map/slice | solution.py:44
  91.6 4.7 %copy.58 = bf16[1024,1,384]{0,2,1:T(8,128)(2,1)} copy(bf16[1024,1,384]{2,1,0:T(2,128)(2,1)} %get-tuple-element.34) | data formatting | bytes 1572864 | tf_op jit(solution)/shard_map/slice | solution.py:44
  96.3 4.8 %fusion.4 = f32[512,4]{0,1:T(4,128)S(1)} fusion(f32[4,1056,512]{2,1,0:T(8,128)} %get-tuple-element.26, f32[512,4]{0,1:T(4,128)S(1)} %get-tuple-element.25, pred[512,1056]{0,1:T(8,128)(4,1)} %copy-done.7), kind=kLoop, calls=%fused_computation.9 | loop fusion | flops 10811392 | bytes 9207808 | tf_op jit(solution)/shard_map/reduce_sum | solution.py:20
  101.1 1.3 copy-done.1
  102.5 2.2 fusion.2
  104.7 1.0 copy.69
  105.7 7.5 %fusion.6 = f32[4,96,512]{2,1,0:T(8,128)} fusion(f32[4,1056,512]{2,1,0:T(8,128)} %get-tuple-element.26, f32[512,4]{0,1:T(4,128)S(1)} %get-tuple-element.25, pred[512,1056]{0,1:T(8,128)(4,1)} %copy-done.7, bf16[32,4,96]{0,2,1:T(8,128)(2,1)} %bitcast.120, bf16[1024,4,96]{0,2,1:T(8,128)(2,1)} %bitcast.113), kind=kOutput, calls=%fused_computation.11 | convolution fusion | flops 427671552 | bytes 10797056 | tf_op jit(solution)/shard_map/qhk,khd->qhd/dot_general | solution.py:21
  113.3 3.7 %fusion.8 = f32[4,96,512]{2,1,0:T(8,128)} fusion(f32[4,1056,512]{2,1,0:T(8,128)S(1)} %bitcast.104, f32[512,4]{0,1:T(4,128)S(1)} %get-tuple-element.27, pred[512,1056]{0,1:T(8,128)(4,1)S(1)} %copy-done.6, bf16[32,4,96]{0,2,1:T(8,128)(2,1)S(1)} %bitcast.119, bf16[1024,4,96]{0,2,1:T(8,128)(2,1)S(1)} %bitcast.111), kind=kOutput, calls=%fused_computation.12 | convolution fusion | flops 427671552 | bytes 10797056 | tf_op jit(solution)/shard_map/qhk,khd->qhd/dot_general | solution.py:21
  117.8 3.1 %copy.64 = f32[1,512,384]{2,0,1:T(1,128)} copy(f32[1,512,384]{1,2,0:T(8,128)} %bitcast.109) | data formatting | bytes 1572864 | tf_op jit(solution)/shard_map/stack;reshape | solution.py:77
  120.9 3.0 %copy.63 = f32[1,512,384]{2,0,1:T(1,128)} copy(f32[1,512,384]{1,2,0:T(8,128)} %bitcast.110) | data formatting | bytes 1572864 | tf_op jit(solution)/shard_map/stack;reshape | solution.py:77
  123.9 2.4 reshape.130
  126.3 7.2 %all-to-all-start.2 = ((f32[16,1,256]{2,1,0:T(1,128)}), f32[16,1,256]{2,1,0:T(1,128)S(1)}, u32[]{:S(2)}, u32[]{:S(2)}) async-start(f32[16,1,256]{2,1,0:T(1,128)} %reshape.130), calls=%async_computation.2 | async-start | bytes 32768 | tf_op jit(solution)/shard_map/all_to_all | solution.py:80
  133.5 3.9 %maximum_bitcast_fusion = f32[1,2,512,384]{3,1,0,2:T(2,128)} fusion(f32[1,512,384]{2,0,1:T(1,128)} %copy.64, f32[1,512,384]{2,0,1:T(1,128)} %copy.63), kind=kLoop, calls=%fused_computation.23 | loop fusion | flops 393216 | bytes 3145728 | tf_op jit(solution)/shard_map/broadcast_in_dim | solution.py:81
  137.4 2.3 all-to-all-done.2
  139.7 5.6 %all-to-all-start = ((f32[1,2,512,384]{3,1,0,2:T(2,128)}), f32[1,2,512,384]{3,1,0,2:T(2,128)}, u32[]{:S(2)}, u32[]{:S(2)}) async-start(f32[1,2,512,384]{3,1,0,2:T(2,128)} %maximum_bitcast_fusion), calls=%async_computation | async-start | bytes 3145728 | tf_op jit(solution)/shard_map/all_to_all | solution.py:81
  147.2 1.6 reshape.129
  148.8 1.3 copy.67
  150.8 1.6 reshape.131
  152.4 1.3 copy.70
  154.2 1.1 copy.68
  155.2 3.2 %mul.89 = f32[16,2,32,4,96]{4,3,2,0,1:T(4,128)} broadcast(f32[16,2,32,4]{3,2,0,1:T(8,128)} %copy.68), dimensions={0,1,2,3} | broadcast | bytes 1589248 | tf_op jit(solution)/shard_map/mul | solution.py:88
  158.4 3.2 %mul.90 = f32[16,1,2,32,384]{4,3,0,2,1:T(8,128)} reshape(f32[16,2,32,4,96]{4,3,2,0,1:T(4,128)} %mul.89) | data formatting | bytes 3145728 | tf_op jit(solution)/shard_map/mul | solution.py:88
  161.6 1.6 copy.65
  163.8 0.9 scatter_custom_fusion
  164.7 13.5 %all_to_all.56 = bf16[32,4,384]{2,1,0:T(4,128)(2,1)S(1)} all-to-all(bf16[32,4,384]{2,1,0:T(4,128)(2,1)S(1)} %reshape.111), channel_id=1, replica_groups=mesh['req'=2,'seq'=16,'tp'=8] {'req','seq'}, dimensions={0} | all-to-all | bytes 196608 | tf_op jit(solution)/shard_map/all_to_all | solution.py:108
  178.3 30.0 %all_gather.7 = bf16[128,3072]{1,0:T(8,128)(2,1)S(1)} all-gather(bf16[128,384]{1,0:T(8,128)(2,1)S(1)} %reshape.112), channel_id=1, replica_groups=mesh['req'=2,'seq'=16,'tp'=8] {'tp'}, dimensions={1}, use_global_device_ids=true | all-gather | bytes 884736 | tf_op jit(solution)/shard_map/all_gather | solution.py:116
  209.2 3.2 %fusion.37 = f32[128,512]{1,0:T(8,128)} fusion(bf16[3072,512]{1,0:T(8,128)(2,1)} %param.16, bf16[128,3072]{1,0:T(8,128)(2,1)S(1)} %all_gather.7, f32[3072]{0:T(1024)S(1)} %copy-done.18, f32[128]{0:T(128)S(1)} %add_rsqrt_fusion), kind=kOutput, calls=%fused_computation.48 | convolution fusion | flops 404226048 | bytes 4207104 | tf_op jit(solution)/shard_map/dot_general | solution.py:118
  212.4 4.2 %convolution_convert_fusion = bf16[128,3072]{1,0:T(8,128)(2,1)} fusion(bf16[512,3072]{1,0:T(8,128)(2,1)S(1)} %copy-done, bf16[3072,512]{1,0:T(8,128)(2,1)} %param.17, f32[128,512]{1,0:T(8,128)} %fusion.37, bf16[128,3072]{1,0:T(8,128)(2,1)} %copy-done.3, f32[3072]{0:T(1024)S(1)} %copy-done.18, f32[128]{0:T(128)S(1)} %add_rsqrt_fusion), kind=kOutput, calls=%fused_computation.15 | convolution fusion | flops 807665664 | bytes 8139264 | tf_op jit(solution)/shard_map/dot_general | solution.py:121
  216.6 2.3 copy.72
  218.9 35.1 %reduce-scatter.4.cloned.1.call-done = bf16[384,128]{1,0:T(8,128)(2,1)} async-done(((bf16[3072,128]{1,0:T(8,128)(2,1)}), bf16[384,128]{1,0:T(8,128)(2,1)}) %reduce-scatter.4.cloned.1.call-update) | async-done | bytes 98320
  254.1 1.0 copy.73
  (81 shorter events, 11.4 us)
Async XLA Ops:
  6.5 205.9 %copy-start = (bf16[512,3072]{1,0:T(8,128)(2,1)S(1)}, bf16[512,3072]{1,0:T(8,128)(2,1)}, u32[]{:S(2)}) copy-start(bf16[512,3072]{1,0:T(8,128)(2,1)} %param.18) | copy-start | bytes 9437188
  51.9 11.2 %copy-start.12 = (bf16[1,512,384]{1,2,0:T(8,128)(2,1)S(1)}, bf16[1,512,384]{1,2,0:T(8,128)(2,1)}, u32[]{:S(2)}) copy-start(bf16[1,512,384]{1,2,0:T(8,128)(2,1)} %copy.62) | copy-start | bytes 1179652
  63.1 6.8 %copy-start.7 = (pred[512,1056]{0,1:T(8,128)(4,1)}, pred[512,1056]{0,1:T(8,128)(4,1)S(1)}, u32[]{:S(2)}) copy-start(pred[512,1056]{0,1:T(8,128)(4,1)S(1)} %get-tuple-element.22) | copy-start | bytes 1622020
  63.1 6.8 %copy-start.4 = (pred[512,1056]{0,1:T(8,128)(4,1)}, pred[512,1056]{0,1:T(8,128)(4,1)S(1)}, u32[]{:S(2)}) copy-start(pred[512,1056]{0,1:T(8,128)(4,1)S(1)} %get-tuple-element.21) | copy-start | bytes 1622020
  63.1 6.7 %copy-start.10 = (bf16[1024,1,384]{0,2,1:T(8,128)(2,1)S(1)}, bf16[1024,1,384]{0,2,1:T(8,128)(2,1)}, u32[]{:S(2)}) copy-start(bf16[1024,1,384]{0,2,1:T(8,128)(2,1)} %copy.55) | copy-start | bytes 2359300
  63.1 6.7 %copy-start.11 = (bf16[1,512,384]{1,2,0:T(8,128)(2,1)S(1)}, bf16[1,512,384]{1,2,0:T(8,128)(2,1)}, u32[]{:S(2)}) copy-start(bf16[1,512,384]{1,2,0:T(8,128)(2,1)} %copy.57) | copy-start | bytes 1179652
  63.1 6.7 %copy-start.15 = (bf16[32,1,384]{0,2,1:T(8,128)(2,1)S(1)}, bf16[32,1,384]{0,2,1:T(8,128)(2,1)}, u32[]{:S(2)}) copy-start(bf16[32,1,384]{0,2,1:T(8,128)(2,1)} %copy.56) | copy-start | bytes 73732
  69.9 16.1 %copy-start.14 = (bf16[32,1,384]{2,1,0:T(2,128)(2,1)S(1)}, bf16[32,1,384]{2,1,0:T(2,128)(2,1)}, u32[]{:S(2)}) copy-start(bf16[32,1,384]{2,1,0:T(2,128)(2,1)} %get-tuple-element.17) | copy-start | bytes 73732
  69.9 16.3 %copy-start.13 = (bf16[32,1,384]{2,1,0:T(2,128)(2,1)S(1)}, bf16[32,1,384]{2,1,0:T(2,128)(2,1)}, u32[]{:S(2)}) copy-start(bf16[32,1,384]{2,1,0:T(2,128)(2,1)} %get-tuple-element.32) | copy-start | bytes 73732
  80.3 45.9 %all-to-all-start.1 = ((f32[16,1,256]{2,1,0:T(1,128)}), f32[16,1,256]{2,1,0:T(1,128)S(1)}, u32[]{:S(2)}, u32[]{:S(2)}) async-start(f32[16,1,256]{2,1,0:T(1,128)} %reshape.128), calls=%async_computation.1 | async-start | bytes 32768 | tf_op jit(solution)/shard_map/all_to_all | solution.py:79
  96.3 6.1 %copy-start.1 = (f32[4,1056,512]{2,1,0:T(8,128)S(1)}, f32[4,1056,512]{2,1,0:T(8,128)}, u32[]{:S(2)}) copy-start(f32[4,1056,512]{2,1,0:T(8,128)} %get-tuple-element.28) | copy-start | bytes 25952260
  96.3 6.2 %copy-start.5 = (pred[512,1056]{0,1:T(8,128)(4,1)S(1)}, pred[512,1056]{0,1:T(8,128)(4,1)}, u32[]{:S(2)}) copy-start(pred[512,1056]{0,1:T(8,128)(4,1)} %copy-done.4) | copy-start | bytes 1622020
  104.6 8.6 %slice-start = ((s8[8650752]{0:T(1024)(128)(4,1)}), s8[262144]{0:T(1024)(128)(4,1)S(1)}, s32[]{:S(2)}) async-start(s8[8650752]{0:T(1024)(128)(4,1)} %bitcast.103), calls=%async_computation.6 | async-start | bytes 524288
  105.7 7.5 %slice-start.1 = ((s8[8650752]{0:T(1024)(128)(4,1)}), s8[4194304]{0:T(1024)(128)(4,1)S(1)}, s32[]{:S(2)}) async-start(s8[8650752]{0:T(1024)(128)(4,1)} %bitcast.103), calls=%async_computation.7 | async-start | bytes 8388608
  105.7 7.5 %slice-start.2 = ((s8[8650752]{0:T(1024)(128)(4,1)}), s8[4194304]{0:T(1024)(128)(4,1)S(1)}, s32[]{:S(2)}) async-start(s8[8650752]{0:T(1024)(128)(4,1)} %bitcast.103), calls=%async_computation.8 | async-start | bytes 8388608
  105.7 7.5 %copy-start.6 = (pred[512,1056]{0,1:T(8,128)(4,1)S(1)}, pred[512,1056]{0,1:T(8,128)(4,1)}, u32[]{:S(2)}) copy-start(pred[512,1056]{0,1:T(8,128)(4,1)} %copy-done.4) | copy-start | bytes 1622020
  105.7 7.5 %copy-start.9 = (bf16[1024,1,384]{0,2,1:T(8,128)(2,1)S(1)}, bf16[1024,1,384]{0,2,1:T(8,128)(2,1)}, u32[]{:S(2)}) copy-start(bf16[1024,1,384]{0,2,1:T(8,128)(2,1)} %copy.53) | copy-start | bytes 2359300
  113.2 3.7 %copy-start.8 = (f32[2,512,4]{2,0,1:T(2,128)S(1)}, f32[2,512,4]{2,0,1:T(2,128)}, u32[]{:S(2)}) copy-start(f32[2,512,4]{2,0,1:T(2,128)} %copy.69) | copy-start | bytes 49156
  126.3 13.5 %all-to-all-start.2 = ((f32[16,1,256]{2,1,0:T(1,128)}), f32[16,1,256]{2,1,0:T(1,128)S(1)}, u32[]{:S(2)}, u32[]{:S(2)}) async-start(f32[16,1,256]{2,1,0:T(1,128)} %reshape.130), calls=%async_computation.2 | async-start | bytes 32768 | tf_op jit(solution)/shard_map/all_to_all | solution.py:80
  133.5 12.1 %copy-start.17 = (s32[1,64,1]{1,2,0:T(1,128)S(1)}, s32[1,64,1]{1,2,0:T(1,128)}, u32[]{:S(2)}) copy-start(s32[1,64,1]{1,2,0:T(1,128)} %param.19) | copy-start | bytes 772
  139.7 21.9 %all-to-all-start = ((f32[1,2,512,384]{3,1,0,2:T(2,128)}), f32[1,2,512,384]{3,1,0,2:T(2,128)}, u32[]{:S(2)}, u32[]{:S(2)}) async-start(f32[1,2,512,384]{3,1,0,2:T(2,128)} %maximum_bitcast_fusion), calls=%async_computation | async-start | bytes 3145728 | tf_op jit(solution)/shard_map/all_to_all | solution.py:81
  145.3 108.8 %reduce-scatter.4.cloned.1.call-start = ((), (), s32[]{:S(2)}) async-start(), calls=%async_computation.5 | async-start | bytes 884736
  161.6 2.2 copy-start.16
  161.6 1.9 copy-start.2
  163.3 45.9 %copy-start.18 = (f32[3072]{0:T(1024)S(1)}, f32[3072]{0:T(1024)}, u32[]{:S(2)}) copy-start(f32[3072]{0:T(1024)} %param.15) | copy-start | bytes 36868
  208.3 0.9 copy-start.3
Sparse Core Ops, SparseCore 0:
  219.1 34.9 reduce-scatter.3
where the time goes:
time: 264 us; the launch traced here: 263 us
  local copies, waits for them, and re-layouts  77.8 us (29%)
  blocking collectives  67.9 us (26%)
  waiting for transfers between devices  37.4 us (14%)
  matrix products  30.5 us (12%)
  starting transfers between devices  18.7 us (7%)
  other arithmetic  16.4 us (6%)
  between operations  13.7 us (5%)
    unnamed x2, waiting for transfers between devices  35.1 us
    all_gather x1, blocking collectives, per_device(): full_rows = lax.all_gather(arrived, 'tp', axis=1, tiled=True)  30 us
    all_gather x1, blocking collectives, per_device(): all_queries = lax.all_gather(queries, 'seq', axis=1, tiled=True)  24.4 us
    unnamed x52, local copies, waits for them, and re-layouts  16.3 us
    slice x3, local copies, waits for them, and re-layouts, slot_partial(): cached_slot[:, 1]  15.6 us
    all_to_all x1, blocking collectives, per_device(): lax.all_to_all(outgoing.reshape(owner_count, slot_cap, width_local), ('re...  13.5 us
    dot_general x2, matrix products, block_stats(): jnp.einsum('qhd,khd->qhk', query_heads, key_heads, preferred_element_type...  11.9 us
    dot_general x2, matrix products, block_stats(): jnp.einsum('qhk,khd->qhd', weights.astype(jnp.bfloat16), value_heads, pre...  11.2 us
  transfers between devices with their start and end apart: 4, of which 2 were waited for; matrix products, arithmetic and copies ran while one was open for 22% of the time, Pallas kernels for 0%

commit v1 on v0

v1 whole, which is shorter than its diff:
```python
import functools

import jax
import jax.numpy as jnp
from jax import lax
from jax.experimental import pallas as pl
from jax.experimental.pallas import tpu as pltpu
from jax.sharding import PartitionSpec as P

HEAD = 96

masked_floor = -1e30

STAT_LANES = 128
TOTAL_LANE = 8


def attention_kernel(meta_ref, q_ref, kc_ref, vc_ref, kf_ref, vf_ref, out_ref, *, tq, heads):
    slot = pl.program_id(0)
    q_block = pl.program_id(1)
    seq_index = meta_ref[0]
    length = meta_ref[1 + slot]
    span = kc_ref.shape[0]
    fresh_count = kf_ref.shape[0]
    width = q_ref.shape[1]
    offset = seq_index * span
    scale = HEAD ** (-0.5)

    q = q_ref[...]
    lane = lax.broadcasted_iota(jnp.int32, (1, width), 1)
    stat_lane = lax.broadcasted_iota(jnp.int32, (1, STAT_LANES), 1)
    rows = q_block * tq + lax.broadcasted_iota(jnp.int32, (tq, 1), 0)
    fresh_cols = seq_index * fresh_count + lax.broadcasted_iota(jnp.int32, (1, fresh_count), 1)
    fresh_visible = fresh_cols <= rows
    cached_visible = (offset + lax.broadcasted_iota(jnp.int32, (1, span), 1)) < length
    contract = (((1,), (1,)), ((), ()))

    def run(with_cache):
        kf = kf_ref[...]
        vf = vf_ref[...]
        if with_cache:
            kc = kc_ref[...]
            vc = vc_ref[...]
        weighted = jnp.zeros((tq, width), jnp.float32)
        stats = jnp.zeros((tq, STAT_LANES), jnp.float32)
        for h in range(heads):
            head_lanes = (lane >= h * HEAD) & (lane < (h + 1) * HEAD)
            qh = jnp.where(head_lanes, q, jnp.zeros_like(q))
            sf = lax.dot_general(qh, kf, contract, preferred_element_type=jnp.float32) * scale
            sf = jnp.where(fresh_visible, sf, masked_floor)
            peak = jnp.max(sf, axis=-1, keepdims=True)
            if with_cache:
                sc = lax.dot_general(qh, kc, contract, preferred_element_type=jnp.float32) * scale
                sc = jnp.where(cached_visible, sc, masked_floor)
                peak = jnp.maximum(peak, jnp.max(sc, axis=-1, keepdims=True))
            pf = jnp.where(fresh_visible, jnp.exp(sf - peak), 0.0)
            total = jnp.sum(pf, axis=-1, keepdims=True)
            oh = jnp.dot(pf.astype(jnp.bfloat16), vf, preferred_element_type=jnp.float32)
            if with_cache:
                pc = jnp.where(cached_visible, jnp.exp(sc - peak), 0.0)
                total = total + jnp.sum(pc, axis=-1, keepdims=True)
                oh = oh + jnp.dot(pc.astype(jnp.bfloat16), vc, preferred_element_type=jnp.float32)
            weighted = jnp.where(head_lanes, oh, weighted)
            stats = jnp.where(stat_lane == h, peak, stats)
            stats = jnp.where(stat_lane == TOTAL_LANE + h, total, stats)
        out_ref[:, :width] = weighted
        out_ref[:, width:] = stats

    @pl.when(offset < length)
    def _():
        run(True)

    @pl.when(offset >= length)
    def _():
        run(False)


def local_attention(all_queries, cache_kv, new_kv, cached_len, seq_index):
    slot_count, query_count, width = all_queries.shape
    span = cache_kv.shape[1]
    fresh_count = new_kv.shape[1]
    heads = width // HEAD
    tq = 256 if query_count % 256 == 0 else query_count
    cache2 = cache_kv.reshape(slot_count, span, 2 * width)
    fresh2 = new_kv.reshape(slot_count, fresh_count, 2 * width)
    meta = jnp.concatenate([jnp.reshape(seq_index, (1,)).astype(jnp.int32), cached_len.astype(jnp.int32)])
    kernel = functools.partial(attention_kernel, tq=tq, heads=heads)
    grid_spec = pltpu.PrefetchScalarGridSpec(
        num_scalar_prefetch=1,
        grid=(slot_count, query_count // tq),
        in_specs=[
            pl.BlockSpec((None, tq, width), lambda s, b, m: (s, b, 0)),
            pl.BlockSpec((None, span, width), lambda s, b, m: (s, 0, 0)),
            pl.BlockSpec((None, span, width), lambda s, b, m: (s, 0, 1)),
            pl.BlockSpec((None, fresh_count, width), lambda s, b, m: (s, 0, 0)),
            pl.BlockSpec((None, fresh_count, width), lambda s, b, m: (s, 0, 1)),
        ],
        out_specs=pl.BlockSpec((None, tq, width + STAT_LANES), lambda s, b, m: (s, b, 0)),
    )
    return pl.pallas_call(
        kernel,
        grid_spec=grid_spec,
        out_shape=jax.ShapeDtypeStruct((slot_count, query_count, width + STAT_LANES), jnp.float32),
    )(meta, all_queries, cache2, cache2, fresh2, fresh2)


def normalize(features, norm_gain):
    values = features.astype(jnp.float32)
    mean_square = jnp.mean(values * values, axis=-1, keepdims=True)
    return (values * lax.rsqrt(mean_square + 1e-05) * norm_gain).astype(jnp.bfloat16)


def per_device(
    queries, new_kv, cache_kv, cached_len, residual_in, norm_gain, gate_w, up_w, down_w, owner
):
    slot_count, token_count, width_local = queries.shape
    head_count = width_local // HEAD
    seq_index = lax.axis_index("seq")
    all_queries = lax.all_gather(queries, "seq", axis=1, tiled=True)
    packed = local_attention(all_queries, cache_kv, new_kv, cached_len, seq_index)
    source = lax.all_to_all(packed[None], "seq", split_axis=2, concat_axis=0, tiled=True)
    source_sum = source[..., :width_local]
    source_peak = source[..., width_local:width_local + head_count]
    source_total = source[..., width_local + TOTAL_LANE:width_local + TOTAL_LANE + head_count]
    joint_peak = jnp.max(source_peak, axis=0)
    source_scale = jnp.exp(source_peak - joint_peak[None])
    own_total = jnp.sum(source_total * source_scale, axis=0)
    grouped = source_sum.reshape(source_sum.shape[:-1] + (head_count, HEAD))
    own_sum = jnp.sum(grouped * source_scale[..., None], axis=0)
    attention = (own_sum / own_total[..., None]).reshape(slot_count, token_count, width_local)
    stream = (residual_in.astype(jnp.float32) + attention).astype(jnp.bfloat16)

    block_rows = stream.reshape(slot_count * token_count, width_local)
    full_rows = lax.all_gather(block_rows, "tp", axis=1, tiled=True)
    normed = normalize(full_rows, norm_gain)
    gate_out = jnp.dot(normed, gate_w, preferred_element_type=jnp.float32)
    up_out = jnp.dot(normed, up_w, preferred_element_type=jnp.float32)
    hidden = (jax.nn.silu(gate_out) * up_out).astype(jnp.bfloat16)
    partial_sum = jnp.dot(hidden, down_w, preferred_element_type=jnp.float32)
    unit_share = lax.psum_scatter(
        partial_sum.astype(jnp.bfloat16), "tp", scatter_dimension=1, tiled=True
    ).astype(jnp.float32)
    finished = (block_rows.astype(jnp.float32) + unit_share).astype(jnp.bfloat16)

    owner_ids = owner.reshape(-1)
    owner_count = lax.axis_size(("req", "seq"))
    row_count = owner_ids.shape[0]
    slot_cap = max(2, 2 * row_count // owner_count)
    matches = (owner_ids[:, None] == jnp.arange(owner_count, dtype=jnp.int32)[None, :]).astype(
        jnp.int32
    )
    ranking = jnp.sum(jnp.cumsum(matches, axis=0) * matches, axis=1) - 1
    outgoing = (
        jnp.zeros((owner_count * slot_cap, width_local), jnp.bfloat16)
        .at[owner_ids * slot_cap + ranking]
        .set(finished)
    )
    incoming = lax.all_to_all(
        outgoing.reshape(owner_count, slot_cap, width_local),
        ("req", "seq"),
        split_axis=0,
        concat_axis=0,
        tiled=True,
    )
    return incoming.reshape(1, owner_count, slot_cap, width_local)


def solution(mesh):
    return jax.shard_map(
        per_device,
        mesh=mesh,
        in_specs=(
            P("req", "seq", "tp"),
            P("req", "seq", None, "tp"),
            P("req", "seq", None, "tp"),
            P("req"),
            P("req", "seq", "tp"),
            P(),
            P(None, "tp"),
            P(None, "tp"),
            P("tp", None),
            P(("req", "seq"), None, None),
        ),
        out_specs=P(("req", "seq"), None, None, "tp"),
        check_vma=False,
    )
```

time: 264 us -> 202 us (0.77)
  the two profiles are of different devices: /device:TPU:2 before, /device:TPU:1 now
where the time goes in v1:
time: 202 us; the launch traced here: 201 us
  blocking collectives  89.7 us (44%)
  waiting for transfers between devices  40.8 us (20%)
  local copies, waits for them, and re-layouts  25.3 us (13%)
  Pallas kernels  18.6 us (9%)
  between operations  13.5 us (7%)
  matrix products  7.21 us (4%)
  other arithmetic  6.32 us (3%)
    unnamed x2, waiting for transfers between devices  40.8 us
    all_to_all x1, blocking collectives, per_device(): lax.all_to_all(packed[None], 'seq', split_axis=2, concat_axis=0, tiled=True)  25 us
    all_gather x1, blocking collectives, per_device(): full_rows = lax.all_gather(block_rows, 'tp', axis=1, tiled=True)  23 us
    all_gather x1, blocking collectives, per_device(): all_queries = lax.all_gather(queries, 'seq', axis=1, tiled=True)  22.2 us
    all_to_all x1, blocking collectives, per_device(): lax.all_to_all(outgoing.reshape(owner_count, slot_cap, width_local), ('re...  19.5 us
    pallas_call x1, Pallas kernels, local_attention(): pl.pallas_call(kernel, grid_spec=grid_spec, out_shape=jax.ShapeDtypeStruc...  18.6 us
    reshape x1, local copies, waits for them, and re-layouts, local_attention(): cache2 = cache_kv.reshape(slot_count, span, 2 * width)  8.2 us
    mul x2, local copies, waits for them, and re-layouts, per_device(): own_sum = jnp.sum(grouped * source_scale[..., None], axis=0)  6.9 us
  transfers between devices with their start and end apart: 1, of which 1 were waited for; matrix products, arithmetic and copies ran while one was open for 0% of the time, Pallas kernels for 0%

profile of v1, /device:TPU:1, one launch (start us, length us, event | category | flops | bytes accessed | tf_op | source)
XLA Modules:
  0.0 201.4 jit_solution(15171648559440616310)
XLA Ops:
  6.5 0.0 copy-start
  6.5 0.0 reduce-scatter.4.cloned.1.call-start
  6.5 0.0 copy-start.4
  6.5 0.0 copy-start.3
  6.5 0.0 copy-start.9
  6.6 8.2 %reshape.73.kc_ref.vc_ref = bf16[2,1024,768]{2,1,0:T(8,128)(2,1)} reshape(bf16[2,1024,2,384]{3,2,1,0:T(2,128)(2,1)} %param.12) | data formatting | bytes 6291456 | tf_op jit(solution)/shard_map/reshape | solution.py:84
  14.8 0.0 copy-done.4
  14.8 22.2 %all_gather.6.q_ref = bf16[2,512,384]{2,1,0:T(8,128)(2,1)} all-gather(bf16[2,32,384]{2,1,0:T(8,128)(2,1)S(1)} %copy-done.4), channel_id=1, replica_groups=mesh['req'=2,'seq'=16,'tp'=8] {'seq'}, dimensions={1}, use_global_device_ids=true | all-gather | bytes 835584 | tf_op jit(solution)/shard_map/all_gather | solution.py:119
  37.0 0.0 copy-done.3
  37.0 0.7 reshape.74.kf_ref.vf_ref
  37.7 0.0 copy-done.9
  37.7 0.6 pad_add_fusion.meta_ref
  38.3 18.6 %shard_map.100 = f32[2,512,512]{2,1,0:T(8,128)} custom-call(s32[3]{0:T(128)} %pad_add_fusion.meta_ref, bf16[2,512,384]{2,1,0:T(8,128)(2,1)} %all_gather.6.q_ref, bf16[2,1024,768]{2,1,0:T(8,128)(2,1)} %reshape.73.kc_ref.vc_ref, bf16[2,1024,768]{2,1,0:T(8,128)(2,1)} %reshape.73.kc_ref.vc_ref, bf16[2,32,768]{2,1,0:T(8,128)(2,1)} %reshape.74.kf_ref.vf_ref, ...), custom_call_target="tpu_custom_call" | custom-call | tf_op jit(solution)/shard_map/pallas_call | solution.py:100
  56.9 3.2 %copy.17 = f32[1,2,512,512]{3,1,0,2:T(2,128)S(1)} copy(f32[1,2,512,512]{3,2,1,0:T(8,128)} %bitcast.28) | data formatting | bytes 4194304 | tf_op jit(solution)/shard_map/broadcast_in_dim | solution.py:121
  60.1 25.0 %all_to_all.23 = f32[1,2,512,512]{3,1,0,2:T(2,128)S(1)} all-to-all(f32[1,2,512,512]{3,1,0,2:T(2,128)S(1)} %copy.17), channel_id=1, replica_groups=mesh['req'=2,'seq'=16,'tp'=8] {'seq'}, dimensions={2} | all-to-all | bytes 4194304 | tf_op jit(solution)/shard_map/all_to_all | solution.py:121
  85.1 0.0 copy-start.1
  85.1 0.2 slice_reduce_fusion
  85.3 1.1 copy-done.1
  86.4 0.7 fusion.5
  87.1 2.2 %mul.63 = f32[16,2,32,4,96]{4,3,1,2,0:T(4,128)} broadcast(f32[16,2,32,4]{3,1,2,0:T(2,128)S(1)} %get-tuple-element.6), dimensions={0,1,2,3} | broadcast | bytes 1589248 | tf_op jit(solution)/shard_map/mul | solution.py:129
  89.4 0.0 copy-start.5
  89.4 4.7 %mul.64 = f32[16,2,32,384]{3,1,2,0:T(2,128)} reshape(f32[16,2,32,4,96]{4,3,1,2,0:T(4,128)} %mul.63) | data formatting | bytes 3145728 | tf_op jit(solution)/shard_map/mul | solution.py:129
  94.0 0.0 copy-start.6
  94.0 3.1 %fusion = f32[2,32,384]{2,0,1:T(2,128)S(1)} fusion(f32[16,2,32,384]{3,1,2,0:T(2,128)} %mul.64, f32[16,2,32,512]{3,1,2,0:T(2,128)} %bitcast.27), kind=kLoop, calls=%fused_computation.3 | loop fusion | flops 761856 | bytes 3244032 | tf_op jit(solution)/shard_map/reduce_sum | solution.py:129
  97.2 0.1 div.21
  97.3 0.1 div.22
  97.4 0.0 copy-done.5
  97.5 0.0 copy-start.2
  97.5 0.6 copy-done.2
  98.1 23.0 %all_gather.7 = bf16[64,3072]{1,0:T(8,128)(2,1)S(1)} all-gather(bf16[64,384]{1,0:T(8,128)(2,1)S(1)} %bitcast.30), channel_id=1, replica_groups=mesh['req'=2,'seq'=16,'tp'=8] {'tp'}, dimensions={1}, use_global_device_ids=true | all-gather | bytes 442368 | tf_op jit(solution)/shard_map/all_gather | solution.py:134
  121.1 0.2 fusion.2
  121.3 0.0 copy-start.8
  121.3 0.5 copy-done.8
  121.8 0.0 copy-done.6
  121.8 3.2 %fusion.13 = f32[64,512]{1,0:T(8,128)} fusion(bf16[3072,512]{1,0:T(8,128)(2,1)} %param.16, bf16[64,3072]{1,0:T(8,128)(2,1)S(1)} %all_gather.7, f32[3072]{0:T(1024)S(1)} %copy-done.6, f32[64]{0:T(128)S(1)} %add_rsqrt_fusion), kind=kOutput, calls=%fused_computation.20 | convolution fusion | flops 202113024 | bytes 3682560 | tf_op jit(solution)/shard_map/dot_general | solution.py:136
  125.0 0.0 copy-done
  125.0 4.0 %convolution_convert_fusion = bf16[64,3072]{1,0:T(8,128)(2,1)} fusion(bf16[512,3072]{1,0:T(8,128)(2,1)S(1)} %copy-done, bf16[3072,512]{1,0:T(8,128)(2,1)} %param.17, f32[64,512]{1,0:T(8,128)} %fusion.13, bf16[64,3072]{1,0:T(8,128)(2,1)S(1)} %all_gather.7, f32[3072]{0:T(1024)S(1)} %copy-done.6, f32[64]{0:T(128)} %copy-done.8), kind=kOutput, calls=%fused_computation.1 | convolution fusion | flops 403832832 | bytes 7221504 | tf_op jit(solution)/shard_map/dot_general | solution.py:139
  129.0 2.1 %copy.20 = bf16[64,3072]{0,1:T(8,128)(2,1)} copy(bf16[64,3072]{1,0:T(8,128)(2,1)} %convolution_convert_fusion) | data formatting | bytes 786432
  131.2 0.0 reduce-scatter.4.cloned.1.call-update
  131.2 0.0 copy-done.7
  131.2 0.1 fusion.20
  131.3 0.1 reduce_window_sum.11
  131.4 0.2 select_reduce_fusion
  131.6 40.8 %reduce-scatter.4.cloned.1.call-done = bf16[384,64]{1,0:T(8,128)(2,1)} async-done(((bf16[3072,64]{1,0:T(8,128)(2,1)}), bf16[384,64]{1,0:T(8,128)(2,1)}) %reduce-scatter.4.cloned.1.call-update) | async-done | bytes 49168
  172.3 1.0 copy.21
  173.3 1.1 scatter_custom_fusion
  174.5 19.5 %all_to_all.24 = bf16[32,4,384]{2,1,0:T(4,128)(2,1)S(1)} all-to-all(bf16[32,4,384]{2,1,0:T(4,128)(2,1)S(1)} %reshape.76), channel_id=1, replica_groups=mesh['req'=2,'seq'=16,'tp'=8] {'req','seq'}, dimensions={0} | all-to-all | bytes 196608 | tf_op jit(solution)/shard_map/all_to_all | solution.py:158
  193.9 0.6 copy.28
  (6 shorter events, 0.1 us)
Async XLA Ops:
  6.5 118.5 %copy-start = (bf16[512,3072]{1,0:T(8,128)(2,1)S(1)}, bf16[512,3072]{1,0:T(8,128)(2,1)}, u32[]{:S(2)}) copy-start(bf16[512,3072]{1,0:T(8,128)(2,1)} %param.18) | copy-start | bytes 9437188
  6.5 165.8 %reduce-scatter.4.cloned.1.call-start = ((), (), s32[]{:S(2)}) async-start(), calls=%async_computation.3 | async-start | bytes 884736
  6.5 8.2 %copy-start.4 = (bf16[2,32,384]{2,1,0:T(8,128)(2,1)S(1)}, bf16[2,32,384]{2,1,0:T(8,128)(2,1)}, u32[]{:S(2)}) copy-start(bf16[2,32,384]{2,1,0:T(8,128)(2,1)} %param.10) | copy-start | bytes 147460
  6.5 30.4 %copy-start.3 = (bf16[2,32,2,384]{3,2,1,0:T(2,128)(2,1)S(1)}, bf16[2,32,2,384]{3,2,1,0:T(2,128)(2,1)}, u32[]{:S(2)}) copy-start(bf16[2,32,2,384]{3,2,1,0:T(2,128)(2,1)} %param.11) | copy-start | bytes 294916
  6.5 31.1 %copy-start.9 = (s32[2]{0:T(128)S(1)}, s32[2]{0:T(128)}, u32[]{:S(2)}) copy-start(s32[2]{0:T(128)} %param.13) | copy-start | bytes 28
  85.1 1.4 copy-start.1
  89.4 8.1 %copy-start.5 = (bf16[2,32,384]{2,1,0:T(8,128)(2,1)S(1)}, bf16[2,32,384]{2,1,0:T(8,128)(2,1)}, u32[]{:S(2)}) copy-start(bf16[2,32,384]{2,1,0:T(8,128)(2,1)} %param.14) | copy-start | bytes 147460
  94.0 27.8 %copy-start.6 = (f32[3072]{0:T(1024)S(1)}, f32[3072]{0:T(1024)}, u32[]{:S(2)}) copy-start(f32[3072]{0:T(1024)} %param.15) | copy-start | bytes 36868
  97.5 0.6 copy-start.2
  121.3 0.5 copy-start.8
  125.0 6.2 %copy-start.7 = (s32[1,64,1]{1,2,0:T(1,128)S(1)}, s32[1,64,1]{1,2,0:T(1,128)}, u32[]{:S(2)}) copy-start(s32[1,64,1]{1,2,0:T(1,128)} %param.19) | copy-start | bytes 772
Sparse Core Ops, SparseCore 0:
  131.3 40.9 reduce-scatter.3

commit v2 on v1

--- a/solution.py
+++ b/solution.py
@@ -22,11 +22,11 @@
     length = meta_ref[1 + slot]
     span = kc_ref.shape[0]
     fresh_count = kf_ref.shape[0]
-    width = q_ref.shape[1]
+    width = q_ref.shape[-1]
     offset = seq_index * span
     scale = HEAD ** (-0.5)
 
-    q = q_ref[...]
+    q = q_ref[...].reshape(tq, q_ref.shape[-1])
     lane = lax.broadcasted_iota(jnp.int32, (1, width), 1)
     stat_lane = lax.broadcasted_iota(jnp.int32, (1, STAT_LANES), 1)
     rows = q_block * tq + lax.broadcasted_iota(jnp.int32, (tq, 1), 0)
@@ -76,7 +76,8 @@
 
 
 def local_attention(all_queries, cache_kv, new_kv, cached_len, seq_index):
-    slot_count, query_count, width = all_queries.shape
+    source_count, slot_count, token_count, width = all_queries.shape
+    query_count = source_count * token_count
     span = cache_kv.shape[1]
     fresh_count = new_kv.shape[1]
     heads = width // HEAD
@@ -89,7 +90,7 @@
         num_scalar_prefetch=1,
         grid=(slot_count, query_count // tq),
         in_specs=[
-            pl.BlockSpec((None, tq, width), lambda s, b, m: (s, b, 0)),
+            pl.BlockSpec((tq // token_count, None, token_count, width), lambda s, b, m: (b, s, 0, 0)),
             pl.BlockSpec((None, span, width), lambda s, b, m: (s, 0, 0)),
             pl.BlockSpec((None, span, width), lambda s, b, m: (s, 0, 1)),
             pl.BlockSpec((None, fresh_count, width), lambda s, b, m: (s, 0, 0)),
@@ -116,7 +117,10 @@
     slot_count, token_count, width_local = queries.shape
     head_count = width_local // HEAD
     seq_index = lax.axis_index("seq")
-    all_queries = lax.all_gather(queries, "seq", axis=1, tiled=True)
+    seq_count = lax.axis_size("seq")
+    all_queries = lax.all_to_all(
+        jnp.broadcast_to(queries[None], (seq_count,) + queries.shape), "seq", 0, 0, tiled=True
+    )
     packed = local_attention(all_queries, cache_kv, new_kv, cached_len, seq_index)
     source = lax.all_to_all(packed[None], "seq", split_axis=2, concat_axis=0, tiled=True)
     source_sum = source[..., :width_local]
@@ -131,20 +135,28 @@
     stream = (residual_in.astype(jnp.float32) + attention).astype(jnp.bfloat16)
 
     block_rows = stream.reshape(slot_count * token_count, width_local)
-    full_rows = lax.all_gather(block_rows, "tp", axis=1, tiled=True)
+    tp_count = lax.axis_size("tp")
+    row_count = block_rows.shape[0]
+    full_rows = (
+        lax.all_to_all(
+            jnp.broadcast_to(block_rows[None], (tp_count,) + block_rows.shape), "tp", 0, 0, tiled=True
+        )
+        .transpose(1, 0, 2)
+        .reshape(row_count, tp_count * width_local)
+    )
     normed = normalize(full_rows, norm_gain)
     gate_out = jnp.dot(normed, gate_w, preferred_element_type=jnp.float32)
     up_out = jnp.dot(normed, up_w, preferred_element_type=jnp.float32)
     hidden = (jax.nn.silu(gate_out) * up_out).astype(jnp.bfloat16)
     partial_sum = jnp.dot(hidden, down_w, preferred_element_type=jnp.float32)
-    unit_share = lax.psum_scatter(
-        partial_sum.astype(jnp.bfloat16), "tp", scatter_dimension=1, tiled=True
-    ).astype(jnp.float32)
+    pieces = partial_sum.astype(jnp.bfloat16).reshape(row_count, tp_count, width_local).transpose(1, 0, 2)
+    unit_share = jnp.sum(
+        lax.all_to_all(pieces, "tp", 0, 0, tiled=True).astype(jnp.float32), axis=0
+    )
     finished = (block_rows.astype(jnp.float32) + unit_share).astype(jnp.bfloat16)
 
     owner_ids = owner.reshape(-1)
     owner_count = lax.axis_size(("req", "seq"))
-    row_count = owner_ids.shape[0]
     slot_cap = max(2, 2 * row_count // owner_count)
     matches = (owner_ids[:, None] == jnp.arange(owner_count, dtype=jnp.int32)[None, :]).astype(
         jnp.int32

time: 202 us -> 147 us (0.73)
  waiting for transfers between devices: 40.8 us -> 11.6 us
  blocking collectives: 89.7 us -> 64.5 us
  between operations: 13.5 us -> 0.2 us
  starting transfers between devices: 0.01 us -> 11.1 us
  other arithmetic: 6.32 us -> 9.87 us
  matrix products: 7.21 us -> 4.84 us
    all_gather x2 -> x0, blocking collectives: 45.2 us -> none  [the longest x1 23 us: per_device(): full_rows = lax.all_gather(block_rows, 'tp', axis=1, tiled=True)]
    unnamed x2 -> x0, waiting for transfers between devices: 40.8 us -> none
    all_to_all x0 -> x1, blocking collectives: none -> 19.2 us  [per_device(): lax.all_to_all(jnp.broadcast_to(block_rows[None], (tp_count,) + block_row...]
    all_to_all x0 -> x2, waiting for transfers between devices: none -> 11.6 us  [the longest x1 7.77 us: per_device(): lax.all_to_all(pieces, 'tp', 0, 0, tiled=True).astype(jnp.float32)]
    all_to_all x0 -> x2, starting transfers between devices: none -> 11.1 us  [the longest x1 7.62 us: per_device(): lax.all_to_all(jnp.broadcast_to(queries[None], (seq_count,) + queries.sha...]
    all_to_all x1, blocking collectives: 25 us -> 29.8 us  [per_device(): lax.all_to_all(packed[None], 'seq', split_axis=2, concat_axis=0, tiled=True)]
    all_to_all x1, blocking collectives: 19.5 us -> 15.5 us  [per_device(): lax.all_to_all(outgoing.reshape(owner_count, slot_cap, width_local), ('re...]
    unnamed x23, local copies, waits for them, and re-layouts: 6.04 us -> 3.08 us
  transfers between devices with their start and end apart: 1 -> 2, of which waited for: 1 -> 2; matrix products, arithmetic and copies ran while one was open for 0% -> 9% of each run, Pallas kernels for 0% -> 0%
where the time goes in v2:
time: 147 us; the launch traced here: 146 us
  blocking collectives  64.5 us (44%)
  local copies, waits for them, and re-layouts  25.1 us (17%)
  Pallas kernels  18.7 us (13%)
  waiting for transfers between devices  11.6 us (8%)
  starting transfers between devices  11.1 us (8%)
  other arithmetic  9.87 us (7%)
  matrix products  4.84 us (3%)
    all_to_all x1, blocking collectives, per_device(): lax.all_to_all(packed[None], 'seq', split_axis=2, concat_axis=0, tiled=True)  29.8 us
    all_to_all x1, blocking collectives, per_device(): lax.all_to_all(jnp.broadcast_to(block_rows[None], (tp_count,) + block_row...  19.2 us
    pallas_call x1, Pallas kernels, local_attention(): pl.pallas_call(kernel, grid_spec=grid_spec, out_shape=jax.ShapeDtypeStruc...  18.7 us
    all_to_all x1, blocking collectives, per_device(): lax.all_to_all(outgoing.reshape(owner_count, slot_cap, width_local), ('re...  15.5 us
    reshape x1, local copies, waits for them, and re-layouts, local_attention(): cache2 = cache_kv.reshape(slot_count, span, 2 * width)  8.08 us
    all_to_all x1, waiting for transfers between devices, per_device(): lax.all_to_all(pieces, 'tp', 0, 0, tiled=True).astype(jnp.float32)  7.77 us
    all_to_all x1, starting transfers between devices, per_device(): lax.all_to_all(jnp.broadcast_to(queries[None], (seq_count,) + queries.sha...  7.62 us
    mul x2, local copies, waits for them, and re-layouts, per_device(): own_sum = jnp.sum(grouped * source_scale[..., None], axis=0)  6.9 us
  transfers between devices with their start and end apart: 2, of which 2 were waited for; matrix products, arithmetic and copies ran while one was open for 9% of the time, Pallas kernels for 0%

profile of v2, /device:TPU:1, one launch (start us, length us, event | category | flops | bytes accessed | tf_op | source)
XLA Modules:
  0.0 145.9 jit_solution(8763275344751887137)
XLA Ops:
  0.0 0.0 copy-start
  0.0 1.9 %broadcast_in_dim.9 = bf16[16,2,32,384]{3,2,1,0:T(8,128)(2,1)} broadcast(bf16[2,32,384]{2,1,0:T(8,128)(2,1)} %param.10), dimensions={1,2,3} | broadcast | bytes 835584 | tf_op jit(solution)/shard_map/broadcast_in_dim | solution.py:122
  1.9 7.6 %all-to-all-start = ((bf16[16,2,32,384]{3,2,1,0:T(8,128)(2,1)}), bf16[16,2,32,384]{3,2,1,0:T(8,128)(2,1)}, u32[]{:S(2)}, u32[]{:S(2)}) async-start(bf16[16,2,32,384]{3,2,1,0:T(8,128)(2,1)} %broadcast_in_dim.9), calls=%async_computation | async-start | bytes 1572864 | tf_op jit(solution)/shard_map/all_to_all | solution.py:121
  9.6 0.0 copy-start.5
  9.6 0.0 copy-start.10
  9.6 8.1 %reshape.81.kc_ref.vc_ref = bf16[2,1024,768]{2,1,0:T(8,128)(2,1)} reshape(bf16[2,1024,2,384]{3,2,1,0:T(2,128)(2,1)} %param.12) | data formatting | bytes 6291456 | tf_op jit(solution)/shard_map/reshape | solution.py:85
  17.7 0.0 copy-done.5
  17.7 0.7 reshape.82.kf_ref.vf_ref
  18.4 0.0 copy-done.10
  18.4 0.6 pad_add_fusion.meta_ref
  19.0 3.9 %all-to-all-done.q_ref = bf16[16,2,32,384]{3,2,1,0:T(8,128)(2,1)} async-done(((bf16[16,2,32,384]{3,2,1,0:T(8,128)(2,1)}), bf16[16,2,32,384]{3,2,1,0:T(8,128)(2,1)}, u32[]{:S(2)}, u32[]{:S(2)}) %all-to-all-start) | async-done | bytes 786464 | tf_op jit(solution)/shard_map/all_to_all | solution.py:121
  22.9 18.7 %shard_map.100 = f32[2,512,512]{2,1,0:T(8,128)} custom-call(s32[3]{0:T(128)} %pad_add_fusion.meta_ref, bf16[16,2,32,384]{3,2,1,0:T(8,128)(2,1)} %all-to-all-done.q_ref, bf16[2,1024,768]{2,1,0:T(8,128)(2,1)} %reshape.81.kc_ref.vc_ref, bf16[2,1024,768]{2,1,0:T(8,128)(2,1)} %reshape.81.kc_ref.vc_ref, bf16[2,32,768]{2,1,0:T(8,128)(2,1)} %reshape.82.kf_ref.vf_ref, ...), custom_call_target="tpu_custom_call" | custom-call | tf_op jit(solution)/shard_map/pallas_call | solution.py:101
  41.6 3.2 %copy.23 = f32[1,2,512,512]{3,1,0,2:T(2,128)S(1)} copy(f32[1,2,512,512]{3,2,1,0:T(8,128)} %bitcast.37) | data formatting | bytes 4194304 | tf_op jit(solution)/shard_map/broadcast_in_dim | solution.py:125
  44.8 29.8 %all_to_all.38 = f32[1,2,512,512]{3,1,0,2:T(2,128)S(1)} all-to-all(f32[1,2,512,512]{3,1,0,2:T(2,128)S(1)} %copy.23), channel_id=1, replica_groups=mesh['req'=2,'seq'=16,'tp'=8] {'seq'}, dimensions={2} | all-to-all | bytes 4194304 | tf_op jit(solution)/shard_map/all_to_all | solution.py:125
  74.6 0.2 slice_reduce_fusion
  74.8 1.1 copy-done.1
  75.9 0.7 fusion.3
  76.6 2.2 %mul.65 = f32[16,2,32,4,96]{4,3,1,2,0:T(4,128)} broadcast(f32[16,2,32,4]{3,1,2,0:T(2,128)S(1)} %get-tuple-element.6), dimensions={0,1,2,3} | broadcast | bytes 1589248 | tf_op jit(solution)/shard_map/mul | solution.py:133
  78.9 4.7 %mul.66 = f32[16,2,32,384]{3,1,2,0:T(2,128)} reshape(f32[16,2,32,4,96]{4,3,1,2,0:T(4,128)} %mul.65) | data formatting | bytes 3145728 | tf_op jit(solution)/shard_map/mul | solution.py:133
  83.5 3.1 %fusion = f32[2,32,384]{2,0,1:T(2,128)S(1)} fusion(f32[16,2,32,384]{3,1,2,0:T(2,128)} %mul.66, f32[16,2,32,512]{3,1,2,0:T(2,128)} %bitcast.36), kind=kLoop, calls=%fused_computation.3 | loop fusion | flops 761856 | bytes 3244032 | tf_op jit(solution)/shard_map/reduce_sum | solution.py:133
  86.7 0.0 copy-start.6
  86.7 0.1 div.21
  86.8 0.1 div.22
  86.9 0.0 copy-done.7
  87.0 0.0 copy-start.3
  87.0 0.0 copy-start.4
  87.0 0.6 copy-done.4
  87.7 19.2 %all_to_all.39 = bf16[8,64,384]{2,1,0:T(8,128)(2,1)S(1)} all-to-all(bf16[8,64,384]{2,1,0:T(8,128)(2,1)S(1)} %broadcast_in_dim.11), channel_id=1, replica_groups=mesh['req'=2,'seq'=16,'tp'=8] {'tp'}, dimensions={0} | all-to-all | bytes 786432 | tf_op jit(solution)/shard_map/all_to_all | solution.py:141
  106.8 0.1 convert_bitcast_fusion
  106.9 0.1 copy.29
  106.9 0.0 copy-start.2
  106.9 0.2 fusion.2
  107.1 0.7 copy-done.2
  107.8 0.0 copy-done.9
  107.8 0.0 copy-done.6
  107.8 0.0 copy-done.3
  107.8 1.4 fusion.17
  109.2 3.5 %convolution_convert_fusion = bf16[64,3072]{1,0:T(8,128)(2,1)S(1)} fusion(bf16[512,3072]{1,0:T(8,128)(2,1)S(1)} %copy-done, bf16[3072,512]{1,0:T(8,128)(2,1)} %param.17, f32[64,512]{1,0:T(8,128)} %fusion.17, f32[64,3072]{1,0:T(8,128)} %bitcast.39, f32[3072]{0:T(1024)S(1)} %copy-done.6, f32[64]{0:T(128)} %copy-done.9), kind=kOutput, calls=%fused_computation.1 | convolution fusion | flops 403636224 | bytes 7614720 | tf_op jit(solution)/shard_map/dot_general | solution.py:151
  112.7 0.8 copy.36
  113.5 3.5 %all-to-all-start.3 = ((bf16[8,64,384]{2,1,0:T(8,128)(2,1)}), bf16[8,64,384]{2,1,0:T(8,128)(2,1)S(1)}, u32[]{:S(2)}, u32[]{:S(2)}) async-start(bf16[8,64,384]{2,1,0:T(8,128)(2,1)} %bitcast.41), calls=%async_computation.3 | async-start | bytes 786432 | tf_op jit(solution)/shard_map/all_to_all | solution.py:154
  116.9 0.7 fusion.14
  117.6 1.4 reduce_window_sum.11
  119.1 0.9 select_reduce_fusion
  120.0 7.8 %all-to-all-done.3 = bf16[8,64,384]{2,1,0:T(8,128)(2,1)S(1)} async-done(((bf16[8,64,384]{2,1,0:T(8,128)(2,1)}), bf16[8,64,384]{2,1,0:T(8,128)(2,1)S(1)}, u32[]{:S(2)}, u32[]{:S(2)}) %all-to-all-start.3) | async-done | bytes 393248 | tf_op jit(solution)/shard_map/all_to_all | solution.py:154
  127.8 0.7 convert_reduce_fusion
  128.5 1.2 scatter_custom_fusion
  129.7 15.5 %all_to_all.40 = bf16[32,4,384]{2,1,0:T(4,128)(2,1)S(1)} all-to-all(bf16[32,4,384]{2,1,0:T(4,128)(2,1)S(1)} %reshape.85), channel_id=1, replica_groups=mesh['req'=2,'seq'=16,'tp'=8] {'req','seq'}, dimensions={0} | all-to-all | bytes 196608 | tf_op jit(solution)/shard_map/all_to_all | solution.py:170
  145.2 0.6 copy.38
  (12 shorter events, 0.1 us)
Async XLA Ops:
  0.0 109.2 %copy-start = (bf16[512,3072]{1,0:T(8,128)(2,1)S(1)}, bf16[512,3072]{1,0:T(8,128)(2,1)}, u32[]{:S(2)}) copy-start(bf16[512,3072]{1,0:T(8,128)(2,1)} %param.18) | copy-start | bytes 9437188
  1.9 20.9 %all-to-all-start = ((bf16[16,2,32,384]{3,2,1,0:T(8,128)(2,1)}), bf16[16,2,32,384]{3,2,1,0:T(8,128)(2,1)}, u32[]{:S(2)}, u32[]{:S(2)}) async-start(bf16[16,2,32,384]{3,2,1,0:T(8,128)(2,1)} %broadcast_in_dim.9), calls=%async_computation | async-start | bytes 1572864 | tf_op jit(solution)/shard_map/all_to_all | solution.py:121
  9.6 8.1 %copy-start.5 = (bf16[2,32,2,384]{3,2,1,0:T(2,128)(2,1)S(1)}, bf16[2,32,2,384]{3,2,1,0:T(2,128)(2,1)}, u32[]{:S(2)}) copy-start(bf16[2,32,2,384]{3,2,1,0:T(2,128)(2,1)} %param.11) | copy-start | bytes 294916
  9.6 8.8 %copy-start.10 = (s32[2]{0:T(128)S(1)}, s32[2]{0:T(128)}, u32[]{:S(2)}) copy-start(s32[2]{0:T(128)} %param.13) | copy-start | bytes 28
  74.6 1.4 copy-start.1
  78.9 8.1 %copy-start.7 = (bf16[2,32,384]{2,1,0:T(8,128)(2,1)S(1)}, bf16[2,32,384]{2,1,0:T(8,128)(2,1)}, u32[]{:S(2)}) copy-start(bf16[2,32,384]{2,1,0:T(8,128)(2,1)} %param.14) | copy-start | bytes 147460
  86.7 21.2 %copy-start.6 = (f32[3072]{0:T(1024)S(1)}, f32[3072]{0:T(1024)}, u32[]{:S(2)}) copy-start(f32[3072]{0:T(1024)} %param.15) | copy-start | bytes 36868
  87.0 20.9 %copy-start.3 = (bf16[3072,512]{1,0:T(8,128)(2,1)S(1)}, bf16[3072,512]{1,0:T(8,128)(2,1)}, u32[]{:S(2)}) copy-start(bf16[3072,512]{1,0:T(8,128)(2,1)} %param.16) | copy-start | bytes 9437188
  87.0 0.6 copy-start.4
  106.9 0.9 copy-start.2
  107.1 0.7 copy-start.9
  109.2 7.7 %copy-start.8 = (s32[1,64,1]{1,2,0:T(1,128)S(1)}, s32[1,64,1]{1,2,0:T(1,128)}, u32[]{:S(2)}) copy-start(s32[1,64,1]{1,2,0:T(1,128)} %param.19) | copy-start | bytes 772
  113.5 14.3 %all-to-all-start.3 = ((bf16[8,64,384]{2,1,0:T(8,128)(2,1)}), bf16[8,64,384]{2,1,0:T(8,128)(2,1)S(1)}, u32[]{:S(2)}, u32[]{:S(2)}) async-start(bf16[8,64,384]{2,1,0:T(8,128)(2,1)} %bitcast.41), calls=%async_computation.3 | async-start | bytes 786432 | tf_op jit(solution)/shard_map/all_to_all | solution.py:154

commit v3 on v2

--- a/solution.py
+++ b/solution.py
@@ -11,11 +11,8 @@
 
 masked_floor = -1e30
 
-STAT_LANES = 128
-TOTAL_LANE = 8
-
-
-def attention_kernel(meta_ref, q_ref, kc_ref, vc_ref, kf_ref, vf_ref, out_ref, *, tq, heads):
+
+def attention_kernel(meta_ref, q_ref, kc_ref, vc_ref, kf_ref, vf_ref, sum_ref, stat_ref, *, tq, heads):
     slot = pl.program_id(0)
     q_block = pl.program_id(1)
     seq_index = meta_ref[0]
@@ -28,7 +25,7 @@
 
     q = q_ref[...].reshape(tq, q_ref.shape[-1])
     lane = lax.broadcasted_iota(jnp.int32, (1, width), 1)
-    stat_lane = lax.broadcasted_iota(jnp.int32, (1, STAT_LANES), 1)
+    stat_lane = lax.broadcasted_iota(jnp.int32, (1, 2 * heads), 1)
     rows = q_block * tq + lax.broadcasted_iota(jnp.int32, (tq, 1), 0)
     fresh_cols = seq_index * fresh_count + lax.broadcasted_iota(jnp.int32, (1, fresh_count), 1)
     fresh_visible = fresh_cols <= rows
@@ -42,7 +39,7 @@
             kc = kc_ref[...]
             vc = vc_ref[...]
         weighted = jnp.zeros((tq, width), jnp.float32)
-        stats = jnp.zeros((tq, STAT_LANES), jnp.float32)
+        stats = jnp.zeros((tq, 2 * heads), jnp.float32)
         for h in range(heads):
             head_lanes = (lane >= h * HEAD) & (lane < (h + 1) * HEAD)
             qh = jnp.where(head_lanes, q, jnp.zeros_like(q))
@@ -62,9 +59,9 @@
                 oh = oh + jnp.dot(pc.astype(jnp.bfloat16), vc, preferred_element_type=jnp.float32)
             weighted = jnp.where(head_lanes, oh, weighted)
             stats = jnp.where(stat_lane == h, peak, stats)
-            stats = jnp.where(stat_lane == TOTAL_LANE + h, total, stats)
-        out_ref[:, :width] = weighted
-        out_ref[:, width:] = stats
+            stats = jnp.where(stat_lane == heads + h, total, stats)
+        sum_ref[...] = weighted.astype(sum_ref.dtype)
+        stat_ref[...] = stats
 
     @pl.when(offset < length)
     def _():
@@ -96,13 +93,44 @@
             pl.BlockSpec((None, fresh_count, width), lambda s, b, m: (s, 0, 0)),
             pl.BlockSpec((None, fresh_count, width), lambda s, b, m: (s, 0, 1)),
         ],
-        out_specs=pl.BlockSpec((None, tq, width + STAT_LANES), lambda s, b, m: (s, b, 0)),
+        out_specs=[
+            pl.BlockSpec((None, tq, width), lambda s, b, m: (s, b, 0)),
+            pl.BlockSpec((None, tq, 2 * heads), lambda s, b, m: (s, b, 0)),
+        ],
     )
     return pl.pallas_call(
         kernel,
         grid_spec=grid_spec,
-        out_shape=jax.ShapeDtypeStruct((slot_count, query_count, width + STAT_LANES), jnp.float32),
+        out_shape=[
+            jax.ShapeDtypeStruct((slot_count, query_count, width), jnp.bfloat16),
+            jax.ShapeDtypeStruct((slot_count, query_count, 2 * heads), jnp.float32),
+        ],
     )(meta, all_queries, cache2, cache2, fresh2, fresh2)
+
+
+def combine_kernel(sum_ref, stat_ref, residual_ref, out_ref, *, heads):
+    stats = stat_ref[...]
+    sums = sum_ref[...].astype(jnp.float32)
+    width = sums.shape[-1]
+    lane = lax.broadcasted_iota(jnp.int32, (1, width), 1)
+    attention = jnp.zeros(sums.shape[1:], jnp.float32)
+    for h in range(heads):
+        peak = stats[:, :, h:h + 1]
+        joint_peak = jnp.max(peak, axis=0)
+        scale = jnp.exp(peak - joint_peak[None])
+        total = jnp.sum(stats[:, :, heads + h:heads + h + 1] * scale, axis=0)
+        head_sum = jnp.sum(sums * scale, axis=0)
+        head_lanes = (lane >= h * HEAD) & (lane < (h + 1) * HEAD)
+        attention = jnp.where(head_lanes, head_sum / total, attention)
+    out_ref[...] = (residual_ref[...].astype(jnp.float32) + attention).astype(out_ref.dtype)
+
+
+def combine(source_sum, source_stats, residual_rows):
+    heads = source_stats.shape[-1] // 2
+    return pl.pallas_call(
+        functools.partial(combine_kernel, heads=heads),
+        out_shape=jax.ShapeDtypeStruct(residual_rows.shape, jnp.bfloat16),
+    )(source_sum, source_stats, residual_rows)
 
 
 def normalize(features, norm_gain):
@@ -121,22 +149,16 @@
     all_queries = lax.all_to_all(
         jnp.broadcast_to(queries[None], (seq_count,) + queries.shape), "seq", 0, 0, tiled=True
     )
-    packed = local_attention(all_queries, cache_kv, new_kv, cached_len, seq_index)
-    source = lax.all_to_all(packed[None], "seq", split_axis=2, concat_axis=0, tiled=True)
-    source_sum = source[..., :width_local]
-    source_peak = source[..., width_local:width_local + head_count]
-    source_total = source[..., width_local + TOTAL_LANE:width_local + TOTAL_LANE + head_count]
-    joint_peak = jnp.max(source_peak, axis=0)
-    source_scale = jnp.exp(source_peak - joint_peak[None])
-    own_total = jnp.sum(source_total * source_scale, axis=0)
-    grouped = source_sum.reshape(source_sum.shape[:-1] + (head_count, HEAD))
-    own_sum = jnp.sum(grouped * source_scale[..., None], axis=0)
-    attention = (own_sum / own_total[..., None]).reshape(slot_count, token_count, width_local)
-    stream = (residual_in.astype(jnp.float32) + attention).astype(jnp.bfloat16)
-
-    block_rows = stream.reshape(slot_count * token_count, width_local)
+    partial_sum, partial_stats = local_attention(all_queries, cache_kv, new_kv, cached_len, seq_index)
+    source_sum = lax.all_to_all(partial_sum[None], "seq", split_axis=2, concat_axis=0, tiled=True)
+    source_stats = lax.all_to_all(partial_stats[None], "seq", split_axis=2, concat_axis=0, tiled=True)
+    row_count = slot_count * token_count
+    block_rows = combine(
+        source_sum.reshape(seq_count, row_count, width_local),
+        source_stats.reshape(seq_count, row_count, 2 * head_count),
+        residual_in.reshape(row_count, width_local),
+    )
     tp_count = lax.axis_size("tp")
-    row_count = block_rows.shape[0]
     full_rows = (
         lax.all_to_all(
             jnp.broadcast_to(block_rows[None], (tp_count,) + block_rows.shape), "tp", 0, 0, tiled=True

time: 147 us -> 138 us (0.939)
  blocking collectives: 64.5 us -> 35.6 us
  waiting for transfers between devices: 11.6 us -> 21.6 us
  starting transfers between devices: 11.1 us -> 18.9 us
  Pallas kernels: 18.7 us -> 22 us
  other arithmetic: 9.87 us -> 6.61 us
  local copies, waits for them, and re-layouts: 25.1 us -> 27.6 us
    all_to_all x1 -> x0, blocking collectives: 29.8 us -> none  [per_device(): lax.all_to_all(packed[None], 'seq', split_axis=2, concat_axis=0, tiled=True)]
    all_to_all x0 -> x2, waiting for transfers between devices: none -> 10.2 us  [the longest x1 6.66 us: per_device(): lax.all_to_all(partial_sum[None], 'seq', split_axis=2, concat_axis=0, til...]
    all_to_all x0 -> x2, starting transfers between devices: none -> 7.78 us  [the longest x1 4.29 us: per_device(): lax.all_to_all(partial_sum[None], 'seq', split_axis=2, concat_axis=0, til...]
    mul x2 -> x0, local copies, waits for them, and re-layouts: 6.9 us -> none  [per_device(): own_sum = jnp.sum(grouped * source_scale[..., None], axis=0)]
    all_to_all x0 -> x3, local copies, waits for them, and re-layouts: none -> 4.6 us  [the longest x2 2.43 us: per_device(): lax.all_to_all(partial_stats[None], 'seq', split_axis=2, concat_axis=0, t...]
    reduce_sum x2 -> x0, other arithmetic: 3.81 us -> none  [the longest x1 3.11 us: per_device(): own_sum = jnp.sum(grouped * source_scale[..., None], axis=0)]
    pallas_call x1 -> x2, Pallas kernels: 18.7 us -> 22 us  [the longest x1 18.6 us: local_attention(): pl.pallas_call(kernel, grid_spec=grid_spec, out_shape=[jax.ShapeDtypeStru...]
    unnamed x23 -> x19, local copies, waits for them, and re-layouts: 3.08 us -> 5.38 us
  transfers between devices with their start and end apart: 2 -> 4, of which waited for: 2 -> 4; matrix products, arithmetic and copies ran while one was open for 9% -> 15% of each run, Pallas kernels for 0% -> 0%
where the time goes in v3:
time: 138 us; the launch traced here: 137 us
  blocking collectives  35.6 us (26%)
  local copies, waits for them, and re-layouts  27.6 us (20%)
  Pallas kernels  22 us (16%)
  waiting for transfers between devices  21.6 us (16%)
  starting transfers between devices  18.9 us (14%)
  other arithmetic  6.61 us (5%)
  matrix products  4.86 us (4%)
    all_to_all x1, blocking collectives, per_device(): lax.all_to_all(jnp.broadcast_to(block_rows[None], (tp_count,) + block_row...  18.7 us
    pallas_call x1, Pallas kernels, local_attention(): pl.pallas_call(kernel, grid_spec=grid_spec, out_shape=[jax.ShapeDtypeStru...  18.6 us
    all_to_all x1, blocking collectives, per_device(): lax.all_to_all(outgoing.reshape(owner_count, slot_cap, width_local), ('re...  16.9 us
    reshape x1, local copies, waits for them, and re-layouts, local_attention(): cache2 = cache_kv.reshape(slot_count, span, 2 * width)  8.09 us
    all_to_all x1, starting transfers between devices, per_device(): lax.all_to_all(jnp.broadcast_to(queries[None], (seq_count,) + queries.sha...  7.62 us
    all_to_all x1, waiting for transfers between devices, per_device(): lax.all_to_all(pieces, 'tp', 0, 0, tiled=True).astype(jnp.float32)  7.55 us
    all_to_all x1, waiting for transfers between devices, per_device(): lax.all_to_all(partial_sum[None], 'seq', split_axis=2, concat_axis=0, til...  6.66 us
    unnamed x19, local copies, waits for them, and re-layouts  5.38 us
  transfers between devices with their start and end apart: 4, of which 4 were waited for; matrix products, arithmetic and copies ran while one was open for 15% of the time, Pallas kernels for 0%

profile of v3, /device:TPU:1, one launch (start us, length us, event | category | flops | bytes accessed | tf_op | source)
XLA Modules:
  0.0 137.3 jit_solution(16508587934582695218)
XLA Ops:
  0.0 0.0 copy-start
  0.0 1.9 %broadcast_in_dim.11 = bf16[16,2,32,384]{3,2,1,0:T(8,128)(2,1)} broadcast(bf16[2,32,384]{2,1,0:T(8,128)(2,1)} %param.10), dimensions={1,2,3} | broadcast | bytes 835584 | tf_op jit(solution)/shard_map/broadcast_in_dim | solution.py:150
  1.9 7.6 %all-to-all-start = ((bf16[16,2,32,384]{3,2,1,0:T(8,128)(2,1)}), bf16[16,2,32,384]{3,2,1,0:T(8,128)(2,1)}, u32[]{:S(2)}, u32[]{:S(2)}) async-start(bf16[16,2,32,384]{3,2,1,0:T(8,128)(2,1)} %broadcast_in_dim.11), calls=%async_computation | async-start | bytes 1572864 | tf_op jit(solution)/shard_map/all_to_all | solution.py:149
  9.6 0.0 copy-start.3
  9.6 0.0 copy-start.7
  9.6 8.1 %reshape.79.kc_ref.vc_ref = bf16[2,1024,768]{2,1,0:T(8,128)(2,1)} reshape(bf16[2,1024,2,384]{3,2,1,0:T(2,128)(2,1)} %param.12) | data formatting | bytes 6291456 | tf_op jit(solution)/shard_map/reshape | solution.py:82
  17.7 0.0 copy-done.3
  17.7 0.7 reshape.80.kf_ref.vf_ref
  18.4 0.0 copy-done.7
  18.4 0.7 pad_add_fusion.meta_ref
  19.0 3.8 %all-to-all-done.q_ref = bf16[16,2,32,384]{3,2,1,0:T(8,128)(2,1)} async-done(((bf16[16,2,32,384]{3,2,1,0:T(8,128)(2,1)}), bf16[16,2,32,384]{3,2,1,0:T(8,128)(2,1)}, u32[]{:S(2)}, u32[]{:S(2)}) %all-to-all-start) | async-done | bytes 786464 | tf_op jit(solution)/shard_map/all_to_all | solution.py:149
  22.9 18.6 %shard_map.100 = (bf16[2,512,384]{2,1,0:T(8,128)(2,1)}, f32[2,512,8]{2,1,0:T(8,128)}) custom-call(s32[3]{0:T(128)} %pad_add_fusion.meta_ref, bf16[16,2,32,384]{3,2,1,0:T(8,128)(2,1)} %all-to-all-done.q_ref, bf16[2,1024,768]{2,1,0:T(8,128)(2,1)} %reshape.79.kc_ref.vc_ref, bf16[2,1024,768]{2,1,0:T(8,128)(2,1)} %reshape.79.kc_ref.vc_ref, ...), custom_call_target="tpu_custom_call" | custom-call | tf_op jit(solution)/shard_map/pallas_call | solution.py:101
  41.5 2.2 %copy.26 = f32[1,2,512,8]{3,1,0,2:T(2,128)} copy(f32[1,2,512,8]{3,2,1,0:T(8,128)} %bitcast.49) | data formatting | bytes 65536 | tf_op jit(solution)/shard_map/broadcast_in_dim | solution.py:154
  43.7 2.4 %reshape.98 = f32[16,1,512]{2,1,0:T(1,128)} reshape(f32[512,1,2,8]{3,2,1,0:T(2,128)} %bitcast.43) | data formatting | bytes 65536
  46.2 3.5 %all-to-all-start.2 = ((f32[16,1,512]{2,1,0:T(1,128)}), f32[16,1,512]{2,1,0:T(1,128)S(1)}, u32[]{:S(2)}, u32[]{:S(2)}) async-start(f32[16,1,512]{2,1,0:T(1,128)} %reshape.98), calls=%async_computation.2 | async-start | bytes 65536 | tf_op jit(solution)/shard_map/all_to_all | solution.py:154
  49.7 2.8 %copy.15 = bf16[1,2,512,384]{3,1,0,2:T(2,128)(2,1)} copy(bf16[1,2,512,384]{3,2,1,0:T(8,128)(2,1)} %bitcast.48) | data formatting | bytes 1572864 | tf_op jit(solution)/shard_map/broadcast_in_dim | solution.py:153
  52.5 3.6 %all-to-all-done.2 = f32[16,1,512]{2,1,0:T(1,128)S(1)} async-done(((f32[16,1,512]{2,1,0:T(1,128)}), f32[16,1,512]{2,1,0:T(1,128)S(1)}, u32[]{:S(2)}, u32[]{:S(2)}) %all-to-all-start.2) | async-done | bytes 32800 | tf_op jit(solution)/shard_map/all_to_all | solution.py:154
  56.1 4.3 %all-to-all-start.1 = ((bf16[1,2,512,384]{3,1,0,2:T(2,128)(2,1)}), bf16[1,2,512,384]{3,1,0,2:T(2,128)(2,1)}, u32[]{:S(2)}, u32[]{:S(2)}) async-start(bf16[1,2,512,384]{3,1,0,2:T(2,128)(2,1)} %copy.15), calls=%async_computation.1 | async-start | bytes 1572864 | tf_op jit(solution)/shard_map/all_to_all | solution.py:153
  60.4 0.5 broadcast.58
  60.9 0.7 reduce.2
  61.6 1.6 %reshape.99 = f32[512,1,2,8]{3,2,1,0:T(2,128)} reshape(f32[16,512]{1,0:T(8,128)S(1)} %reduce.2) | data formatting | bytes 65536
  63.2 1.9 %copy.18 = f32[1,2,16,32,8]{4,3,1,2,0:T(8,128)} copy(f32[1,2,16,32,8]{4,1,3,2,0:T(2,128)} %bitcast.44) | data formatting | bytes 65536 | tf_op jit(solution)/shard_map/all_to_all | solution.py:154
  65.1 6.7 %all-to-all-done.1 = bf16[1,2,512,384]{3,1,0,2:T(2,128)(2,1)} async-done(((bf16[1,2,512,384]{3,1,0,2:T(2,128)(2,1)}), bf16[1,2,512,384]{3,1,0,2:T(2,128)(2,1)}, u32[]{:S(2)}, u32[]{:S(2)}) %all-to-all-start.1) | async-done | bytes 786464 | tf_op jit(solution)/shard_map/all_to_all | solution.py:153
  71.8 2.2 %copy.16 = bf16[1,2,16,32,384]{4,3,1,2,0:T(8,128)(2,1)} copy(bf16[1,2,16,32,384]{4,1,3,2,0:T(2,128)(2,1)} %bitcast.6) | data formatting | bytes 1572864 | tf_op jit(solution)/shard_map/all_to_all | solution.py:153
  74.0 3.4 %shard_map.101 = bf16[64,384]{1,0:T(8,128)(2,1)} custom-call(bf16[16,64,384]{2,1,0:T(8,128)(2,1)} %bitcast.42, f32[16,64,8]{2,1,0:T(8,128)} %bitcast.45, bf16[64,384]{1,0:T(8,128)(2,1)} %bitcast.51), custom_call_target="tpu_custom_call" | custom-call | tf_op jit(solution)/shard_map/pallas_call | solution.py:130
  77.3 1.0 broadcast_in_dim.14
  78.3 18.7 %all_to_all.50 = bf16[8,64,384]{2,1,0:T(8,128)(2,1)S(1)} all-to-all(bf16[8,64,384]{2,1,0:T(8,128)(2,1)S(1)} %broadcast_in_dim.14), channel_id=1, replica_groups=mesh['req'=2,'seq'=16,'tp'=8] {'tp'}, dimensions={0} | all-to-all | bytes 786432 | tf_op jit(solution)/shard_map/all_to_all | solution.py:163
  97.0 0.1 convert_bitcast_fusion
  97.1 0.1 copy.22
  97.2 0.0 copy-start.1
  97.2 0.2 fusion.1
  97.4 0.7 copy-done.1
  98.0 0.0 copy-done.6
  98.0 0.0 copy-done.4
  98.0 0.0 copy-done.2
  98.0 1.4 fusion.13
  99.4 3.5 %convolution_convert_fusion = bf16[64,3072]{1,0:T(8,128)(2,1)S(1)} fusion(bf16[512,3072]{1,0:T(8,128)(2,1)S(1)} %copy-done, bf16[3072,512]{1,0:T(8,128)(2,1)} %param.17, f32[64,512]{1,0:T(8,128)} %fusion.13, f32[64,3072]{1,0:T(8,128)} %bitcast.41, f32[3072]{0:T(1024)S(1)} %copy-done.4, f32[64]{0:T(128)} %copy-done.6), kind=kOutput, calls=%fused_computation.1 | convolution fusion | flops 403636224 | bytes 7614720 | tf_op jit(solution)/shard_map/dot_general | solution.py:173
  102.9 0.8 copy.25
  103.7 3.5 %all-to-all-start.4 = ((bf16[8,64,384]{2,1,0:T(8,128)(2,1)}), bf16[8,64,384]{2,1,0:T(8,128)(2,1)S(1)}, u32[]{:S(2)}, u32[]{:S(2)}) async-start(bf16[8,64,384]{2,1,0:T(8,128)(2,1)} %bitcast.47), calls=%async_computation.4 | async-start | bytes 786432 | tf_op jit(solution)/shard_map/all_to_all | solution.py:176
  107.2 0.0 copy-done.5
  107.2 0.7 fusion.10
  107.9 1.5 %reduce_window_sum.11 = s32[64,32]{1,0:T(8,128)} reduce-window(s32[64,32]{1,0:T(8,128)} %fusion.10, s32[]{:T(128)} %constant.13.clone.1), window={size=64x1 pad=63_0x0_0}, to_apply=%region_0.0 | reduce-window | flops 129024 | bytes 16388 | tf_op jit(solution)/shard_map/jit(cumsum)/reduce_window_sum | solution.py:186
  109.3 0.9 select_reduce_fusion
  110.3 7.6 %all-to-all-done.4 = bf16[8,64,384]{2,1,0:T(8,128)(2,1)S(1)} async-done(((bf16[8,64,384]{2,1,0:T(8,128)(2,1)}), bf16[8,64,384]{2,1,0:T(8,128)(2,1)S(1)}, u32[]{:S(2)}, u32[]{:S(2)}) %all-to-all-start.4) | async-done | bytes 393248 | tf_op jit(solution)/shard_map/all_to_all | solution.py:176
  117.8 0.7 convert_reduce_fusion
  118.5 1.2 scatter_custom_fusion
  119.8 16.9 %all_to_all.51 = bf16[32,4,384]{2,1,0:T(4,128)(2,1)S(1)} all-to-all(bf16[32,4,384]{2,1,0:T(4,128)(2,1)S(1)} %reshape.85), channel_id=1, replica_groups=mesh['req'=2,'seq'=16,'tp'=8] {'req','seq'}, dimensions={0} | all-to-all | bytes 196608 | tf_op jit(solution)/shard_map/all_to_all | solution.py:192
  136.6 0.6 copy.28
  (8 shorter events, 0.1 us)
Async XLA Ops:
  0.0 99.4 %copy-start = (bf16[512,3072]{1,0:T(8,128)(2,1)S(1)}, bf16[512,3072]{1,0:T(8,128)(2,1)}, u32[]{:S(2)}) copy-start(bf16[512,3072]{1,0:T(8,128)(2,1)} %param.18) | copy-start | bytes 9437188
  1.9 20.9 %all-to-all-start = ((bf16[16,2,32,384]{3,2,1,0:T(8,128)(2,1)}), bf16[16,2,32,384]{3,2,1,0:T(8,128)(2,1)}, u32[]{:S(2)}, u32[]{:S(2)}) async-start(bf16[16,2,32,384]{3,2,1,0:T(8,128)(2,1)} %broadcast_in_dim.11), calls=%async_computation | async-start | bytes 1572864 | tf_op jit(solution)/shard_map/all_to_all | solution.py:149
  9.6 8.1 %copy-start.3 = (bf16[2,32,2,384]{3,2,1,0:T(2,128)(2,1)S(1)}, bf16[2,32,2,384]{3,2,1,0:T(2,128)(2,1)}, u32[]{:S(2)}) copy-start(bf16[2,32,2,384]{3,2,1,0:T(2,128)(2,1)} %param.11) | copy-start | bytes 294916
  9.6 8.8 %copy-start.7 = (s32[2]{0:T(128)S(1)}, s32[2]{0:T(128)}, u32[]{:S(2)}) copy-start(s32[2]{0:T(128)} %param.13) | copy-start | bytes 28
  46.2 9.9 %all-to-all-start.2 = ((f32[16,1,512]{2,1,0:T(1,128)}), f32[16,1,512]{2,1,0:T(1,128)S(1)}, u32[]{:S(2)}, u32[]{:S(2)}) async-start(f32[16,1,512]{2,1,0:T(1,128)} %reshape.98), calls=%async_computation.2 | async-start | bytes 65536 | tf_op jit(solution)/shard_map/all_to_all | solution.py:154
  56.1 15.7 %all-to-all-start.1 = ((bf16[1,2,512,384]{3,1,0,2:T(2,128)(2,1)}), bf16[1,2,512,384]{3,1,0,2:T(2,128)(2,1)}, u32[]{:S(2)}, u32[]{:S(2)}) async-start(bf16[1,2,512,384]{3,1,0,2:T(2,128)(2,1)} %copy.15), calls=%async_computation.1 | async-start | bytes 1572864 | tf_op jit(solution)/shard_map/all_to_all | solution.py:153
  74.0 24.1 %copy-start.4 = (f32[3072]{0:T(1024)S(1)}, f32[3072]{0:T(1024)}, u32[]{:S(2)}) copy-start(f32[3072]{0:T(1024)} %param.15) | copy-start | bytes 36868
  77.3 20.7 %copy-start.2 = (bf16[3072,512]{1,0:T(8,128)(2,1)S(1)}, bf16[3072,512]{1,0:T(8,128)(2,1)}, u32[]{:S(2)}) copy-start(bf16[3072,512]{1,0:T(8,128)(2,1)} %param.16) | copy-start | bytes 9437188
  97.2 0.9 copy-start.1
  97.4 0.7 copy-start.6
  99.4 7.7 %copy-start.5 = (s32[1,64,1]{1,2,0:T(1,128)S(1)}, s32[1,64,1]{1,2,0:T(1,128)}, u32[]{:S(2)}) copy-start(s32[1,64,1]{1,2,0:T(1,128)} %param.19) | copy-start | bytes 772
  103.7 14.1 %all-to-all-start.4 = ((bf16[8,64,384]{2,1,0:T(8,128)(2,1)}), bf16[8,64,384]{2,1,0:T(8,128)(2,1)S(1)}, u32[]{:S(2)}, u32[]{:S(2)}) async-start(bf16[8,64,384]{2,1,0:T(8,128)(2,1)} %bitcast.47), calls=%async_computation.4 | async-start | bytes 786432 | tf_op jit(solution)/shard_map/all_to_all | solution.py:176

commit v4 on v3

--- a/solution.py
+++ b/solution.py
@@ -60,8 +60,8 @@
             weighted = jnp.where(head_lanes, oh, weighted)
             stats = jnp.where(stat_lane == h, peak, stats)
             stats = jnp.where(stat_lane == heads + h, total, stats)
-        sum_ref[...] = weighted.astype(sum_ref.dtype)
-        stat_ref[...] = stats
+        sum_ref[...] = weighted.reshape(sum_ref.shape).astype(sum_ref.dtype)
+        stat_ref[...] = stats.reshape(stat_ref.shape)
 
     @pl.when(offset < length)
     def _():
@@ -94,16 +94,16 @@
             pl.BlockSpec((None, fresh_count, width), lambda s, b, m: (s, 0, 1)),
         ],
         out_specs=[
-            pl.BlockSpec((None, tq, width), lambda s, b, m: (s, b, 0)),
-            pl.BlockSpec((None, tq, 2 * heads), lambda s, b, m: (s, b, 0)),
+            pl.BlockSpec((tq // token_count, None, token_count, width), lambda s, b, m: (b, s, 0, 0)),
+            pl.BlockSpec((tq // token_count, None, token_count, 2 * heads), lambda s, b, m: (b, s, 0, 0)),
         ],
     )
     return pl.pallas_call(
         kernel,
         grid_spec=grid_spec,
         out_shape=[
-            jax.ShapeDtypeStruct((slot_count, query_count, width), jnp.bfloat16),
-            jax.ShapeDtypeStruct((slot_count, query_count, 2 * heads), jnp.float32),
+            jax.ShapeDtypeStruct((source_count, slot_count, token_count, width), jnp.bfloat16),
+            jax.ShapeDtypeStruct((source_count, slot_count, token_count, 2 * heads), jnp.float32),
         ],
     )(meta, all_queries, cache2, cache2, fresh2, fresh2)
 
@@ -150,8 +150,8 @@
         jnp.broadcast_to(queries[None], (seq_count,) + queries.shape), "seq", 0, 0, tiled=True
     )
     partial_sum, partial_stats = local_attention(all_queries, cache_kv, new_kv, cached_len, seq_index)
-    source_sum = lax.all_to_all(partial_sum[None], "seq", split_axis=2, concat_axis=0, tiled=True)
-    source_stats = lax.all_to_all(partial_stats[None], "seq", split_axis=2, concat_axis=0, tiled=True)
+    source_sum = lax.all_to_all(partial_sum, "seq", 0, 0, tiled=True)
+    source_stats = lax.all_to_all(partial_stats, "seq", 0, 0, tiled=True)
     row_count = slot_count * token_count
     block_rows = combine(
         source_sum.reshape(seq_count, row_count, width_local),

time: 138 us -> 132 us (0.957)
  local copies, waits for them, and re-layouts: 27.6 us -> 16.9 us
  blocking collectives: 35.6 us -> 44.7 us
  starting transfers between devices: 18.9 us -> 15.4 us
    all_to_all x0 -> x1, blocking collectives: none -> 9 us  [per_device(): source_stats = lax.all_to_all(partial_stats, 'seq', 0, 0, tiled=True)]
    broadcast_in_dim x2 -> x0, local copies, waits for them, and re-layouts: 5.07 us -> none  [the longest x1 2.84 us: per_device(): partial_sum[None]]
    unnamed x19, local copies, waits for them, and re-layouts: 5.38 us -> 1.56 us
    all_to_all x2 -> x1, starting transfers between devices: 7.78 us -> 4.29 us  [per_device(): source_sum = lax.all_to_all(partial_sum, 'seq', 0, 0, tiled=True)]
    all_to_all x3 -> x2, local copies, waits for them, and re-layouts: 4.6 us -> 1.54 us  [per_device(): source_stats = lax.all_to_all(partial_stats, 'seq', 0, 0, tiled=True)]
    all_to_all x2 -> x1, waiting for transfers between devices: 10.2 us -> 8.97 us  [per_device(): source_sum = lax.all_to_all(partial_sum, 'seq', 0, 0, tiled=True)]
  transfers between devices with their start and end apart: 4 -> 3, of which waited for: 4 -> 3; matrix products, arithmetic and copies ran while one was open for 15% -> 11% of each run, Pallas kernels for 0% -> 0%
where the time goes in v4:
time: 132 us; the launch traced here: 131 us
  blocking collectives  44.7 us (34%)
  Pallas kernels  22 us (17%)
  waiting for transfers between devices  20.4 us (15%)
  local copies, waits for them, and re-layouts  16.9 us (13%)
  starting transfers between devices  15.4 us (12%)
  other arithmetic  6.55 us (5%)
  matrix products  4.84 us (4%)
    all_to_all x1, blocking collectives, per_device(): lax.all_to_all(jnp.broadcast_to(block_rows[None], (tp_count,) + block_row...  18.8 us
    pallas_call x1, Pallas kernels, local_attention(): pl.pallas_call(kernel, grid_spec=grid_spec, out_shape=[jax.ShapeDtypeStru...  18.7 us
    all_to_all x1, blocking collectives, per_device(): lax.all_to_all(outgoing.reshape(owner_count, slot_cap, width_local), ('re...  16.8 us
    all_to_all x1, blocking collectives, per_device(): source_stats = lax.all_to_all(partial_stats, 'seq', 0, 0, tiled=True)  9 us
    all_to_all x1, waiting for transfers between devices, per_device(): source_sum = lax.all_to_all(partial_sum, 'seq', 0, 0, tiled=True)  8.97 us
    reshape x1, local copies, waits for them, and re-layouts, local_attention(): cache2 = cache_kv.reshape(slot_count, span, 2 * width)  8.08 us
    all_to_all x1, starting transfers between devices, per_device(): lax.all_to_all(jnp.broadcast_to(queries[None], (seq_count,) + queries.sha...  7.62 us
    all_to_all x1, waiting for transfers between devices, per_device(): lax.all_to_all(pieces, 'tp', 0, 0, tiled=True).astype(jnp.float32)  7.57 us
  transfers between devices with their start and end apart: 3, of which 3 were waited for; matrix products, arithmetic and copies ran while one was open for 11% of the time, Pallas kernels for 0%

profile of v4, /device:TPU:1, one launch (start us, length us, event | category | flops | bytes accessed | tf_op | source)
XLA Modules:
  0.0 130.9 jit_solution(1629737705350791182)
XLA Ops:
  0.0 0.0 copy-start
  0.0 1.9 %broadcast_in_dim.7 = bf16[16,2,32,384]{3,2,1,0:T(8,128)(2,1)} broadcast(bf16[2,32,384]{2,1,0:T(8,128)(2,1)} %param.10), dimensions={1,2,3} | broadcast | bytes 835584 | tf_op jit(solution)/shard_map/broadcast_in_dim | solution.py:150
  1.9 7.6 %all-to-all-start = ((bf16[16,2,32,384]{3,2,1,0:T(8,128)(2,1)}), bf16[16,2,32,384]{3,2,1,0:T(8,128)(2,1)}, u32[]{:S(2)}, u32[]{:S(2)}) async-start(bf16[16,2,32,384]{3,2,1,0:T(8,128)(2,1)} %broadcast_in_dim.7), calls=%async_computation | async-start | bytes 1572864 | tf_op jit(solution)/shard_map/all_to_all | solution.py:149
  9.6 0.0 copy-start.3
  9.6 0.0 copy-start.7
  9.6 8.1 %reshape.77.kc_ref.vc_ref = bf16[2,1024,768]{2,1,0:T(8,128)(2,1)} reshape(bf16[2,1024,2,384]{3,2,1,0:T(2,128)(2,1)} %param.12) | data formatting | bytes 6291456 | tf_op jit(solution)/shard_map/reshape | solution.py:82
  17.7 0.0 copy-done.3
  17.7 0.7 reshape.78.kf_ref.vf_ref
  18.4 0.0 copy-done.7
  18.4 0.6 pad_add_fusion.meta_ref
  19.0 3.9 %all-to-all-done.q_ref = bf16[16,2,32,384]{3,2,1,0:T(8,128)(2,1)} async-done(((bf16[16,2,32,384]{3,2,1,0:T(8,128)(2,1)}), bf16[16,2,32,384]{3,2,1,0:T(8,128)(2,1)}, u32[]{:S(2)}, u32[]{:S(2)}) %all-to-all-start) | async-done | bytes 786464 | tf_op jit(solution)/shard_map/all_to_all | solution.py:149
  22.9 18.7 %shard_map.100 = (bf16[16,2,32,384]{3,2,1,0:T(8,128)(2,1)}, f32[16,2,32,8]{3,2,1,0:T(8,128)}) custom-call(s32[3]{0:T(128)} %pad_add_fusion.meta_ref, bf16[16,2,32,384]{3,2,1,0:T(8,128)(2,1)} %all-to-all-done.q_ref, bf16[2,1024,768]{2,1,0:T(8,128)(2,1)} %reshape.77.kc_ref.vc_ref, bf16[2,1024,768]{2,1,0:T(8,128)(2,1)} %reshape.77.kc_ref.vc_ref, ...), custom_call_target="tpu_custom_call" | custom-call | tf_op jit(solution)/shard_map/pallas_call | solution.py:101
  41.5 1.2 copy.11
  42.7 0.1 reshape.96
  42.9 9.0 %all_to_all.30 = f32[16,1,512]{2,1,0:T(1,128)S(1)} all-to-all(f32[16,1,512]{2,1,0:T(1,128)S(1)} %reshape.96), channel_id=1, replica_groups=mesh['req'=2,'seq'=16,'tp'=8] {'seq'}, dimensions={0} | all-to-all | bytes 65536 | tf_op jit(solution)/shard_map/all_to_all | solution.py:154
  51.9 4.3 %all-to-all-start.1 = ((bf16[16,2,32,384]{3,2,1,0:T(8,128)(2,1)}), bf16[16,2,32,384]{3,2,1,0:T(8,128)(2,1)}, u32[]{:S(2)}, u32[]{:S(2)}) async-start(bf16[16,2,32,384]{3,2,1,0:T(8,128)(2,1)} %get-tuple-element.7), calls=%async_computation.1 | async-start | bytes 1572864 | tf_op jit(solution)/shard_map/all_to_all | solution.py:153
  56.2 0.5 broadcast.58
  56.7 0.7 reduce.2
  57.4 0.1 reshape.97
  57.5 0.0 copy-start.4
  57.5 1.0 copy.12
  58.5 9.0 %all-to-all-done.1 = bf16[16,2,32,384]{3,2,1,0:T(8,128)(2,1)} async-done(((bf16[16,2,32,384]{3,2,1,0:T(8,128)(2,1)}), bf16[16,2,32,384]{3,2,1,0:T(8,128)(2,1)}, u32[]{:S(2)}, u32[]{:S(2)}) %all-to-all-start.1) | async-done | bytes 786464 | tf_op jit(solution)/shard_map/all_to_all | solution.py:153
  67.5 3.3 %shard_map.101 = bf16[64,384]{1,0:T(8,128)(2,1)} custom-call(bf16[16,64,384]{2,1,0:T(8,128)(2,1)} %bitcast.5.sum_ref, f32[16,64,8]{2,1,0:T(8,128)} %bitcast.32, bf16[64,384]{1,0:T(8,128)(2,1)} %bitcast.38), custom_call_target="tpu_custom_call" | custom-call | tf_op jit(solution)/shard_map/pallas_call | solution.py:130
  70.9 0.0 copy-start.2
  70.9 1.0 broadcast_in_dim.8
  71.9 18.8 %all_to_all.31 = bf16[8,64,384]{2,1,0:T(8,128)(2,1)S(1)} all-to-all(bf16[8,64,384]{2,1,0:T(8,128)(2,1)S(1)} %broadcast_in_dim.8), channel_id=1, replica_groups=mesh['req'=2,'seq'=16,'tp'=8] {'tp'}, dimensions={0} | all-to-all | bytes 786432 | tf_op jit(solution)/shard_map/all_to_all | solution.py:163
  90.7 0.1 convert_bitcast_fusion
  90.8 0.1 copy.16
  90.8 0.0 copy-start.1
  90.8 0.2 fusion.1
  91.0 0.7 copy-done.1
  91.7 0.0 copy-done.6
  91.7 0.0 copy-done.4
  91.7 0.0 copy-done.2
  91.7 1.4 %fusion.13 = f32[64,512]{1,0:T(8,128)} fusion(bf16[3072,512]{1,0:T(8,128)(2,1)S(1)} %copy-done.2, f32[64,3072]{1,0:T(8,128)S(1)} %bitcast.30, f32[3072]{0:T(1024)S(1)} %copy-done.4, f32[64]{0:T(128)S(1)} %add_rsqrt_fusion), kind=kOutput, calls=%fused_computation.28 | convolution fusion | flops 201916416 | bytes 4075776 | tf_op jit(solution)/shard_map/dot_general | solution.py:170
  93.1 0.0 copy-done
  93.1 3.5 %convolution_convert_fusion = bf16[64,3072]{1,0:T(8,128)(2,1)S(1)} fusion(bf16[512,3072]{1,0:T(8,128)(2,1)S(1)} %copy-done, bf16[3072,512]{1,0:T(8,128)(2,1)} %param.17, f32[64,512]{1,0:T(8,128)} %fusion.13, f32[64,3072]{1,0:T(8,128)} %bitcast.31, f32[3072]{0:T(1024)S(1)} %copy-done.4, f32[64]{0:T(128)} %copy-done.6), kind=kOutput, calls=%fused_computation.1 | convolution fusion | flops 403636224 | bytes 7614720 | tf_op jit(solution)/shard_map/dot_general | solution.py:173
  96.6 0.8 copy.18
  97.4 3.5 %all-to-all-start.4 = ((bf16[8,64,384]{2,1,0:T(8,128)(2,1)}), bf16[8,64,384]{2,1,0:T(8,128)(2,1)S(1)}, u32[]{:S(2)}, u32[]{:S(2)}) async-start(bf16[8,64,384]{2,1,0:T(8,128)(2,1)} %bitcast.34), calls=%async_computation.4 | async-start | bytes 786432 | tf_op jit(solution)/shard_map/all_to_all | solution.py:176
  100.8 0.0 copy-done.5
  100.8 0.7 fusion.10
  101.5 1.4 %reduce_window_sum.11 = s32[64,32]{1,0:T(8,128)} reduce-window(s32[64,32]{1,0:T(8,128)} %fusion.10, s32[]{:T(128)} %constant.13.clone.1), window={size=64x1 pad=63_0x0_0}, to_apply=%region_0.0 | reduce-window | flops 129024 | bytes 16388 | tf_op jit(solution)/shard_map/jit(cumsum)/reduce_window_sum | solution.py:186
  103.0 0.9 select_reduce_fusion
  103.9 7.6 %all-to-all-done.4 = bf16[8,64,384]{2,1,0:T(8,128)(2,1)S(1)} async-done(((bf16[8,64,384]{2,1,0:T(8,128)(2,1)}), bf16[8,64,384]{2,1,0:T(8,128)(2,1)S(1)}, u32[]{:S(2)}, u32[]{:S(2)}) %all-to-all-start.4) | async-done | bytes 393248 | tf_op jit(solution)/shard_map/all_to_all | solution.py:176
  111.5 0.7 convert_reduce_fusion
  112.2 1.2 scatter_custom_fusion
  113.4 16.8 %all_to_all.32 = bf16[32,4,384]{2,1,0:T(4,128)(2,1)S(1)} all-to-all(bf16[32,4,384]{2,1,0:T(4,128)(2,1)S(1)} %reshape.83), channel_id=1, replica_groups=mesh['req'=2,'seq'=16,'tp'=8] {'req','seq'}, dimensions={0} | all-to-all | bytes 196608 | tf_op jit(solution)/shard_map/all_to_all | solution.py:192
  130.3 0.6 copy.20
  (5 shorter events, 0.0 us)
Async XLA Ops:
  0.0 93.1 %copy-start = (bf16[512,3072]{1,0:T(8,128)(2,1)S(1)}, bf16[512,3072]{1,0:T(8,128)(2,1)}, u32[]{:S(2)}) copy-start(bf16[512,3072]{1,0:T(8,128)(2,1)} %param.18) | copy-start | bytes 9437188
  1.9 20.9 %all-to-all-start = ((bf16[16,2,32,384]{3,2,1,0:T(8,128)(2,1)}), bf16[16,2,32,384]{3,2,1,0:T(8,128)(2,1)}, u32[]{:S(2)}, u32[]{:S(2)}) async-start(bf16[16,2,32,384]{3,2,1,0:T(8,128)(2,1)} %broadcast_in_dim.7), calls=%async_computation | async-start | bytes 1572864 | tf_op jit(solution)/shard_map/all_to_all | solution.py:149
  9.6 8.1 %copy-start.3 = (bf16[2,32,2,384]{3,2,1,0:T(2,128)(2,1)S(1)}, bf16[2,32,2,384]{3,2,1,0:T(2,128)(2,1)}, u32[]{:S(2)}) copy-start(bf16[2,32,2,384]{3,2,1,0:T(2,128)(2,1)} %param.11) | copy-start | bytes 294916
  9.6 8.8 %copy-start.7 = (s32[2]{0:T(128)S(1)}, s32[2]{0:T(128)}, u32[]{:S(2)}) copy-start(s32[2]{0:T(128)} %param.13) | copy-start | bytes 28
  51.9 15.6 %all-to-all-start.1 = ((bf16[16,2,32,384]{3,2,1,0:T(8,128)(2,1)}), bf16[16,2,32,384]{3,2,1,0:T(8,128)(2,1)}, u32[]{:S(2)}, u32[]{:S(2)}) async-start(bf16[16,2,32,384]{3,2,1,0:T(8,128)(2,1)} %get-tuple-element.7), calls=%async_computation.1 | async-start | bytes 1572864 | tf_op jit(solution)/shard_map/all_to_all | solution.py:153
  57.5 34.2 %copy-start.4 = (f32[3072]{0:T(1024)S(1)}, f32[3072]{0:T(1024)}, u32[]{:S(2)}) copy-start(f32[3072]{0:T(1024)} %param.15) | copy-start | bytes 36868
  70.9 20.8 %copy-start.2 = (bf16[3072,512]{1,0:T(8,128)(2,1)S(1)}, bf16[3072,512]{1,0:T(8,128)(2,1)}, u32[]{:S(2)}) copy-start(bf16[3072,512]{1,0:T(8,128)(2,1)} %param.16) | copy-start | bytes 9437188
  90.8 0.9 copy-start.1
  91.0 0.7 copy-start.6
  93.1 7.7 %copy-start.5 = (s32[1,64,1]{1,2,0:T(1,128)S(1)}, s32[1,64,1]{1,2,0:T(1,128)}, u32[]{:S(2)}) copy-start(s32[1,64,1]{1,2,0:T(1,128)} %param.19) | copy-start | bytes 772
  97.4 14.1 %all-to-all-start.4 = ((bf16[8,64,384]{2,1,0:T(8,128)(2,1)}), bf16[8,64,384]{2,1,0:T(8,128)(2,1)S(1)}, u32[]{:S(2)}, u32[]{:S(2)}) async-start(bf16[8,64,384]{2,1,0:T(8,128)(2,1)} %bitcast.34), calls=%async_computation.4 | async-start | bytes 786432 | tf_op jit(solution)/shard_map/all_to_all | solution.py:176

commit v5 on v4

--- a/solution.py
+++ b/solution.py
@@ -10,6 +10,7 @@
 HEAD = 96
 
 masked_floor = -1e30
+LANE = 128
 
 
 def attention_kernel(meta_ref, q_ref, kc_ref, vc_ref, kf_ref, vf_ref, sum_ref, stat_ref, *, tq, heads):
@@ -38,28 +39,33 @@
         if with_cache:
             kc = kc_ref[...]
             vc = vc_ref[...]
-        weighted = jnp.zeros((tq, width), jnp.float32)
+        tiles = [jnp.zeros((tq, LANE), jnp.float32) for _ in range(width // LANE)]
         stats = jnp.zeros((tq, 2 * heads), jnp.float32)
         for h in range(heads):
+            lo = h * HEAD // LANE * LANE
+            hi = -(-(h + 1) * HEAD // LANE) * LANE
             head_lanes = (lane >= h * HEAD) & (lane < (h + 1) * HEAD)
-            qh = jnp.where(head_lanes, q, jnp.zeros_like(q))
-            sf = lax.dot_general(qh, kf, contract, preferred_element_type=jnp.float32) * scale
+            qh = jnp.where(head_lanes[:, lo:hi], q[:, lo:hi], jnp.zeros_like(q[:, lo:hi]))
+            sf = lax.dot_general(qh, kf[:, lo:hi], contract, preferred_element_type=jnp.float32)
             sf = jnp.where(fresh_visible, sf, masked_floor)
             peak = jnp.max(sf, axis=-1, keepdims=True)
             if with_cache:
-                sc = lax.dot_general(qh, kc, contract, preferred_element_type=jnp.float32) * scale
+                sc = lax.dot_general(qh, kc[:, lo:hi], contract, preferred_element_type=jnp.float32)
                 sc = jnp.where(cached_visible, sc, masked_floor)
                 peak = jnp.maximum(peak, jnp.max(sc, axis=-1, keepdims=True))
-            pf = jnp.where(fresh_visible, jnp.exp(sf - peak), 0.0)
+            pf = jnp.where(fresh_visible, jnp.exp((sf - peak) * scale), 0.0)
             total = jnp.sum(pf, axis=-1, keepdims=True)
-            oh = jnp.dot(pf.astype(jnp.bfloat16), vf, preferred_element_type=jnp.float32)
+            oh = jnp.dot(pf.astype(jnp.bfloat16), vf[:, lo:hi], preferred_element_type=jnp.float32)
             if with_cache:
-                pc = jnp.where(cached_visible, jnp.exp(sc - peak), 0.0)
+                pc = jnp.exp((sc - peak) * scale)
                 total = total + jnp.sum(pc, axis=-1, keepdims=True)
-                oh = oh + jnp.dot(pc.astype(jnp.bfloat16), vc, preferred_element_type=jnp.float32)
-            weighted = jnp.where(head_lanes, oh, weighted)
-            stats = jnp.where(stat_lane == h, peak, stats)
+                oh = oh + jnp.dot(pc.astype(jnp.bfloat16), vc[:, lo:hi], preferred_element_type=jnp.float32)
+            for j in range(lo // LANE, hi // LANE):
+                part = oh[:, j * LANE - lo:(j + 1) * LANE - lo]
+                tiles[j] = jnp.where(head_lanes[:, j * LANE:(j + 1) * LANE], part, tiles[j])
+            stats = jnp.where(stat_lane == h, peak * scale, stats)
             stats = jnp.where(stat_lane == heads + h, total, stats)
+        weighted = jnp.concatenate(tiles, axis=1)
         sum_ref[...] = weighted.reshape(sum_ref.shape).astype(sum_ref.dtype)
         stat_ref[...] = stats.reshape(stat_ref.shape)
 

time: 132 us -> 126 us (0.955)
  Pallas kernels: 22 us -> 15.8 us
    pallas_call x1, Pallas kernels: 18.7 us -> 12.4 us  [local_attention(): pl.pallas_call(kernel, grid_spec=grid_spec, out_shape=[jax.ShapeDtypeStru...]
  transfers between devices with their start and end apart: 3 -> 3, of which waited for: 3 -> 3; matrix products, arithmetic and copies ran while one was open for 11% -> 12% of each run, Pallas kernels for 0% -> 0%
where the time goes in v5:
time: 126 us; the launch traced here: 125 us
  blocking collectives  44.7 us (35%)
  waiting for transfers between devices  20.4 us (16%)
  local copies, waits for them, and re-layouts  16.9 us (13%)
  Pallas kernels  15.8 us (13%)
  starting transfers between devices  15.4 us (12%)
  other arithmetic  6.55 us (5%)
  matrix products  4.84 us (4%)
    all_to_all x1, blocking collectives, per_device(): lax.all_to_all(jnp.broadcast_to(block_rows[None], (tp_count,) + block_row...  18.8 us
    all_to_all x1, blocking collectives, per_device(): lax.all_to_all(outgoing.reshape(owner_count, slot_cap, width_local), ('re...  16.8 us
    pallas_call x1, Pallas kernels, local_attention(): pl.pallas_call(kernel, grid_spec=grid_spec, out_shape=[jax.ShapeDtypeStru...  12.4 us
    all_to_all x1, blocking collectives, per_device(): source_stats = lax.all_to_all(partial_stats, 'seq', 0, 0, tiled=True)  9 us
    all_to_all x1, waiting for transfers between devices, per_device(): source_sum = lax.all_to_all(partial_sum, 'seq', 0, 0, tiled=True)  8.98 us
    reshape x1, local copies, waits for them, and re-layouts, local_attention(): cache2 = cache_kv.reshape(slot_count, span, 2 * width)  8.08 us
    all_to_all x1, starting transfers between devices, per_device(): lax.all_to_all(jnp.broadcast_to(queries[None], (seq_count,) + queries.sha...  7.62 us
    all_to_all x1, waiting for transfers between devices, per_device(): lax.all_to_all(pieces, 'tp', 0, 0, tiled=True).astype(jnp.float32)  7.57 us
  transfers between devices with their start and end apart: 3, of which 3 were waited for; matrix products, arithmetic and copies ran while one was open for 12% of the time, Pallas kernels for 0%

profile of v5, /device:TPU:1, one launch (start us, length us, event | category | flops | bytes accessed | tf_op | source)
XLA Modules:
  0.0 124.7 jit_solution(13570579925917691538)
XLA Ops:
  0.0 0.0 copy-start
  0.0 1.9 %broadcast_in_dim.7 = bf16[16,2,32,384]{3,2,1,0:T(8,128)(2,1)} broadcast(bf16[2,32,384]{2,1,0:T(8,128)(2,1)} %param.10), dimensions={1,2,3} | broadcast | bytes 835584 | tf_op jit(solution)/shard_map/broadcast_in_dim | solution.py:156
  1.9 7.6 %all-to-all-start = ((bf16[16,2,32,384]{3,2,1,0:T(8,128)(2,1)}), bf16[16,2,32,384]{3,2,1,0:T(8,128)(2,1)}, u32[]{:S(2)}, u32[]{:S(2)}) async-start(bf16[16,2,32,384]{3,2,1,0:T(8,128)(2,1)} %broadcast_in_dim.7), calls=%async_computation | async-start | bytes 1572864 | tf_op jit(solution)/shard_map/all_to_all | solution.py:155
  9.6 0.0 copy-start.3
  9.6 0.0 copy-start.7
  9.6 8.1 %reshape.77.kc_ref.vc_ref = bf16[2,1024,768]{2,1,0:T(8,128)(2,1)} reshape(bf16[2,1024,2,384]{3,2,1,0:T(2,128)(2,1)} %param.12) | data formatting | bytes 6291456 | tf_op jit(solution)/shard_map/reshape | solution.py:88
  17.7 0.0 copy-done.3
  17.7 0.7 reshape.78.kf_ref.vf_ref
  18.4 0.0 copy-done.7
  18.4 0.6 pad_add_fusion.meta_ref
  19.0 3.9 %all-to-all-done.q_ref = bf16[16,2,32,384]{3,2,1,0:T(8,128)(2,1)} async-done(((bf16[16,2,32,384]{3,2,1,0:T(8,128)(2,1)}), bf16[16,2,32,384]{3,2,1,0:T(8,128)(2,1)}, u32[]{:S(2)}, u32[]{:S(2)}) %all-to-all-start) | async-done | bytes 786464 | tf_op jit(solution)/shard_map/all_to_all | solution.py:155
  22.9 12.4 %shard_map.100 = (bf16[16,2,32,384]{3,2,1,0:T(8,128)(2,1)}, f32[16,2,32,8]{3,2,1,0:T(8,128)}) custom-call(s32[3]{0:T(128)} %pad_add_fusion.meta_ref, bf16[16,2,32,384]{3,2,1,0:T(8,128)(2,1)} %all-to-all-done.q_ref, bf16[2,1024,768]{2,1,0:T(8,128)(2,1)} %reshape.77.kc_ref.vc_ref, bf16[2,1024,768]{2,1,0:T(8,128)(2,1)} %reshape.77.kc_ref.vc_ref, ...), custom_call_target="tpu_custom_call" | custom-call | tf_op jit(solution)/shard_map/pallas_call | solution.py:107
  35.3 1.2 copy.11
  36.5 0.1 reshape.96
  36.6 9.0 %all_to_all.30 = f32[16,1,512]{2,1,0:T(1,128)S(1)} all-to-all(f32[16,1,512]{2,1,0:T(1,128)S(1)} %reshape.96), channel_id=1, replica_groups=mesh['req'=2,'seq'=16,'tp'=8] {'seq'}, dimensions={0} | all-to-all | bytes 65536 | tf_op jit(solution)/shard_map/all_to_all | solution.py:160
  45.6 4.3 %all-to-all-start.1 = ((bf16[16,2,32,384]{3,2,1,0:T(8,128)(2,1)}), bf16[16,2,32,384]{3,2,1,0:T(8,128)(2,1)}, u32[]{:S(2)}, u32[]{:S(2)}) async-start(bf16[16,2,32,384]{3,2,1,0:T(8,128)(2,1)} %get-tuple-element.7), calls=%async_computation.1 | async-start | bytes 1572864 | tf_op jit(solution)/shard_map/all_to_all | solution.py:159
  49.9 0.5 broadcast.58
  50.4 0.7 reduce.2
  51.2 0.1 reshape.97
  51.3 0.0 copy-start.4
  51.3 1.0 copy.12
  52.3 9.0 %all-to-all-done.1 = bf16[16,2,32,384]{3,2,1,0:T(8,128)(2,1)} async-done(((bf16[16,2,32,384]{3,2,1,0:T(8,128)(2,1)}), bf16[16,2,32,384]{3,2,1,0:T(8,128)(2,1)}, u32[]{:S(2)}, u32[]{:S(2)}) %all-to-all-start.1) | async-done | bytes 786464 | tf_op jit(solution)/shard_map/all_to_all | solution.py:159
  61.3 3.3 %shard_map.101 = bf16[64,384]{1,0:T(8,128)(2,1)} custom-call(bf16[16,64,384]{2,1,0:T(8,128)(2,1)} %bitcast.5.sum_ref, f32[16,64,8]{2,1,0:T(8,128)} %bitcast.32, bf16[64,384]{1,0:T(8,128)(2,1)} %bitcast.38), custom_call_target="tpu_custom_call" | custom-call | tf_op jit(solution)/shard_map/pallas_call | solution.py:136
  64.6 0.0 copy-start.2
  64.6 1.0 broadcast_in_dim.8
  65.6 18.8 %all_to_all.31 = bf16[8,64,384]{2,1,0:T(8,128)(2,1)S(1)} all-to-all(bf16[8,64,384]{2,1,0:T(8,128)(2,1)S(1)} %broadcast_in_dim.8), channel_id=1, replica_groups=mesh['req'=2,'seq'=16,'tp'=8] {'tp'}, dimensions={0} | all-to-all | bytes 786432 | tf_op jit(solution)/shard_map/all_to_all | solution.py:169
  84.5 0.1 convert_bitcast_fusion
  84.5 0.1 copy.16
  84.6 0.0 copy-start.1
  84.6 0.2 fusion.1
  84.8 0.7 copy-done.1
  85.5 0.0 copy-done.6
  85.5 0.0 copy-done.4
  85.5 0.0 copy-done.2
  85.5 1.4 %fusion.13 = f32[64,512]{1,0:T(8,128)} fusion(bf16[3072,512]{1,0:T(8,128)(2,1)S(1)} %copy-done.2, f32[64,3072]{1,0:T(8,128)S(1)} %bitcast.30, f32[3072]{0:T(1024)S(1)} %copy-done.4, f32[64]{0:T(128)S(1)} %add_rsqrt_fusion), kind=kOutput, calls=%fused_computation.28 | convolution fusion | flops 201916416 | bytes 4075776 | tf_op jit(solution)/shard_map/dot_general | solution.py:176
  86.8 0.0 copy-done
  86.8 3.5 %convolution_convert_fusion = bf16[64,3072]{1,0:T(8,128)(2,1)S(1)} fusion(bf16[512,3072]{1,0:T(8,128)(2,1)S(1)} %copy-done, bf16[3072,512]{1,0:T(8,128)(2,1)} %param.17, f32[64,512]{1,0:T(8,128)} %fusion.13, f32[64,3072]{1,0:T(8,128)} %bitcast.31, f32[3072]{0:T(1024)S(1)} %copy-done.4, f32[64]{0:T(128)} %copy-done.6), kind=kOutput, calls=%fused_computation.1 | convolution fusion | flops 403636224 | bytes 7614720 | tf_op jit(solution)/shard_map/dot_general | solution.py:179
  90.3 0.8 copy.18
  91.1 3.5 %all-to-all-start.4 = ((bf16[8,64,384]{2,1,0:T(8,128)(2,1)}), bf16[8,64,384]{2,1,0:T(8,128)(2,1)S(1)}, u32[]{:S(2)}, u32[]{:S(2)}) async-start(bf16[8,64,384]{2,1,0:T(8,128)(2,1)} %bitcast.34), calls=%async_computation.4 | async-start | bytes 786432 | tf_op jit(solution)/shard_map/all_to_all | solution.py:182
  94.6 0.0 copy-done.5
  94.6 0.7 fusion.10
  95.3 1.4 %reduce_window_sum.11 = s32[64,32]{1,0:T(8,128)} reduce-window(s32[64,32]{1,0:T(8,128)} %fusion.10, s32[]{:T(128)} %constant.13.clone.1), window={size=64x1 pad=63_0x0_0}, to_apply=%region_0.0 | reduce-window | flops 129024 | bytes 16388 | tf_op jit(solution)/shard_map/jit(cumsum)/reduce_window_sum | solution.py:192
  96.7 0.9 select_reduce_fusion
  97.6 7.6 %all-to-all-done.4 = bf16[8,64,384]{2,1,0:T(8,128)(2,1)S(1)} async-done(((bf16[8,64,384]{2,1,0:T(8,128)(2,1)}), bf16[8,64,384]{2,1,0:T(8,128)(2,1)S(1)}, u32[]{:S(2)}, u32[]{:S(2)}) %all-to-all-start.4) | async-done | bytes 393248 | tf_op jit(solution)/shard_map/all_to_all | solution.py:182
  105.2 0.7 convert_reduce_fusion
  105.9 1.2 scatter_custom_fusion
  107.2 16.8 %all_to_all.32 = bf16[32,4,384]{2,1,0:T(4,128)(2,1)S(1)} all-to-all(bf16[32,4,384]{2,1,0:T(4,128)(2,1)S(1)} %reshape.83), channel_id=1, replica_groups=mesh['req'=2,'seq'=16,'tp'=8] {'req','seq'}, dimensions={0} | all-to-all | bytes 196608 | tf_op jit(solution)/shard_map/all_to_all | solution.py:198
  124.0 0.6 copy.20
  (5 shorter events, 0.0 us)
Async XLA Ops:
  0.0 86.8 %copy-start = (bf16[512,3072]{1,0:T(8,128)(2,1)S(1)}, bf16[512,3072]{1,0:T(8,128)(2,1)}, u32[]{:S(2)}) copy-start(bf16[512,3072]{1,0:T(8,128)(2,1)} %param.18) | copy-start | bytes 9437188
  1.9 20.9 %all-to-all-start = ((bf16[16,2,32,384]{3,2,1,0:T(8,128)(2,1)}), bf16[16,2,32,384]{3,2,1,0:T(8,128)(2,1)}, u32[]{:S(2)}, u32[]{:S(2)}) async-start(bf16[16,2,32,384]{3,2,1,0:T(8,128)(2,1)} %broadcast_in_dim.7), calls=%async_computation | async-start | bytes 1572864 | tf_op jit(solution)/shard_map/all_to_all | solution.py:155
  9.6 8.1 %copy-start.3 = (bf16[2,32,2,384]{3,2,1,0:T(2,128)(2,1)S(1)}, bf16[2,32,2,384]{3,2,1,0:T(2,128)(2,1)}, u32[]{:S(2)}) copy-start(bf16[2,32,2,384]{3,2,1,0:T(2,128)(2,1)} %param.11) | copy-start | bytes 294916
  9.6 8.8 %copy-start.7 = (s32[2]{0:T(128)S(1)}, s32[2]{0:T(128)}, u32[]{:S(2)}) copy-start(s32[2]{0:T(128)} %param.13) | copy-start | bytes 28
  45.6 15.6 %all-to-all-start.1 = ((bf16[16,2,32,384]{3,2,1,0:T(8,128)(2,1)}), bf16[16,2,32,384]{3,2,1,0:T(8,128)(2,1)}, u32[]{:S(2)}, u32[]{:S(2)}) async-start(bf16[16,2,32,384]{3,2,1,0:T(8,128)(2,1)} %get-tuple-element.7), calls=%async_computation.1 | async-start | bytes 1572864 | tf_op jit(solution)/shard_map/all_to_all | solution.py:159
  51.3 34.2 %copy-start.4 = (f32[3072]{0:T(1024)S(1)}, f32[3072]{0:T(1024)}, u32[]{:S(2)}) copy-start(f32[3072]{0:T(1024)} %param.15) | copy-start | bytes 36868
  64.6 20.8 %copy-start.2 = (bf16[3072,512]{1,0:T(8,128)(2,1)S(1)}, bf16[3072,512]{1,0:T(8,128)(2,1)}, u32[]{:S(2)}) copy-start(bf16[3072,512]{1,0:T(8,128)(2,1)} %param.16) | copy-start | bytes 9437188
  84.6 0.9 copy-start.1
  84.8 0.7 copy-start.6
  86.8 7.7 %copy-start.5 = (s32[1,64,1]{1,2,0:T(1,128)S(1)}, s32[1,64,1]{1,2,0:T(1,128)}, u32[]{:S(2)}) copy-start(s32[1,64,1]{1,2,0:T(1,128)} %param.19) | copy-start | bytes 772
  91.1 14.1 %all-to-all-start.4 = ((bf16[8,64,384]{2,1,0:T(8,128)(2,1)}), bf16[8,64,384]{2,1,0:T(8,128)(2,1)S(1)}, u32[]{:S(2)}, u32[]{:S(2)}) async-start(bf16[8,64,384]{2,1,0:T(8,128)(2,1)} %bitcast.34), calls=%async_computation.4 | async-start | bytes 786432 | tf_op jit(solution)/shard_map/all_to_all | solution.py:182

commit v6 on v5

--- a/solution.py
+++ b/solution.py
@@ -33,7 +33,7 @@
     cached_visible = (offset + lax.broadcasted_iota(jnp.int32, (1, span), 1)) < length
     contract = (((1,), (1,)), ((), ()))
 
-    def run(with_cache):
+    def run(with_cache, masked=True):
         kf = kf_ref[...]
         vf = vf_ref[...]
         if with_cache:
@@ -51,7 +51,8 @@
             peak = jnp.max(sf, axis=-1, keepdims=True)
             if with_cache:
                 sc = lax.dot_general(qh, kc[:, lo:hi], contract, preferred_element_type=jnp.float32)
-                sc = jnp.where(cached_visible, sc, masked_floor)
+                if masked:
+                    sc = jnp.where(cached_visible, sc, masked_floor)
                 peak = jnp.maximum(peak, jnp.max(sc, axis=-1, keepdims=True))
             pf = jnp.where(fresh_visible, jnp.exp((sf - peak) * scale), 0.0)
             total = jnp.sum(pf, axis=-1, keepdims=True)
@@ -69,9 +70,13 @@
         sum_ref[...] = weighted.reshape(sum_ref.shape).astype(sum_ref.dtype)
         stat_ref[...] = stats.reshape(stat_ref.shape)
 
-    @pl.when(offset < length)
+    @pl.when((offset < length) & (offset + span > length))
     def _():
         run(True)
+
+    @pl.when(offset + span <= length)
+    def _():
+        run(True, masked=False)
 
     @pl.when(offset >= length)
     def _():

time: 126 us -> 126 us (level)
  no operation moved by 1% of the time
where the time goes in v6:
time: 126 us; the launch traced here: 125 us
  blocking collectives  44.3 us (35%)
  waiting for transfers between devices  21 us (17%)
  local copies, waits for them, and re-layouts  16.9 us (13%)
  Pallas kernels  15.8 us (13%)
  starting transfers between devices  15.4 us (12%)
  other arithmetic  6.55 us (5%)
  matrix products  4.85 us (4%)
    all_to_all x1, blocking collectives, per_device(): lax.all_to_all(jnp.broadcast_to(block_rows[None], (tp_count,) + block_row...  18.7 us
    all_to_all x1, blocking collectives, per_device(): lax.all_to_all(outgoing.reshape(owner_count, slot_cap, width_local), ('re...  16.6 us
    pallas_call x1, Pallas kernels, local_attention(): pl.pallas_call(kernel, grid_spec=grid_spec, out_shape=[jax.ShapeDtypeStru...  12.4 us
    all_to_all x1, waiting for transfers between devices, per_device(): source_sum = lax.all_to_all(partial_sum, 'seq', 0, 0, tiled=True)  9.46 us
    all_to_all x1, blocking collectives, per_device(): source_stats = lax.all_to_all(partial_stats, 'seq', 0, 0, tiled=True)  9 us
    reshape x1, local copies, waits for them, and re-layouts, local_attention(): cache2 = cache_kv.reshape(slot_count, span, 2 * width)  8.08 us
    all_to_all x1, waiting for transfers between devices, per_device(): lax.all_to_all(pieces, 'tp', 0, 0, tiled=True).astype(jnp.float32)  7.67 us
    all_to_all x1, starting transfers between devices, per_device(): lax.all_to_all(jnp.broadcast_to(queries[None], (seq_count,) + queries.sha...  7.62 us
  transfers between devices with their start and end apart: 3, of which 3 were waited for; matrix products, arithmetic and copies ran while one was open for 12% of the time, Pallas kernels for 0%

profile of v6, /device:TPU:1, one launch (start us, length us, event | category | flops | bytes accessed | tf_op | source)
XLA Modules:
  0.0 124.8 jit_solution(9450759604475725763)
XLA Ops:
  0.0 0.0 copy-start
  0.0 1.9 %broadcast_in_dim.7 = bf16[16,2,32,384]{3,2,1,0:T(8,128)(2,1)} broadcast(bf16[2,32,384]{2,1,0:T(8,128)(2,1)} %param.10), dimensions={1,2,3} | broadcast | bytes 835584 | tf_op jit(solution)/shard_map/broadcast_in_dim | solution.py:161
  1.9 7.6 %all-to-all-start = ((bf16[16,2,32,384]{3,2,1,0:T(8,128)(2,1)}), bf16[16,2,32,384]{3,2,1,0:T(8,128)(2,1)}, u32[]{:S(2)}, u32[]{:S(2)}) async-start(bf16[16,2,32,384]{3,2,1,0:T(8,128)(2,1)} %broadcast_in_dim.7), calls=%async_computation | async-start | bytes 1572864 | tf_op jit(solution)/shard_map/all_to_all | solution.py:160
  9.6 0.0 copy-start.3
  9.6 0.0 copy-start.7
  9.6 8.1 %reshape.77.kc_ref.vc_ref = bf16[2,1024,768]{2,1,0:T(8,128)(2,1)} reshape(bf16[2,1024,2,384]{3,2,1,0:T(2,128)(2,1)} %param.12) | data formatting | bytes 6291456 | tf_op jit(solution)/shard_map/reshape | solution.py:93
  17.7 0.0 copy-done.3
  17.7 0.7 reshape.78.kf_ref.vf_ref
  18.4 0.0 copy-done.7
  18.4 0.6 pad_add_fusion.meta_ref
  19.0 3.9 %all-to-all-done.q_ref = bf16[16,2,32,384]{3,2,1,0:T(8,128)(2,1)} async-done(((bf16[16,2,32,384]{3,2,1,0:T(8,128)(2,1)}), bf16[16,2,32,384]{3,2,1,0:T(8,128)(2,1)}, u32[]{:S(2)}, u32[]{:S(2)}) %all-to-all-start) | async-done | bytes 786464 | tf_op jit(solution)/shard_map/all_to_all | solution.py:160
  22.9 12.4 %shard_map.100 = (bf16[16,2,32,384]{3,2,1,0:T(8,128)(2,1)}, f32[16,2,32,8]{3,2,1,0:T(8,128)}) custom-call(s32[3]{0:T(128)} %pad_add_fusion.meta_ref, bf16[16,2,32,384]{3,2,1,0:T(8,128)(2,1)} %all-to-all-done.q_ref, bf16[2,1024,768]{2,1,0:T(8,128)(2,1)} %reshape.77.kc_ref.vc_ref, bf16[2,1024,768]{2,1,0:T(8,128)(2,1)} %reshape.77.kc_ref.vc_ref, ...), custom_call_target="tpu_custom_call" | custom-call | tf_op jit(solution)/shard_map/pallas_call | solution.py:112
  35.3 1.2 copy.11
  36.5 0.1 reshape.96
  36.6 9.0 %all_to_all.30 = f32[16,1,512]{2,1,0:T(1,128)S(1)} all-to-all(f32[16,1,512]{2,1,0:T(1,128)S(1)} %reshape.96), channel_id=1, replica_groups=mesh['req'=2,'seq'=16,'tp'=8] {'seq'}, dimensions={0} | all-to-all | bytes 65536 | tf_op jit(solution)/shard_map/all_to_all | solution.py:165
  45.6 4.3 %all-to-all-start.1 = ((bf16[16,2,32,384]{3,2,1,0:T(8,128)(2,1)}), bf16[16,2,32,384]{3,2,1,0:T(8,128)(2,1)}, u32[]{:S(2)}, u32[]{:S(2)}) async-start(bf16[16,2,32,384]{3,2,1,0:T(8,128)(2,1)} %get-tuple-element.7), calls=%async_computation.1 | async-start | bytes 1572864 | tf_op jit(solution)/shard_map/all_to_all | solution.py:164
  49.9 0.5 broadcast.58
  50.4 0.7 reduce.2
  51.2 0.1 reshape.97
  51.3 0.0 copy-start.4
  51.3 1.0 copy.12
  52.3 9.5 %all-to-all-done.1 = bf16[16,2,32,384]{3,2,1,0:T(8,128)(2,1)} async-done(((bf16[16,2,32,384]{3,2,1,0:T(8,128)(2,1)}), bf16[16,2,32,384]{3,2,1,0:T(8,128)(2,1)}, u32[]{:S(2)}, u32[]{:S(2)}) %all-to-all-start.1) | async-done | bytes 786464 | tf_op jit(solution)/shard_map/all_to_all | solution.py:164
  61.7 3.3 %shard_map.101 = bf16[64,384]{1,0:T(8,128)(2,1)} custom-call(bf16[16,64,384]{2,1,0:T(8,128)(2,1)} %bitcast.5.sum_ref, f32[16,64,8]{2,1,0:T(8,128)} %bitcast.32, bf16[64,384]{1,0:T(8,128)(2,1)} %bitcast.38), custom_call_target="tpu_custom_call" | custom-call | tf_op jit(solution)/shard_map/pallas_call | solution.py:141
  65.1 0.0 copy-start.2
  65.1 1.0 broadcast_in_dim.8
  66.1 18.7 %all_to_all.31 = bf16[8,64,384]{2,1,0:T(8,128)(2,1)S(1)} all-to-all(bf16[8,64,384]{2,1,0:T(8,128)(2,1)S(1)} %broadcast_in_dim.8), channel_id=1, replica_groups=mesh['req'=2,'seq'=16,'tp'=8] {'tp'}, dimensions={0} | all-to-all | bytes 786432 | tf_op jit(solution)/shard_map/all_to_all | solution.py:174
  84.7 0.1 convert_bitcast_fusion
  84.8 0.1 copy.16
  84.9 0.0 copy-start.1
  84.9 0.2 fusion.1
  85.1 0.7 copy-done.1
  85.8 0.0 copy-done.6
  85.8 0.0 copy-done.4
  85.8 0.0 copy-done.2
  85.8 1.4 %fusion.13 = f32[64,512]{1,0:T(8,128)} fusion(bf16[3072,512]{1,0:T(8,128)(2,1)S(1)} %copy-done.2, f32[64,3072]{1,0:T(8,128)S(1)} %bitcast.30, f32[3072]{0:T(1024)S(1)} %copy-done.4, f32[64]{0:T(128)S(1)} %add_rsqrt_fusion), kind=kOutput, calls=%fused_computation.28 | convolution fusion | flops 201916416 | bytes 4075776 | tf_op jit(solution)/shard_map/dot_general | solution.py:181
  87.1 0.0 copy-done
  87.1 3.5 %convolution_convert_fusion = bf16[64,3072]{1,0:T(8,128)(2,1)S(1)} fusion(bf16[512,3072]{1,0:T(8,128)(2,1)S(1)} %copy-done, bf16[3072,512]{1,0:T(8,128)(2,1)} %param.17, f32[64,512]{1,0:T(8,128)} %fusion.13, f32[64,3072]{1,0:T(8,128)} %bitcast.31, f32[3072]{0:T(1024)S(1)} %copy-done.4, f32[64]{0:T(128)} %copy-done.6), kind=kOutput, calls=%fused_computation.1 | convolution fusion | flops 403636224 | bytes 7614720 | tf_op jit(solution)/shard_map/dot_general | solution.py:184
  90.6 0.8 copy.18
  91.4 3.5 %all-to-all-start.4 = ((bf16[8,64,384]{2,1,0:T(8,128)(2,1)}), bf16[8,64,384]{2,1,0:T(8,128)(2,1)S(1)}, u32[]{:S(2)}, u32[]{:S(2)}) async-start(bf16[8,64,384]{2,1,0:T(8,128)(2,1)} %bitcast.34), calls=%async_computation.4 | async-start | bytes 786432 | tf_op jit(solution)/shard_map/all_to_all | solution.py:187
  94.9 0.0 copy-done.5
  94.9 0.7 fusion.10
  95.6 1.4 %reduce_window_sum.11 = s32[64,32]{1,0:T(8,128)} reduce-window(s32[64,32]{1,0:T(8,128)} %fusion.10, s32[]{:T(128)} %constant.13.clone.1), window={size=64x1 pad=63_0x0_0}, to_apply=%region_0.0 | reduce-window | flops 129024 | bytes 16388 | tf_op jit(solution)/shard_map/jit(cumsum)/reduce_window_sum | solution.py:197
  97.0 0.9 select_reduce_fusion
  97.9 7.7 %all-to-all-done.4 = bf16[8,64,384]{2,1,0:T(8,128)(2,1)S(1)} async-done(((bf16[8,64,384]{2,1,0:T(8,128)(2,1)}), bf16[8,64,384]{2,1,0:T(8,128)(2,1)S(1)}, u32[]{:S(2)}, u32[]{:S(2)}) %all-to-all-start.4) | async-done | bytes 393248 | tf_op jit(solution)/shard_map/all_to_all | solution.py:187
  105.6 0.7 convert_reduce_fusion
  106.3 1.2 scatter_custom_fusion
  107.6 16.6 %all_to_all.32 = bf16[32,4,384]{2,1,0:T(4,128)(2,1)S(1)} all-to-all(bf16[32,4,384]{2,1,0:T(4,128)(2,1)S(1)} %reshape.83), channel_id=1, replica_groups=mesh['req'=2,'seq'=16,'tp'=8] {'req','seq'}, dimensions={0} | all-to-all | bytes 196608 | tf_op jit(solution)/shard_map/all_to_all | solution.py:203
  124.2 0.6 copy.20
  (5 shorter events, 0.0 us)
Async XLA Ops:
  0.0 87.1 %copy-start = (bf16[512,3072]{1,0:T(8,128)(2,1)S(1)}, bf16[512,3072]{1,0:T(8,128)(2,1)}, u32[]{:S(2)}) copy-start(bf16[512,3072]{1,0:T(8,128)(2,1)} %param.18) | copy-start | bytes 9437188
  1.9 20.9 %all-to-all-start = ((bf16[16,2,32,384]{3,2,1,0:T(8,128)(2,1)}), bf16[16,2,32,384]{3,2,1,0:T(8,128)(2,1)}, u32[]{:S(2)}, u32[]{:S(2)}) async-start(bf16[16,2,32,384]{3,2,1,0:T(8,128)(2,1)} %broadcast_in_dim.7), calls=%async_computation | async-start | bytes 1572864 | tf_op jit(solution)/shard_map/all_to_all | solution.py:160
  9.6 8.1 %copy-start.3 = (bf16[2,32,2,384]{3,2,1,0:T(2,128)(2,1)S(1)}, bf16[2,32,2,384]{3,2,1,0:T(2,128)(2,1)}, u32[]{:S(2)}) copy-start(bf16[2,32,2,384]{3,2,1,0:T(2,128)(2,1)} %param.11) | copy-start | bytes 294916
  9.6 8.8 %copy-start.7 = (s32[2]{0:T(128)S(1)}, s32[2]{0:T(128)}, u32[]{:S(2)}) copy-start(s32[2]{0:T(128)} %param.13) | copy-start | bytes 28
  45.6 16.1 %all-to-all-start.1 = ((bf16[16,2,32,384]{3,2,1,0:T(8,128)(2,1)}), bf16[16,2,32,384]{3,2,1,0:T(8,128)(2,1)}, u32[]{:S(2)}, u32[]{:S(2)}) async-start(bf16[16,2,32,384]{3,2,1,0:T(8,128)(2,1)} %get-tuple-element.7), calls=%async_computation.1 | async-start | bytes 1572864 | tf_op jit(solution)/shard_map/all_to_all | solution.py:164
  51.3 34.5 %copy-start.4 = (f32[3072]{0:T(1024)S(1)}, f32[3072]{0:T(1024)}, u32[]{:S(2)}) copy-start(f32[3072]{0:T(1024)} %param.15) | copy-start | bytes 36868
  65.1 20.7 %copy-start.2 = (bf16[3072,512]{1,0:T(8,128)(2,1)S(1)}, bf16[3072,512]{1,0:T(8,128)(2,1)}, u32[]{:S(2)}) copy-start(bf16[3072,512]{1,0:T(8,128)(2,1)} %param.16) | copy-start | bytes 9437188
  84.9 0.9 copy-start.1
  85.1 0.7 copy-start.6
  87.1 7.7 %copy-start.5 = (s32[1,64,1]{1,2,0:T(1,128)S(1)}, s32[1,64,1]{1,2,0:T(1,128)}, u32[]{:S(2)}) copy-start(s32[1,64,1]{1,2,0:T(1,128)} %param.19) | copy-start | bytes 772
  91.4 14.2 %all-to-all-start.4 = ((bf16[8,64,384]{2,1,0:T(8,128)(2,1)}), bf16[8,64,384]{2,1,0:T(8,128)(2,1)S(1)}, u32[]{:S(2)}, u32[]{:S(2)}) async-start(bf16[8,64,384]{2,1,0:T(8,128)(2,1)} %bitcast.34), calls=%async_computation.4 | async-start | bytes 786432 | tf_op jit(solution)/shard_map/all_to_all | solution.py:187

commit v7 on v6

--- a/solution.py
+++ b/solution.py
@@ -89,9 +89,9 @@
     span = cache_kv.shape[1]
     fresh_count = new_kv.shape[1]
     heads = width // HEAD
-    tq = 256 if query_count % 256 == 0 else query_count
-    cache2 = cache_kv.reshape(slot_count, span, 2 * width)
-    fresh2 = new_kv.reshape(slot_count, fresh_count, 2 * width)
+    tq = query_count
+    cache2 = cache_kv.transpose(0, 2, 1, 3)
+    fresh2 = new_kv.transpose(0, 2, 1, 3)
     meta = jnp.concatenate([jnp.reshape(seq_index, (1,)).astype(jnp.int32), cached_len.astype(jnp.int32)])
     kernel = functools.partial(attention_kernel, tq=tq, heads=heads)
     grid_spec = pltpu.PrefetchScalarGridSpec(
@@ -99,10 +99,10 @@
         grid=(slot_count, query_count // tq),
         in_specs=[
             pl.BlockSpec((tq // token_count, None, token_count, width), lambda s, b, m: (b, s, 0, 0)),
-            pl.BlockSpec((None, span, width), lambda s, b, m: (s, 0, 0)),
-            pl.BlockSpec((None, span, width), lambda s, b, m: (s, 0, 1)),
-            pl.BlockSpec((None, fresh_count, width), lambda s, b, m: (s, 0, 0)),
-            pl.BlockSpec((None, fresh_count, width), lambda s, b, m: (s, 0, 1)),
+            pl.BlockSpec((None, None, span, width), lambda s, b, m: (s, 0, 0, 0)),
+            pl.BlockSpec((None, None, span, width), lambda s, b, m: (s, 1, 0, 0)),
+            pl.BlockSpec((None, None, fresh_count, width), lambda s, b, m: (s, 0, 0, 0)),
+            pl.BlockSpec((None, None, fresh_count, width), lambda s, b, m: (s, 1, 0, 0)),
         ],
         out_specs=[
             pl.BlockSpec((tq // token_count, None, token_count, width), lambda s, b, m: (b, s, 0, 0)),

time: 126 us -> 124 us (0.984)
  local copies, waits for them, and re-layouts: 16.9 us -> 12.8 us
  waiting for transfers between devices: 21 us -> 23.6 us
    reshape x2 -> x0, local copies, waits for them, and re-layouts: 8.79 us -> none  [the longest x1 8.08 us: local_attention(): cache2 = cache_kv.reshape(slot_count, span, 2 * width)]
    unnamed x19 -> x21, local copies, waits for them, and re-layouts: 1.56 us -> 6.21 us
    all_to_all x1, waiting for transfers between devices: 3.86 us -> 7.99 us  [per_device(): lax.all_to_all(jnp.broadcast_to(queries[None], (seq_count,) + queries.sha...]
    all_to_all x1, waiting for transfers between devices: 9.46 us -> 7.96 us  [per_device(): source_sum = lax.all_to_all(partial_sum, 'seq', 0, 0, tiled=True)]
  transfers between devices with their start and end apart: 3 -> 3, of which waited for: 3 -> 3; matrix products, arithmetic and copies ran while one was open for 12% -> 9% of each run, Pallas kernels for 0% -> 0%
where the time goes in v7:
time: 124 us
  blocking collectives  45.5 us (37%)
  waiting for transfers between devices  23.6 us (19%)
  starting transfers between devices  15.5 us (12%)
  Pallas kernels  14.8 us (12%)
  local copies, waits for them, and re-layouts  12.8 us (10%)
  other arithmetic  6.55 us (5%)
  matrix products  4.84 us (4%)
    all_to_all x1, blocking collectives, per_device(): lax.all_to_all(jnp.broadcast_to(block_rows[None], (tp_count,) + block_row...  18.9 us
    all_to_all x1, blocking collectives, per_device(): lax.all_to_all(outgoing.reshape(owner_count, slot_cap, width_local), ('re...  17.6 us
    pallas_call x1, Pallas kernels, local_attention(): pl.pallas_call(kernel, grid_spec=grid_spec, out_shape=[jax.ShapeDtypeStru...  11.5 us
    all_to_all x1, blocking collectives, per_device(): source_stats = lax.all_to_all(partial_stats, 'seq', 0, 0, tiled=True)  9 us
    all_to_all x1, waiting for transfers between devices, per_device(): lax.all_to_all(jnp.broadcast_to(queries[None], (seq_count,) + queries.sha...  7.99 us
    all_to_all x1, waiting for transfers between devices, per_device(): source_sum = lax.all_to_all(partial_sum, 'seq', 0, 0, tiled=True)  7.96 us
    all_to_all x1, waiting for transfers between devices, per_device(): lax.all_to_all(pieces, 'tp', 0, 0, tiled=True).astype(jnp.float32)  7.66 us
    all_to_all x1, starting transfers between devices, per_device(): lax.all_to_all(jnp.broadcast_to(queries[None], (seq_count,) + queries.sha...  7.62 us
  transfers between devices with their start and end apart: 3, of which 3 were waited for; matrix products, arithmetic and copies ran while one was open for 9% of the time, Pallas kernels for 0%

profile of v7, /device:TPU:1, one launch (start us, length us, event | category | flops | bytes accessed | tf_op | source)
XLA Modules:
  0.0 123.8 jit_solution(11307239162711049465)
XLA Ops:
  0.0 0.0 copy-start
  0.0 1.9 %broadcast_in_dim.7 = bf16[16,2,32,384]{3,2,1,0:T(8,128)(2,1)} broadcast(bf16[2,32,384]{2,1,0:T(8,128)(2,1)} %param.10), dimensions={1,2,3} | broadcast | bytes 835584 | tf_op jit(solution)/shard_map/broadcast_in_dim | solution.py:161
  1.9 7.6 %all-to-all-start = ((bf16[16,2,32,384]{3,2,1,0:T(8,128)(2,1)}), bf16[16,2,32,384]{3,2,1,0:T(8,128)(2,1)}, u32[]{:S(2)}, u32[]{:S(2)}) async-start(bf16[16,2,32,384]{3,2,1,0:T(8,128)(2,1)} %broadcast_in_dim.7), calls=%async_computation | async-start | bytes 1572864 | tf_op jit(solution)/shard_map/all_to_all | solution.py:160
  9.6 0.0 copy-start.3
  9.6 0.0 copy-start.7
  9.6 4.0 %copy.26 = bf16[2,1024,2,384]{3,1,2,0:T(8,128)(2,1)} copy(bf16[2,1024,2,384]{3,2,1,0:T(2,128)(2,1)} %param.12) | data formatting | bytes 6291456 | tf_op args[2]
  13.6 0.0 copy-done.3
  13.6 0.7 copy.28
  14.2 0.0 copy-done.7
  14.3 0.6 pad_add_fusion.meta_ref
  14.9 8.0 %all-to-all-done.q_ref = bf16[16,2,32,384]{3,2,1,0:T(8,128)(2,1)} async-done(((bf16[16,2,32,384]{3,2,1,0:T(8,128)(2,1)}), bf16[16,2,32,384]{3,2,1,0:T(8,128)(2,1)}, u32[]{:S(2)}, u32[]{:S(2)}) %all-to-all-start) | async-done | bytes 786464 | tf_op jit(solution)/shard_map/all_to_all | solution.py:160
  22.9 11.5 %shard_map.100 = (bf16[16,2,32,384]{3,2,1,0:T(8,128)(2,1)}, f32[16,2,32,8]{3,2,1,0:T(8,128)}) custom-call(s32[3]{0:T(128)} %pad_add_fusion.meta_ref, bf16[16,2,32,384]{3,2,1,0:T(8,128)(2,1)} %all-to-all-done.q_ref, bf16[2,2,1024,384]{3,2,1,0:T(8,128)(2,1)} %bitcast.36, bf16[2,2,1024,384]{3,2,1,0:T(8,128)(2,1)} %bitcast.37, bf16[2,2,32,384]{3,2,1,0:T(8,128)(2,1)} %bitcast.43, ...), custom_call_target="tpu_custom_call" | custom-call | tf_op jit(solution)/shard_map/pallas_call | solution.py:112
  34.3 1.2 copy.17
  35.6 0.1 reshape.88
  35.7 9.0 %all_to_all.30 = f32[16,1,512]{2,1,0:T(1,128)S(1)} all-to-all(f32[16,1,512]{2,1,0:T(1,128)S(1)} %reshape.88), channel_id=1, replica_groups=mesh['req'=2,'seq'=16,'tp'=8] {'seq'}, dimensions={0} | all-to-all | bytes 65536 | tf_op jit(solution)/shard_map/all_to_all | solution.py:165
  44.7 4.5 %all-to-all-start.1 = ((bf16[16,2,32,384]{3,2,1,0:T(8,128)(2,1)}), bf16[16,2,32,384]{3,2,1,0:T(8,128)(2,1)}, u32[]{:S(2)}, u32[]{:S(2)}) async-start(bf16[16,2,32,384]{3,2,1,0:T(8,128)(2,1)} %get-tuple-element.7), calls=%async_computation.1 | async-start | bytes 1572864 | tf_op jit(solution)/shard_map/all_to_all | solution.py:164
  49.2 0.5 broadcast.58
  49.7 0.7 reduce.2
  50.4 0.1 reshape.89
  50.5 0.0 copy-start.4
  50.5 1.0 copy.18
  51.5 8.0 %all-to-all-done.1 = bf16[16,2,32,384]{3,2,1,0:T(8,128)(2,1)} async-done(((bf16[16,2,32,384]{3,2,1,0:T(8,128)(2,1)}), bf16[16,2,32,384]{3,2,1,0:T(8,128)(2,1)}, u32[]{:S(2)}, u32[]{:S(2)}) %all-to-all-start.1) | async-done | bytes 786464 | tf_op jit(solution)/shard_map/all_to_all | solution.py:164
  59.5 3.3 %shard_map.101 = bf16[64,384]{1,0:T(8,128)(2,1)} custom-call(bf16[16,64,384]{2,1,0:T(8,128)(2,1)} %bitcast.7.sum_ref, f32[16,64,8]{2,1,0:T(8,128)} %bitcast.40, bf16[64,384]{1,0:T(8,128)(2,1)} %bitcast.48), custom_call_target="tpu_custom_call" | custom-call | tf_op jit(solution)/shard_map/pallas_call | solution.py:141
  62.8 0.0 copy-start.2
  62.8 1.0 broadcast_in_dim.8
  63.8 18.9 %all_to_all.31 = bf16[8,64,384]{2,1,0:T(8,128)(2,1)S(1)} all-to-all(bf16[8,64,384]{2,1,0:T(8,128)(2,1)S(1)} %broadcast_in_dim.8), channel_id=1, replica_groups=mesh['req'=2,'seq'=16,'tp'=8] {'tp'}, dimensions={0} | all-to-all | bytes 786432 | tf_op jit(solution)/shard_map/all_to_all | solution.py:174
  82.8 0.1 convert_bitcast_fusion
  82.8 0.1 copy.22
  82.9 0.0 copy-start.1
  82.9 0.2 fusion.1
  83.1 0.7 copy-done.1
  83.8 0.0 copy-done.6
  83.8 0.0 copy-done.4
  83.8 0.0 copy-done.2
  83.8 1.4 %fusion.13 = f32[64,512]{1,0:T(8,128)} fusion(bf16[3072,512]{1,0:T(8,128)(2,1)S(1)} %copy-done.2, f32[64,3072]{1,0:T(8,128)S(1)} %bitcast.38, f32[3072]{0:T(1024)S(1)} %copy-done.4, f32[64]{0:T(128)S(1)} %add_rsqrt_fusion), kind=kOutput, calls=%fused_computation.30 | convolution fusion | flops 201916416 | bytes 4075776 | tf_op jit(solution)/shard_map/dot_general | solution.py:181
  85.1 0.0 copy-done
  85.1 3.5 %convolution_convert_fusion = bf16[64,3072]{1,0:T(8,128)(2,1)S(1)} fusion(bf16[512,3072]{1,0:T(8,128)(2,1)S(1)} %copy-done, bf16[3072,512]{1,0:T(8,128)(2,1)} %param.17, f32[64,512]{1,0:T(8,128)} %fusion.13, f32[64,3072]{1,0:T(8,128)} %bitcast.39, f32[3072]{0:T(1024)S(1)} %copy-done.4, f32[64]{0:T(128)} %copy-done.6), kind=kOutput, calls=%fused_computation.1 | convolution fusion | flops 403636224 | bytes 7614720 | tf_op jit(solution)/shard_map/dot_general | solution.py:184
  88.6 0.8 copy.27
  89.4 3.5 %all-to-all-start.4 = ((bf16[8,64,384]{2,1,0:T(8,128)(2,1)}), bf16[8,64,384]{2,1,0:T(8,128)(2,1)S(1)}, u32[]{:S(2)}, u32[]{:S(2)}) async-start(bf16[8,64,384]{2,1,0:T(8,128)(2,1)} %bitcast.42), calls=%async_computation.4 | async-start | bytes 786432 | tf_op jit(solution)/shard_map/all_to_all | solution.py:187
  92.9 0.0 copy-done.5
  92.9 0.7 fusion.10
  93.6 1.4 %reduce_window_sum.11 = s32[64,32]{1,0:T(8,128)} reduce-window(s32[64,32]{1,0:T(8,128)} %fusion.10, s32[]{:T(128)} %constant.13.clone.1), window={size=64x1 pad=63_0x0_0}, to_apply=%region_0.0 | reduce-window | flops 129024 | bytes 16388 | tf_op jit(solution)/shard_map/jit(cumsum)/reduce_window_sum | solution.py:197
  95.0 0.9 select_reduce_fusion
  96.0 7.7 %all-to-all-done.4 = bf16[8,64,384]{2,1,0:T(8,128)(2,1)S(1)} async-done(((bf16[8,64,384]{2,1,0:T(8,128)(2,1)}), bf16[8,64,384]{2,1,0:T(8,128)(2,1)S(1)}, u32[]{:S(2)}, u32[]{:S(2)}) %all-to-all-start.4) | async-done | bytes 393248 | tf_op jit(solution)/shard_map/all_to_all | solution.py:187
  103.6 0.7 convert_reduce_fusion
  104.3 1.2 scatter_custom_fusion
  105.6 17.6 %all_to_all.32 = bf16[32,4,384]{2,1,0:T(4,128)(2,1)S(1)} all-to-all(bf16[32,4,384]{2,1,0:T(4,128)(2,1)S(1)} %reshape.75), channel_id=1, replica_groups=mesh['req'=2,'seq'=16,'tp'=8] {'req','seq'}, dimensions={0} | all-to-all | bytes 196608 | tf_op jit(solution)/shard_map/all_to_all | solution.py:203
  123.1 0.6 copy.30
  (5 shorter events, 0.0 us)
Async XLA Ops:
  0.0 85.1 %copy-start = (bf16[512,3072]{1,0:T(8,128)(2,1)S(1)}, bf16[512,3072]{1,0:T(8,128)(2,1)}, u32[]{:S(2)}) copy-start(bf16[512,3072]{1,0:T(8,128)(2,1)} %param.18) | copy-start | bytes 9437188
  1.9 20.9 %all-to-all-start = ((bf16[16,2,32,384]{3,2,1,0:T(8,128)(2,1)}), bf16[16,2,32,384]{3,2,1,0:T(8,128)(2,1)}, u32[]{:S(2)}, u32[]{:S(2)}) async-start(bf16[16,2,32,384]{3,2,1,0:T(8,128)(2,1)} %broadcast_in_dim.7), calls=%async_computation | async-start | bytes 1572864 | tf_op jit(solution)/shard_map/all_to_all | solution.py:160
  9.6 4.0 %copy-start.3 = (bf16[2,32,2,384]{3,2,1,0:T(2,128)(2,1)S(1)}, bf16[2,32,2,384]{3,2,1,0:T(2,128)(2,1)}, u32[]{:S(2)}) copy-start(bf16[2,32,2,384]{3,2,1,0:T(2,128)(2,1)} %param.11) | copy-start | bytes 294916
  9.6 4.7 %copy-start.7 = (s32[2]{0:T(128)S(1)}, s32[2]{0:T(128)}, u32[]{:S(2)}) copy-start(s32[2]{0:T(128)} %param.13) | copy-start | bytes 28
  44.7 14.8 %all-to-all-start.1 = ((bf16[16,2,32,384]{3,2,1,0:T(8,128)(2,1)}), bf16[16,2,32,384]{3,2,1,0:T(8,128)(2,1)}, u32[]{:S(2)}, u32[]{:S(2)}) async-start(bf16[16,2,32,384]{3,2,1,0:T(8,128)(2,1)} %get-tuple-element.7), calls=%async_computation.1 | async-start | bytes 1572864 | tf_op jit(solution)/shard_map/all_to_all | solution.py:164
  50.5 33.3 %copy-start.4 = (f32[3072]{0:T(1024)S(1)}, f32[3072]{0:T(1024)}, u32[]{:S(2)}) copy-start(f32[3072]{0:T(1024)} %param.15) | copy-start | bytes 36868
  62.8 20.9 %copy-start.2 = (bf16[3072,512]{1,0:T(8,128)(2,1)S(1)}, bf16[3072,512]{1,0:T(8,128)(2,1)}, u32[]{:S(2)}) copy-start(bf16[3072,512]{1,0:T(8,128)(2,1)} %param.16) | copy-start | bytes 9437188
  82.9 0.9 copy-start.1
  83.1 0.7 copy-start.6
  85.1 7.7 %copy-start.5 = (s32[1,64,1]{1,2,0:T(1,128)S(1)}, s32[1,64,1]{1,2,0:T(1,128)}, u32[]{:S(2)}) copy-start(s32[1,64,1]{1,2,0:T(1,128)} %param.19) | copy-start | bytes 772
  89.4 14.2 %all-to-all-start.4 = ((bf16[8,64,384]{2,1,0:T(8,128)(2,1)}), bf16[8,64,384]{2,1,0:T(8,128)(2,1)S(1)}, u32[]{:S(2)}, u32[]{:S(2)}) async-start(bf16[8,64,384]{2,1,0:T(8,128)(2,1)} %bitcast.42), calls=%async_computation.4 | async-start | bytes 786432 | tf_op jit(solution)/shard_map/all_to_all | solution.py:187

commit v8 on v7

--- a/solution.py
+++ b/solution.py
@@ -119,28 +119,40 @@
     )(meta, all_queries, cache2, cache2, fresh2, fresh2)
 
 
-def combine_kernel(sum_ref, stat_ref, residual_ref, out_ref, *, heads):
+def combine_kernel(sum_ref, stat_ref, residual_ref, out_ref, copies_ref, *, heads):
     stats = stat_ref[...]
-    sums = sum_ref[...].astype(jnp.float32)
-    width = sums.shape[-1]
+    width = sum_ref.shape[-1]
     lane = lax.broadcasted_iota(jnp.int32, (1, width), 1)
-    attention = jnp.zeros(sums.shape[1:], jnp.float32)
+    tiles = [jnp.zeros((sum_ref.shape[1], LANE), jnp.float32) for _ in range(width // LANE)]
     for h in range(heads):
+        lo = h * HEAD // LANE * LANE
+        hi = -(-(h + 1) * HEAD // LANE) * LANE
         peak = stats[:, :, h:h + 1]
         joint_peak = jnp.max(peak, axis=0)
         scale = jnp.exp(peak - joint_peak[None])
         total = jnp.sum(stats[:, :, heads + h:heads + h + 1] * scale, axis=0)
-        head_sum = jnp.sum(sums * scale, axis=0)
-        head_lanes = (lane >= h * HEAD) & (lane < (h + 1) * HEAD)
-        attention = jnp.where(head_lanes, head_sum / total, attention)
-    out_ref[...] = (residual_ref[...].astype(jnp.float32) + attention).astype(out_ref.dtype)
-
-
-def combine(source_sum, source_stats, residual_rows):
+        head_sum = jnp.sum(sum_ref[:, :, lo:hi].astype(jnp.float32) * scale, axis=0)
+        value = head_sum / total
+        for j in range(lo // LANE, hi // LANE):
+            head_lanes = (lane[:, j * LANE:(j + 1) * LANE] >= h * HEAD) & (
+                lane[:, j * LANE:(j + 1) * LANE] < (h + 1) * HEAD
+            )
+            tiles[j] = jnp.where(head_lanes, value[:, j * LANE - lo:(j + 1) * LANE - lo], tiles[j])
+    attention = jnp.concatenate(tiles, axis=1)
+    rows = (residual_ref[...].astype(jnp.float32) + attention).astype(out_ref.dtype)
+    out_ref[...] = rows
+    for k in range(copies_ref.shape[0]):
+        copies_ref[k] = rows
+
+
+def combine(source_sum, source_stats, residual_rows, copies):
     heads = source_stats.shape[-1] // 2
     return pl.pallas_call(
         functools.partial(combine_kernel, heads=heads),
-        out_shape=jax.ShapeDtypeStruct(residual_rows.shape, jnp.bfloat16),
+        out_shape=[
+            jax.ShapeDtypeStruct(residual_rows.shape, jnp.bfloat16),
+            jax.ShapeDtypeStruct((copies,) + residual_rows.shape, jnp.bfloat16),
+        ],
     )(source_sum, source_stats, residual_rows)
 
 
@@ -164,15 +176,16 @@
     source_sum = lax.all_to_all(partial_sum, "seq", 0, 0, tiled=True)
     source_stats = lax.all_to_all(partial_stats, "seq", 0, 0, tiled=True)
     row_count = slot_count * token_count
-    block_rows = combine(
+    tp_count = lax.axis_size("tp")
+    block_rows, row_copies = combine(
         source_sum.reshape(seq_count, row_count, width_local),
         source_stats.reshape(seq_count, row_count, 2 * head_count),
         residual_in.reshape(row_count, width_local),
-    )
-    tp_count = lax.axis_size("tp")
+        tp_count,
+    )
     full_rows = (
         lax.all_to_all(
-            jnp.broadcast_to(block_rows[None], (tp_count,) + block_rows.shape), "tp", 0, 0, tiled=True
+            row_copies, "tp", 0, 0, tiled=True
         )
         .transpose(1, 0, 2)
         .reshape(row_count, tp_count * width_local)

time: 124 us -> 125 us (level)
  waiting for transfers between devices: 23.6 us -> 24.9 us
    all_to_all x1, waiting for transfers between devices: 7.96 us -> 9.28 us  [per_device(): source_sum = lax.all_to_all(partial_sum, 'seq', 0, 0, tiled=True)]
where the time goes in v8:
time: 125 us; the launch traced here: 124 us
  blocking collectives  44.8 us (36%)
  waiting for transfers between devices  24.9 us (20%)
  starting transfers between devices  15.5 us (12%)
  Pallas kernels  15.4 us (12%)
  local copies, waits for them, and re-layouts  11.8 us (9%)
  other arithmetic  6.55 us (5%)
  matrix products  4.84 us (4%)
    all_to_all x1, blocking collectives, per_device(): lax.all_to_all(row_copies, 'tp', 0, 0, tiled=True).transpose(1, 0, 2)  19.1 us
    all_to_all x1, blocking collectives, per_device(): lax.all_to_all(outgoing.reshape(owner_count, slot_cap, width_local), ('re...  16.6 us
    pallas_call x1, Pallas kernels, local_attention(): pl.pallas_call(kernel, grid_spec=grid_spec, out_shape=[jax.ShapeDtypeStru...  11.9 us
    all_to_all x1, waiting for transfers between devices, per_device(): source_sum = lax.all_to_all(partial_sum, 'seq', 0, 0, tiled=True)  9.28 us
    all_to_all x1, blocking collectives, per_device(): source_stats = lax.all_to_all(partial_stats, 'seq', 0, 0, tiled=True)  9 us
    all_to_all x1, waiting for transfers between devices, per_device(): lax.all_to_all(jnp.broadcast_to(queries[None], (seq_count,) + queries.sha...  7.99 us
    all_to_all x1, waiting for transfers between devices, per_device(): lax.all_to_all(pieces, 'tp', 0, 0, tiled=True).astype(jnp.float32)  7.67 us
    all_to_all x1, starting transfers between devices, per_device(): lax.all_to_all(jnp.broadcast_to(queries[None], (seq_count,) + queries.sha...  7.62 us
  transfers between devices with their start and end apart: 3, of which 3 were waited for; matrix products, arithmetic and copies ran while one was open for 9% of the time, Pallas kernels for 0%

profile of v8, /device:TPU:1, one launch (start us, length us, event | category | flops | bytes accessed | tf_op | source)
XLA Modules:
  0.0 123.9 jit_solution(5659078419134303170)
XLA Ops:
  0.0 0.0 copy-start
  0.0 1.9 %broadcast_in_dim.5 = bf16[16,2,32,384]{3,2,1,0:T(8,128)(2,1)} broadcast(bf16[2,32,384]{2,1,0:T(8,128)(2,1)} %param.10), dimensions={1,2,3} | broadcast | bytes 835584 | tf_op jit(solution)/shard_map/broadcast_in_dim | solution.py:173
  1.9 7.6 %all-to-all-start = ((bf16[16,2,32,384]{3,2,1,0:T(8,128)(2,1)}), bf16[16,2,32,384]{3,2,1,0:T(8,128)(2,1)}, u32[]{:S(2)}, u32[]{:S(2)}) async-start(bf16[16,2,32,384]{3,2,1,0:T(8,128)(2,1)} %broadcast_in_dim.5), calls=%async_computation | async-start | bytes 1572864 | tf_op jit(solution)/shard_map/all_to_all | solution.py:172
  9.6 0.0 copy-start.3
  9.6 0.0 copy-start.7
  9.6 4.0 %copy.27 = bf16[2,1024,2,384]{3,1,2,0:T(8,128)(2,1)} copy(bf16[2,1024,2,384]{3,2,1,0:T(2,128)(2,1)} %param.12) | data formatting | bytes 6291456 | tf_op args[2]
  13.6 0.0 copy-done.3
  13.6 0.7 copy.29
  14.2 0.0 copy-done.7
  14.3 0.6 pad_add_fusion.meta_ref
  14.9 8.0 %all-to-all-done.q_ref = bf16[16,2,32,384]{3,2,1,0:T(8,128)(2,1)} async-done(((bf16[16,2,32,384]{3,2,1,0:T(8,128)(2,1)}), bf16[16,2,32,384]{3,2,1,0:T(8,128)(2,1)}, u32[]{:S(2)}, u32[]{:S(2)}) %all-to-all-start) | async-done | bytes 786464 | tf_op jit(solution)/shard_map/all_to_all | solution.py:172
  22.9 11.9 %shard_map.100 = (bf16[16,2,32,384]{3,2,1,0:T(8,128)(2,1)}, f32[16,2,32,8]{3,2,1,0:T(8,128)}) custom-call(s32[3]{0:T(128)} %pad_add_fusion.meta_ref, bf16[16,2,32,384]{3,2,1,0:T(8,128)(2,1)} %all-to-all-done.q_ref, bf16[2,2,1024,384]{3,2,1,0:T(8,128)(2,1)} %bitcast.36, bf16[2,2,1024,384]{3,2,1,0:T(8,128)(2,1)} %bitcast.37, bf16[2,2,32,384]{3,2,1,0:T(8,128)(2,1)} %bitcast.43, ...), custom_call_target="tpu_custom_call" | custom-call | tf_op jit(solution)/shard_map/pallas_call | solution.py:112
  34.7 1.2 copy.18
  36.0 0.1 reshape.87
  36.1 9.0 %all_to_all.30 = f32[16,1,512]{2,1,0:T(1,128)S(1)} all-to-all(f32[16,1,512]{2,1,0:T(1,128)S(1)} %reshape.87), channel_id=1, replica_groups=mesh['req'=2,'seq'=16,'tp'=8] {'seq'}, dimensions={0} | all-to-all | bytes 65536 | tf_op jit(solution)/shard_map/all_to_all | solution.py:177
  45.1 4.5 %all-to-all-start.1 = ((bf16[16,2,32,384]{3,2,1,0:T(8,128)(2,1)}), bf16[16,2,32,384]{3,2,1,0:T(8,128)(2,1)}, u32[]{:S(2)}, u32[]{:S(2)}) async-start(bf16[16,2,32,384]{3,2,1,0:T(8,128)(2,1)} %get-tuple-element.9), calls=%async_computation.1 | async-start | bytes 1572864 | tf_op jit(solution)/shard_map/all_to_all | solution.py:176
  49.6 0.0 copy-start.4
  49.6 0.5 broadcast.57
  50.1 0.7 reduce.2
  50.8 0.1 reshape.88
  50.9 1.0 copy.19
  51.9 9.3 %all-to-all-done.1 = bf16[16,2,32,384]{3,2,1,0:T(8,128)(2,1)} async-done(((bf16[16,2,32,384]{3,2,1,0:T(8,128)(2,1)}), bf16[16,2,32,384]{3,2,1,0:T(8,128)(2,1)}, u32[]{:S(2)}, u32[]{:S(2)}) %all-to-all-start.1) | async-done | bytes 786464 | tf_op jit(solution)/shard_map/all_to_all | solution.py:176
  61.2 3.5 %shard_map.101 = (bf16[64,384]{1,0:T(8,128)(2,1)}, bf16[8,64,384]{2,1,0:T(8,128)(2,1)}) custom-call(bf16[16,64,384]{2,1,0:T(8,128)(2,1)} %bitcast.7.sum_ref, f32[16,64,8]{2,1,0:T(8,128)} %bitcast.40, bf16[64,384]{1,0:T(8,128)(2,1)} %bitcast.48), custom_call_target="tpu_custom_call" | custom-call | tf_op jit(solution)/shard_map/pallas_call | solution.py:150
  64.7 0.0 copy-start.2
  64.7 19.1 %all_to_all.31 = bf16[8,64,384]{2,1,0:T(8,128)(2,1)S(1)} all-to-all(bf16[8,64,384]{2,1,0:T(8,128)(2,1)} %get-tuple-element.12), channel_id=1, replica_groups=mesh['req'=2,'seq'=16,'tp'=8] {'tp'}, dimensions={0} | all-to-all | bytes 786432 | tf_op jit(solution)/shard_map/all_to_all | solution.py:187
  83.8 0.1 convert_bitcast_fusion
  83.9 0.1 copy.23
  84.0 0.0 copy-start.1
  84.0 0.2 fusion.1
  84.2 0.0 copy-start.6
  84.2 0.7 copy-done.1
  84.8 0.0 copy-done.6
  84.8 0.0 copy-done.4
  84.8 0.0 copy-done.2
  84.9 1.4 %fusion.13 = f32[64,512]{1,0:T(8,128)} fusion(bf16[3072,512]{1,0:T(8,128)(2,1)S(1)} %copy-done.2, f32[64,3072]{1,0:T(8,128)S(1)} %bitcast.38, f32[3072]{0:T(1024)S(1)} %copy-done.4, f32[64]{0:T(128)S(1)} %add_rsqrt_fusion), kind=kOutput, calls=%fused_computation.30 | convolution fusion | flops 201916416 | bytes 4075776 | tf_op jit(solution)/shard_map/dot_general | solution.py:194
  86.2 0.0 copy-done
  86.2 3.5 %convolution_convert_fusion = bf16[64,3072]{1,0:T(8,128)(2,1)S(1)} fusion(bf16[512,3072]{1,0:T(8,128)(2,1)S(1)} %copy-done, bf16[3072,512]{1,0:T(8,128)(2,1)} %param.17, f32[64,512]{1,0:T(8,128)} %fusion.13, f32[64,3072]{1,0:T(8,128)} %bitcast.39, f32[3072]{0:T(1024)S(1)} %copy-done.4, f32[64]{0:T(128)} %copy-done.6), kind=kOutput, calls=%fused_computation.1 | convolution fusion | flops 403636224 | bytes 7614720 | tf_op jit(solution)/shard_map/dot_general | solution.py:197
  89.7 0.8 copy.28
  90.5 3.5 %all-to-all-start.4 = ((bf16[8,64,384]{2,1,0:T(8,128)(2,1)}), bf16[8,64,384]{2,1,0:T(8,128)(2,1)S(1)}, u32[]{:S(2)}, u32[]{:S(2)}) async-start(bf16[8,64,384]{2,1,0:T(8,128)(2,1)} %bitcast.42), calls=%async_computation.4 | async-start | bytes 786432 | tf_op jit(solution)/shard_map/all_to_all | solution.py:200
  94.0 0.0 copy-done.5
  94.0 0.7 fusion.10
  94.7 1.4 %reduce_window_sum.11 = s32[64,32]{1,0:T(8,128)} reduce-window(s32[64,32]{1,0:T(8,128)} %fusion.10, s32[]{:T(128)} %constant.13.clone.1), window={size=64x1 pad=63_0x0_0}, to_apply=%region_0.0 | reduce-window | flops 129024 | bytes 16388 | tf_op jit(solution)/shard_map/jit(cumsum)/reduce_window_sum | solution.py:210
  96.1 0.9 select_reduce_fusion
  97.0 7.7 %all-to-all-done.4 = bf16[8,64,384]{2,1,0:T(8,128)(2,1)S(1)} async-done(((bf16[8,64,384]{2,1,0:T(8,128)(2,1)}), bf16[8,64,384]{2,1,0:T(8,128)(2,1)S(1)}, u32[]{:S(2)}, u32[]{:S(2)}) %all-to-all-start.4) | async-done | bytes 393248 | tf_op jit(solution)/shard_map/all_to_all | solution.py:200
  104.7 0.7 convert_reduce_fusion
  105.4 1.2 scatter_custom_fusion
  106.7 16.6 %all_to_all.32 = bf16[32,4,384]{2,1,0:T(4,128)(2,1)S(1)} all-to-all(bf16[32,4,384]{2,1,0:T(4,128)(2,1)S(1)} %reshape.74), channel_id=1, replica_groups=mesh['req'=2,'seq'=16,'tp'=8] {'req','seq'}, dimensions={0} | all-to-all | bytes 196608 | tf_op jit(solution)/shard_map/all_to_all | solution.py:216
  123.3 0.6 copy.31
  (4 shorter events, 0.0 us)
Async XLA Ops:
  0.0 86.2 %copy-start = (bf16[512,3072]{1,0:T(8,128)(2,1)S(1)}, bf16[512,3072]{1,0:T(8,128)(2,1)}, u32[]{:S(2)}) copy-start(bf16[512,3072]{1,0:T(8,128)(2,1)} %param.18) | copy-start | bytes 9437188
  1.9 20.9 %all-to-all-start = ((bf16[16,2,32,384]{3,2,1,0:T(8,128)(2,1)}), bf16[16,2,32,384]{3,2,1,0:T(8,128)(2,1)}, u32[]{:S(2)}, u32[]{:S(2)}) async-start(bf16[16,2,32,384]{3,2,1,0:T(8,128)(2,1)} %broadcast_in_dim.5), calls=%async_computation | async-start | bytes 1572864 | tf_op jit(solution)/shard_map/all_to_all | solution.py:172
  9.6 4.0 %copy-start.3 = (bf16[2,32,2,384]{3,2,1,0:T(2,128)(2,1)S(1)}, bf16[2,32,2,384]{3,2,1,0:T(2,128)(2,1)}, u32[]{:S(2)}) copy-start(bf16[2,32,2,384]{3,2,1,0:T(2,128)(2,1)} %param.11) | copy-start | bytes 294916
  9.6 4.7 %copy-start.7 = (s32[2]{0:T(128)S(1)}, s32[2]{0:T(128)}, u32[]{:S(2)}) copy-start(s32[2]{0:T(128)} %param.13) | copy-start | bytes 28
  45.1 16.1 %all-to-all-start.1 = ((bf16[16,2,32,384]{3,2,1,0:T(8,128)(2,1)}), bf16[16,2,32,384]{3,2,1,0:T(8,128)(2,1)}, u32[]{:S(2)}, u32[]{:S(2)}) async-start(bf16[16,2,32,384]{3,2,1,0:T(8,128)(2,1)} %get-tuple-element.9), calls=%async_computation.1 | async-start | bytes 1572864 | tf_op jit(solution)/shard_map/all_to_all | solution.py:176
  49.6 35.3 %copy-start.4 = (f32[3072]{0:T(1024)S(1)}, f32[3072]{0:T(1024)}, u32[]{:S(2)}) copy-start(f32[3072]{0:T(1024)} %param.15) | copy-start | bytes 36868
  64.7 20.1 %copy-start.2 = (bf16[3072,512]{1,0:T(8,128)(2,1)S(1)}, bf16[3072,512]{1,0:T(8,128)(2,1)}, u32[]{:S(2)}) copy-start(bf16[3072,512]{1,0:T(8,128)(2,1)} %param.16) | copy-start | bytes 9437188
  84.0 0.9 copy-start.1
  84.2 0.7 copy-start.6
  86.2 7.7 %copy-start.5 = (s32[1,64,1]{1,2,0:T(1,128)S(1)}, s32[1,64,1]{1,2,0:T(1,128)}, u32[]{:S(2)}) copy-start(s32[1,64,1]{1,2,0:T(1,128)} %param.19) | copy-start | bytes 772
  90.5 14.2 %all-to-all-start.4 = ((bf16[8,64,384]{2,1,0:T(8,128)(2,1)}), bf16[8,64,384]{2,1,0:T(8,128)(2,1)S(1)}, u32[]{:S(2)}, u32[]{:S(2)}) async-start(bf16[8,64,384]{2,1,0:T(8,128)(2,1)} %bitcast.42), calls=%async_computation.4 | async-start | bytes 786432 | tf_op jit(solution)/shard_map/all_to_all | solution.py:200

commit v9 on v8

--- a/solution.py
+++ b/solution.py
@@ -11,6 +11,7 @@
 
 masked_floor = -1e30
 LANE = 128
+KEY_BLOCK = 256
 
 
 def attention_kernel(meta_ref, q_ref, kc_ref, vc_ref, kf_ref, vf_ref, sum_ref, stat_ref, *, tq, heads):
@@ -33,12 +34,13 @@
     cached_visible = (offset + lax.broadcasted_iota(jnp.int32, (1, span), 1)) < length
     contract = (((1,), (1,)), ((), ()))
 
-    def run(with_cache, masked=True):
+    def run(with_cache, masked=True, keys=span):
         kf = kf_ref[...]
         vf = vf_ref[...]
         if with_cache:
-            kc = kc_ref[...]
-            vc = vc_ref[...]
+            kc = kc_ref[:keys, :]
+            vc = vc_ref[:keys, :]
+            visible = cached_visible[:, :keys]
         tiles = [jnp.zeros((tq, LANE), jnp.float32) for _ in range(width // LANE)]
         stats = jnp.zeros((tq, 2 * heads), jnp.float32)
         for h in range(heads):
@@ -52,7 +54,7 @@
             if with_cache:
                 sc = lax.dot_general(qh, kc[:, lo:hi], contract, preferred_element_type=jnp.float32)
                 if masked:
-                    sc = jnp.where(cached_visible, sc, masked_floor)
+                    sc = jnp.where(visible, sc, masked_floor)
                 peak = jnp.maximum(peak, jnp.max(sc, axis=-1, keepdims=True))
             pf = jnp.where(fresh_visible, jnp.exp((sf - peak) * scale), 0.0)
             total = jnp.sum(pf, axis=-1, keepdims=True)
@@ -70,9 +72,14 @@
         sum_ref[...] = weighted.reshape(sum_ref.shape).astype(sum_ref.dtype)
         stat_ref[...] = stats.reshape(stat_ref.shape)
 
-    @pl.when((offset < length) & (offset + span > length))
-    def _():
-        run(True)
+    partial = (offset < length) & (offset + span > length)
+    key_blocks = span // KEY_BLOCK
+    used_blocks = (length - offset + KEY_BLOCK - 1) // KEY_BLOCK
+    for used in range(1, key_blocks + 1):
+
+        @pl.when(partial & (used_blocks == used))
+        def _():
+            run(True, keys=used * KEY_BLOCK)
 
     @pl.when(offset + span <= length)
     def _():

time: 125 us -> 123 us (0.984)
  blocking collectives: 44.8 us -> 48.4 us
  Pallas kernels: 15.4 us -> 12.2 us
  waiting for transfers between devices: 24.9 us -> 23.6 us
    all_to_all x1, blocking collectives: 16.6 us -> 20.3 us  [per_device(): lax.all_to_all(outgoing.reshape(owner_count, slot_cap, width_local), ('re...]
    pallas_call x1, Pallas kernels: 11.9 us -> 8.73 us  [local_attention(): pl.pallas_call(kernel, grid_spec=grid_spec, out_shape=[jax.ShapeDtypeStru...]
where the time goes in v9:
time: 123 us
  blocking collectives  48.4 us (39%)
  waiting for transfers between devices  23.6 us (19%)
  starting transfers between devices  15.4 us (13%)
  Pallas kernels  12.2 us (10%)
  local copies, waits for them, and re-layouts  11.8 us (10%)
  other arithmetic  6.55 us (5%)
  matrix products  4.85 us (4%)
    all_to_all x1, blocking collectives, per_device(): lax.all_to_all(outgoing.reshape(owner_count, slot_cap, width_local), ('re...  20.3 us
    all_to_all x1, blocking collectives, per_device(): lax.all_to_all(row_copies, 'tp', 0, 0, tiled=True).transpose(1, 0, 2)  19.2 us
    all_to_all x1, blocking collectives, per_device(): source_stats = lax.all_to_all(partial_stats, 'seq', 0, 0, tiled=True)  9 us
    pallas_call x1, Pallas kernels, local_attention(): pl.pallas_call(kernel, grid_spec=grid_spec, out_shape=[jax.ShapeDtypeStru...  8.73 us
    all_to_all x1, waiting for transfers between devices, per_device(): source_sum = lax.all_to_all(partial_sum, 'seq', 0, 0, tiled=True)  8.08 us
    all_to_all x1, waiting for transfers between devices, per_device(): lax.all_to_all(jnp.broadcast_to(queries[None], (seq_count,) + queries.sha...  7.99 us
    all_to_all x1, starting transfers between devices, per_device(): lax.all_to_all(jnp.broadcast_to(queries[None], (seq_count,) + queries.sha...  7.62 us
    all_to_all x1, waiting for transfers between devices, per_device(): lax.all_to_all(pieces, 'tp', 0, 0, tiled=True).astype(jnp.float32)  7.56 us
  transfers between devices with their start and end apart: 3, of which 3 were waited for; matrix products, arithmetic and copies ran while one was open for 9% of the time, Pallas kernels for 0%

profile of v9, /device:TPU:1, one launch (start us, length us, event | category | flops | bytes accessed | tf_op | source)
XLA Modules:
  0.0 123.0 jit_solution(10033125325259302552)
XLA Ops:
  0.0 0.0 copy-start
  0.0 1.9 %broadcast_in_dim.5 = bf16[16,2,32,384]{3,2,1,0:T(8,128)(2,1)} broadcast(bf16[2,32,384]{2,1,0:T(8,128)(2,1)} %param.10), dimensions={1,2,3} | broadcast | bytes 835584 | tf_op jit(solution)/shard_map/broadcast_in_dim | solution.py:180
  1.9 7.6 %all-to-all-start = ((bf16[16,2,32,384]{3,2,1,0:T(8,128)(2,1)}), bf16[16,2,32,384]{3,2,1,0:T(8,128)(2,1)}, u32[]{:S(2)}, u32[]{:S(2)}) async-start(bf16[16,2,32,384]{3,2,1,0:T(8,128)(2,1)} %broadcast_in_dim.5), calls=%async_computation | async-start | bytes 1572864 | tf_op jit(solution)/shard_map/all_to_all | solution.py:179
  9.6 0.0 copy-start.3
  9.6 0.0 copy-start.7
  9.6 4.0 %copy.27 = bf16[2,1024,2,384]{3,1,2,0:T(8,128)(2,1)} copy(bf16[2,1024,2,384]{3,2,1,0:T(2,128)(2,1)} %param.12) | data formatting | bytes 6291456 | tf_op args[2]
  13.6 0.0 copy-done.3
  13.6 0.7 copy.29
  14.2 0.0 copy-done.7
  14.3 0.6 pad_add_fusion.meta_ref
  14.9 8.0 %all-to-all-done.q_ref = bf16[16,2,32,384]{3,2,1,0:T(8,128)(2,1)} async-done(((bf16[16,2,32,384]{3,2,1,0:T(8,128)(2,1)}), bf16[16,2,32,384]{3,2,1,0:T(8,128)(2,1)}, u32[]{:S(2)}, u32[]{:S(2)}) %all-to-all-start) | async-done | bytes 786464 | tf_op jit(solution)/shard_map/all_to_all | solution.py:179
  22.9 8.7 %shard_map.100 = (bf16[16,2,32,384]{3,2,1,0:T(8,128)(2,1)}, f32[16,2,32,8]{3,2,1,0:T(8,128)}) custom-call(s32[3]{0:T(128)} %pad_add_fusion.meta_ref, bf16[16,2,32,384]{3,2,1,0:T(8,128)(2,1)} %all-to-all-done.q_ref, bf16[2,2,1024,384]{3,2,1,0:T(8,128)(2,1)} %bitcast.36, bf16[2,2,1024,384]{3,2,1,0:T(8,128)(2,1)} %bitcast.37, bf16[2,2,32,384]{3,2,1,0:T(8,128)(2,1)} %bitcast.43, ...), custom_call_target="tpu_custom_call" | custom-call | tf_op jit(solution)/shard_map/pallas_call | solution.py:119
  31.6 1.2 copy.18
  32.8 0.1 reshape.87
  32.9 9.0 %all_to_all.30 = f32[16,1,512]{2,1,0:T(1,128)S(1)} all-to-all(f32[16,1,512]{2,1,0:T(1,128)S(1)} %reshape.87), channel_id=1, replica_groups=mesh['req'=2,'seq'=16,'tp'=8] {'seq'}, dimensions={0} | all-to-all | bytes 65536 | tf_op jit(solution)/shard_map/all_to_all | solution.py:184
  41.9 4.3 %all-to-all-start.1 = ((bf16[16,2,32,384]{3,2,1,0:T(8,128)(2,1)}), bf16[16,2,32,384]{3,2,1,0:T(8,128)(2,1)}, u32[]{:S(2)}, u32[]{:S(2)}) async-start(bf16[16,2,32,384]{3,2,1,0:T(8,128)(2,1)} %get-tuple-element.9), calls=%async_computation.1 | async-start | bytes 1572864 | tf_op jit(solution)/shard_map/all_to_all | solution.py:183
  46.2 0.0 copy-start.4
  46.3 0.5 broadcast.57
  46.8 0.7 reduce.2
  47.5 0.1 reshape.88
  47.6 1.0 copy.19
  48.6 8.1 %all-to-all-done.1 = bf16[16,2,32,384]{3,2,1,0:T(8,128)(2,1)} async-done(((bf16[16,2,32,384]{3,2,1,0:T(8,128)(2,1)}), bf16[16,2,32,384]{3,2,1,0:T(8,128)(2,1)}, u32[]{:S(2)}, u32[]{:S(2)}) %all-to-all-start.1) | async-done | bytes 786464 | tf_op jit(solution)/shard_map/all_to_all | solution.py:183
  56.7 3.5 %shard_map.101 = (bf16[64,384]{1,0:T(8,128)(2,1)}, bf16[8,64,384]{2,1,0:T(8,128)(2,1)}) custom-call(bf16[16,64,384]{2,1,0:T(8,128)(2,1)} %bitcast.7.sum_ref, f32[16,64,8]{2,1,0:T(8,128)} %bitcast.40, bf16[64,384]{1,0:T(8,128)(2,1)} %bitcast.48), custom_call_target="tpu_custom_call" | custom-call | tf_op jit(solution)/shard_map/pallas_call | solution.py:157
  60.2 0.0 copy-start.2
  60.2 19.2 %all_to_all.31 = bf16[8,64,384]{2,1,0:T(8,128)(2,1)S(1)} all-to-all(bf16[8,64,384]{2,1,0:T(8,128)(2,1)} %get-tuple-element.12), channel_id=1, replica_groups=mesh['req'=2,'seq'=16,'tp'=8] {'tp'}, dimensions={0} | all-to-all | bytes 786432 | tf_op jit(solution)/shard_map/all_to_all | solution.py:194
  79.4 0.1 convert_bitcast_fusion
  79.4 0.1 copy.23
  79.5 0.0 copy-start.1
  79.5 0.2 fusion.1
  79.7 0.0 copy-start.6
  79.7 0.7 copy-done.1
  80.4 0.0 copy-done.6
  80.4 0.0 copy-done.4
  80.4 0.0 copy-done.2
  80.4 1.4 %fusion.13 = f32[64,512]{1,0:T(8,128)} fusion(bf16[3072,512]{1,0:T(8,128)(2,1)S(1)} %copy-done.2, f32[64,3072]{1,0:T(8,128)S(1)} %bitcast.38, f32[3072]{0:T(1024)S(1)} %copy-done.4, f32[64]{0:T(128)S(1)} %add_rsqrt_fusion), kind=kOutput, calls=%fused_computation.30 | convolution fusion | flops 201916416 | bytes 4075776 | tf_op jit(solution)/shard_map/dot_general | solution.py:201
  81.7 0.0 copy-done
  81.7 3.5 %convolution_convert_fusion = bf16[64,3072]{1,0:T(8,128)(2,1)S(1)} fusion(bf16[512,3072]{1,0:T(8,128)(2,1)S(1)} %copy-done, bf16[3072,512]{1,0:T(8,128)(2,1)} %param.17, f32[64,512]{1,0:T(8,128)} %fusion.13, f32[64,3072]{1,0:T(8,128)} %bitcast.39, f32[3072]{0:T(1024)S(1)} %copy-done.4, f32[64]{0:T(128)} %copy-done.6), kind=kOutput, calls=%fused_computation.1 | convolution fusion | flops 403636224 | bytes 7614720 | tf_op jit(solution)/shard_map/dot_general | solution.py:204
  85.2 0.8 copy.28
  86.0 3.5 %all-to-all-start.4 = ((bf16[8,64,384]{2,1,0:T(8,128)(2,1)}), bf16[8,64,384]{2,1,0:T(8,128)(2,1)S(1)}, u32[]{:S(2)}, u32[]{:S(2)}) async-start(bf16[8,64,384]{2,1,0:T(8,128)(2,1)} %bitcast.42), calls=%async_computation.4 | async-start | bytes 786432 | tf_op jit(solution)/shard_map/all_to_all | solution.py:207
  89.5 0.0 copy-done.5
  89.5 0.7 fusion.10
  90.2 1.4 %reduce_window_sum.11 = s32[64,32]{1,0:T(8,128)} reduce-window(s32[64,32]{1,0:T(8,128)} %fusion.10, s32[]{:T(128)} %constant.13.clone.1), window={size=64x1 pad=63_0x0_0}, to_apply=%region_0.0 | reduce-window | flops 129024 | bytes 16388 | tf_op jit(solution)/shard_map/jit(cumsum)/reduce_window_sum | solution.py:217
  91.6 0.9 select_reduce_fusion
  92.6 7.6 %all-to-all-done.4 = bf16[8,64,384]{2,1,0:T(8,128)(2,1)S(1)} async-done(((bf16[8,64,384]{2,1,0:T(8,128)(2,1)}), bf16[8,64,384]{2,1,0:T(8,128)(2,1)S(1)}, u32[]{:S(2)}, u32[]{:S(2)}) %all-to-all-start.4) | async-done | bytes 393248 | tf_op jit(solution)/shard_map/all_to_all | solution.py:207
  100.1 0.7 convert_reduce_fusion
  100.8 1.2 scatter_custom_fusion
  102.1 20.3 %all_to_all.32 = bf16[32,4,384]{2,1,0:T(4,128)(2,1)S(1)} all-to-all(bf16[32,4,384]{2,1,0:T(4,128)(2,1)S(1)} %reshape.74), channel_id=1, replica_groups=mesh['req'=2,'seq'=16,'tp'=8] {'req','seq'}, dimensions={0} | all-to-all | bytes 196608 | tf_op jit(solution)/shard_map/all_to_all | solution.py:223
  122.4 0.6 copy.31
  (4 shorter events, 0.0 us)
Async XLA Ops:
  0.0 81.7 %copy-start = (bf16[512,3072]{1,0:T(8,128)(2,1)S(1)}, bf16[512,3072]{1,0:T(8,128)(2,1)}, u32[]{:S(2)}) copy-start(bf16[512,3072]{1,0:T(8,128)(2,1)} %param.18) | copy-start | bytes 9437188
  1.9 20.9 %all-to-all-start = ((bf16[16,2,32,384]{3,2,1,0:T(8,128)(2,1)}), bf16[16,2,32,384]{3,2,1,0:T(8,128)(2,1)}, u32[]{:S(2)}, u32[]{:S(2)}) async-start(bf16[16,2,32,384]{3,2,1,0:T(8,128)(2,1)} %broadcast_in_dim.5), calls=%async_computation | async-start | bytes 1572864 | tf_op jit(solution)/shard_map/all_to_all | solution.py:179
  9.6 4.0 %copy-start.3 = (bf16[2,32,2,384]{3,2,1,0:T(2,128)(2,1)S(1)}, bf16[2,32,2,384]{3,2,1,0:T(2,128)(2,1)}, u32[]{:S(2)}) copy-start(bf16[2,32,2,384]{3,2,1,0:T(2,128)(2,1)} %param.11) | copy-start | bytes 294916
  9.6 4.7 %copy-start.7 = (s32[2]{0:T(128)S(1)}, s32[2]{0:T(128)}, u32[]{:S(2)}) copy-start(s32[2]{0:T(128)} %param.13) | copy-start | bytes 28
  41.9 14.8 %all-to-all-start.1 = ((bf16[16,2,32,384]{3,2,1,0:T(8,128)(2,1)}), bf16[16,2,32,384]{3,2,1,0:T(8,128)(2,1)}, u32[]{:S(2)}, u32[]{:S(2)}) async-start(bf16[16,2,32,384]{3,2,1,0:T(8,128)(2,1)} %get-tuple-element.9), calls=%async_computation.1 | async-start | bytes 1572864 | tf_op jit(solution)/shard_map/all_to_all | solution.py:183
  46.2 34.1 %copy-start.4 = (f32[3072]{0:T(1024)S(1)}, f32[3072]{0:T(1024)}, u32[]{:S(2)}) copy-start(f32[3072]{0:T(1024)} %param.15) | copy-start | bytes 36868
  60.2 20.2 %copy-start.2 = (bf16[3072,512]{1,0:T(8,128)(2,1)S(1)}, bf16[3072,512]{1,0:T(8,128)(2,1)}, u32[]{:S(2)}) copy-start(bf16[3072,512]{1,0:T(8,128)(2,1)} %param.16) | copy-start | bytes 9437188
  79.5 0.9 copy-start.1
  79.7 0.7 copy-start.6
  81.7 7.7 %copy-start.5 = (s32[1,64,1]{1,2,0:T(1,128)S(1)}, s32[1,64,1]{1,2,0:T(1,128)}, u32[]{:S(2)}) copy-start(s32[1,64,1]{1,2,0:T(1,128)} %param.19) | copy-start | bytes 772
  86.0 14.1 %all-to-all-start.4 = ((bf16[8,64,384]{2,1,0:T(8,128)(2,1)}), bf16[8,64,384]{2,1,0:T(8,128)(2,1)S(1)}, u32[]{:S(2)}, u32[]{:S(2)}) async-start(bf16[8,64,384]{2,1,0:T(8,128)(2,1)} %bitcast.42), calls=%async_computation.4 | async-start | bytes 786432 | tf_op jit(solution)/shard_map/all_to_all | solution.py:207

commit v10 on v9

--- a/solution.py
+++ b/solution.py
@@ -154,8 +154,20 @@
 
 def combine(source_sum, source_stats, residual_rows, copies):
     heads = source_stats.shape[-1] // 2
+    source_count, row_count, width = source_sum.shape
+    rows = 16 if row_count % 16 == 0 else row_count
     return pl.pallas_call(
         functools.partial(combine_kernel, heads=heads),
+        grid=(row_count // rows,),
+        in_specs=[
+            pl.BlockSpec((source_count, rows, width), lambda i: (0, i, 0)),
+            pl.BlockSpec((source_count, rows, 2 * heads), lambda i: (0, i, 0)),
+            pl.BlockSpec((rows, width), lambda i: (i, 0)),
+        ],
+        out_specs=[
+            pl.BlockSpec((rows, width), lambda i: (i, 0)),
+            pl.BlockSpec((copies, rows, width), lambda i: (0, i, 0)),
+        ],
         out_shape=[
             jax.ShapeDtypeStruct(residual_rows.shape, jnp.bfloat16),
             jax.ShapeDtypeStruct((copies,) + residual_rows.shape, jnp.bfloat16),

time: 123 us -> 127 us (1.033)
  waiting for transfers between devices: 23.6 us -> 27.4 us
  Pallas kernels: 12.2 us -> 15.2 us
  blocking collectives: 48.4 us -> 45.9 us
    all_to_all x1, blocking collectives: 20.3 us -> 16.5 us  [per_device(): lax.all_to_all(outgoing.reshape(owner_count, slot_cap, width_local), ('re...]
    all_to_all x1, waiting for transfers between devices: 8.08 us -> 11.1 us  [per_device(): source_sum = lax.all_to_all(partial_sum, 'seq', 0, 0, tiled=True)]
    pallas_call x1, Pallas kernels: 8.73 us -> 10.8 us  [local_attention(): pl.pallas_call(kernel, grid_spec=grid_spec, out_shape=[jax.ShapeDtypeStru...]
  transfers between devices with their start and end apart: 3 -> 3, of which waited for: 3 -> 3; matrix products, arithmetic and copies ran while one was open for 9% -> 8% of each run, Pallas kernels for 0% -> 0%
where the time goes in v10:
time: 127 us; the launch traced here: 128 us
  blocking collectives  45.9 us (36%)
  waiting for transfers between devices  27.4 us (22%)
  starting transfers between devices  15.8 us (12%)
  Pallas kernels  15.2 us (12%)
  local copies, waits for them, and re-layouts  11.8 us (9%)
  other arithmetic  6.55 us (5%)
  matrix products  4.84 us (4%)
    all_to_all x1, blocking collectives, per_device(): lax.all_to_all(row_copies, 'tp', 0, 0, tiled=True).transpose(1, 0, 2)  20.2 us
    all_to_all x1, blocking collectives, per_device(): lax.all_to_all(outgoing.reshape(owner_count, slot_cap, width_local), ('re...  16.5 us
    all_to_all x1, waiting for transfers between devices, per_device(): source_sum = lax.all_to_all(partial_sum, 'seq', 0, 0, tiled=True)  11.1 us
    pallas_call x1, Pallas kernels, local_attention(): pl.pallas_call(kernel, grid_spec=grid_spec, out_shape=[jax.ShapeDtypeStru...  10.8 us
    all_to_all x1, blocking collectives, per_device(): source_stats = lax.all_to_all(partial_stats, 'seq', 0, 0, tiled=True)  9.18 us
    all_to_all x1, waiting for transfers between devices, per_device(): lax.all_to_all(pieces, 'tp', 0, 0, tiled=True).astype(jnp.float32)  8.25 us
    all_to_all x1, waiting for transfers between devices, per_device(): lax.all_to_all(jnp.broadcast_to(queries[None], (seq_count,) + queries.sha...  7.99 us
    all_to_all x1, starting transfers between devices, per_device(): lax.all_to_all(jnp.broadcast_to(queries[None], (seq_count,) + queries.sha...  7.62 us
  transfers between devices with their start and end apart: 3, of which 3 were waited for; matrix products, arithmetic and copies ran while one was open for 8% of the time, Pallas kernels for 0%

profile of v10, /device:TPU:1, one launch (start us, length us, event | category | flops | bytes accessed | tf_op | source)
XLA Modules:
  0.0 127.6 jit_solution(244689384230158557)
XLA Ops:
  0.0 0.0 copy-start
  0.0 1.9 %broadcast_in_dim.5 = bf16[16,2,32,384]{3,2,1,0:T(8,128)(2,1)} broadcast(bf16[2,32,384]{2,1,0:T(8,128)(2,1)} %param.10), dimensions={1,2,3} | broadcast | bytes 835584 | tf_op jit(solution)/shard_map/broadcast_in_dim | solution.py:192
  1.9 7.6 %all-to-all-start = ((bf16[16,2,32,384]{3,2,1,0:T(8,128)(2,1)}), bf16[16,2,32,384]{3,2,1,0:T(8,128)(2,1)}, u32[]{:S(2)}, u32[]{:S(2)}) async-start(bf16[16,2,32,384]{3,2,1,0:T(8,128)(2,1)} %broadcast_in_dim.5), calls=%async_computation | async-start | bytes 1572864 | tf_op jit(solution)/shard_map/all_to_all | solution.py:191
  9.6 0.0 copy-start.3
  9.6 0.0 copy-start.7
  9.6 4.0 %copy.27 = bf16[2,1024,2,384]{3,1,2,0:T(8,128)(2,1)} copy(bf16[2,1024,2,384]{3,2,1,0:T(2,128)(2,1)} %param.12) | data formatting | bytes 6291456 | tf_op args[2]
  13.6 0.0 copy-done.3
  13.6 0.7 copy.29
  14.2 0.0 copy-done.7
  14.3 0.6 pad_add_fusion.meta_ref
  14.9 8.0 %all-to-all-done.q_ref = bf16[16,2,32,384]{3,2,1,0:T(8,128)(2,1)} async-done(((bf16[16,2,32,384]{3,2,1,0:T(8,128)(2,1)}), bf16[16,2,32,384]{3,2,1,0:T(8,128)(2,1)}, u32[]{:S(2)}, u32[]{:S(2)}) %all-to-all-start) | async-done | bytes 786464 | tf_op jit(solution)/shard_map/all_to_all | solution.py:191
  22.9 10.8 %shard_map.100 = (bf16[16,2,32,384]{3,2,1,0:T(8,128)(2,1)}, f32[16,2,32,8]{3,2,1,0:T(8,128)}) custom-call(s32[3]{0:T(128)} %pad_add_fusion.meta_ref, bf16[16,2,32,384]{3,2,1,0:T(8,128)(2,1)} %all-to-all-done.q_ref, bf16[2,2,1024,384]{3,2,1,0:T(8,128)(2,1)} %bitcast.36, bf16[2,2,1024,384]{3,2,1,0:T(8,128)(2,1)} %bitcast.37, bf16[2,2,32,384]{3,2,1,0:T(8,128)(2,1)} %bitcast.43, ...), custom_call_target="tpu_custom_call" | custom-call | tf_op jit(solution)/shard_map/pallas_call | solution.py:119
  33.6 1.2 copy.18
  34.9 0.1 reshape.87
  35.0 9.2 %all_to_all.30 = f32[16,1,512]{2,1,0:T(1,128)S(1)} all-to-all(f32[16,1,512]{2,1,0:T(1,128)S(1)} %reshape.87), channel_id=1, replica_groups=mesh['req'=2,'seq'=16,'tp'=8] {'seq'}, dimensions={0} | all-to-all | bytes 65536 | tf_op jit(solution)/shard_map/all_to_all | solution.py:196
  44.2 4.3 %all-to-all-start.1 = ((bf16[16,2,32,384]{3,2,1,0:T(8,128)(2,1)}), bf16[16,2,32,384]{3,2,1,0:T(8,128)(2,1)}, u32[]{:S(2)}, u32[]{:S(2)}) async-start(bf16[16,2,32,384]{3,2,1,0:T(8,128)(2,1)} %get-tuple-element.9), calls=%async_computation.1 | async-start | bytes 1572864 | tf_op jit(solution)/shard_map/all_to_all | solution.py:195
  48.5 0.0 copy-start.4
  48.5 0.5 broadcast.57
  49.0 0.7 reduce.2
  49.7 0.1 reshape.88
  49.8 1.0 copy.19
  50.8 11.1 %all-to-all-done.1 = bf16[16,2,32,384]{3,2,1,0:T(8,128)(2,1)} async-done(((bf16[16,2,32,384]{3,2,1,0:T(8,128)(2,1)}), bf16[16,2,32,384]{3,2,1,0:T(8,128)(2,1)}, u32[]{:S(2)}, u32[]{:S(2)}) %all-to-all-start.1) | async-done | bytes 786464 | tf_op jit(solution)/shard_map/all_to_all | solution.py:195
  62.0 4.4 %shard_map.101 = (bf16[64,384]{1,0:T(8,128)(2,1)}, bf16[8,64,384]{2,1,0:T(8,128)(2,1)}) custom-call(bf16[16,64,384]{2,1,0:T(8,128)(2,1)} %bitcast.7.sum_ref, f32[16,64,8]{2,1,0:T(8,128)} %bitcast.40, bf16[64,384]{1,0:T(8,128)(2,1)} %bitcast.48), custom_call_target="tpu_custom_call" | custom-call | tf_op jit(solution)/shard_map/pallas_call | solution.py:159
  66.4 0.0 copy-start.2
  66.4 20.2 %all_to_all.31 = bf16[8,64,384]{2,1,0:T(8,128)(2,1)S(1)} all-to-all(bf16[8,64,384]{2,1,0:T(8,128)(2,1)} %get-tuple-element.12), channel_id=1, replica_groups=mesh['req'=2,'seq'=16,'tp'=8] {'tp'}, dimensions={0} | all-to-all | bytes 786432 | tf_op jit(solution)/shard_map/all_to_all | solution.py:206
  86.6 0.1 convert_bitcast_fusion
  86.6 0.1 copy.23
  86.7 0.0 copy-start.1
  86.7 0.2 fusion.1
  86.9 0.0 copy-start.6
  86.9 0.7 copy-done.1
  87.6 0.0 copy-done.6
  87.6 0.0 copy-done.4
  87.6 0.0 copy-done.2
  87.6 1.4 %fusion.13 = f32[64,512]{1,0:T(8,128)} fusion(bf16[3072,512]{1,0:T(8,128)(2,1)S(1)} %copy-done.2, f32[64,3072]{1,0:T(8,128)S(1)} %bitcast.38, f32[3072]{0:T(1024)S(1)} %copy-done.4, f32[64]{0:T(128)S(1)} %add_rsqrt_fusion), kind=kOutput, calls=%fused_computation.30 | convolution fusion | flops 201916416 | bytes 4075776 | tf_op jit(solution)/shard_map/dot_general | solution.py:213
  88.9 0.0 copy-done
  88.9 3.5 %convolution_convert_fusion = bf16[64,3072]{1,0:T(8,128)(2,1)S(1)} fusion(bf16[512,3072]{1,0:T(8,128)(2,1)S(1)} %copy-done, bf16[3072,512]{1,0:T(8,128)(2,1)} %param.17, f32[64,512]{1,0:T(8,128)} %fusion.13, f32[64,3072]{1,0:T(8,128)} %bitcast.39, f32[3072]{0:T(1024)S(1)} %copy-done.4, f32[64]{0:T(128)} %copy-done.6), kind=kOutput, calls=%fused_computation.1 | convolution fusion | flops 403636224 | bytes 7614720 | tf_op jit(solution)/shard_map/dot_general | solution.py:216
  92.4 0.8 copy.28
  93.2 3.9 %all-to-all-start.4 = ((bf16[8,64,384]{2,1,0:T(8,128)(2,1)}), bf16[8,64,384]{2,1,0:T(8,128)(2,1)S(1)}, u32[]{:S(2)}, u32[]{:S(2)}) async-start(bf16[8,64,384]{2,1,0:T(8,128)(2,1)} %bitcast.42), calls=%async_computation.4 | async-start | bytes 786432 | tf_op jit(solution)/shard_map/all_to_all | solution.py:219
  97.1 0.0 copy-done.5
  97.1 0.7 fusion.10
  97.8 1.4 %reduce_window_sum.11 = s32[64,32]{1,0:T(8,128)} reduce-window(s32[64,32]{1,0:T(8,128)} %fusion.10, s32[]{:T(128)} %constant.13.clone.1), window={size=64x1 pad=63_0x0_0}, to_apply=%region_0.0 | reduce-window | flops 129024 | bytes 16388 | tf_op jit(solution)/shard_map/jit(cumsum)/reduce_window_sum | solution.py:229
  99.3 0.9 select_reduce_fusion
  100.2 8.2 %all-to-all-done.4 = bf16[8,64,384]{2,1,0:T(8,128)(2,1)S(1)} async-done(((bf16[8,64,384]{2,1,0:T(8,128)(2,1)}), bf16[8,64,384]{2,1,0:T(8,128)(2,1)S(1)}, u32[]{:S(2)}, u32[]{:S(2)}) %all-to-all-start.4) | async-done | bytes 393248 | tf_op jit(solution)/shard_map/all_to_all | solution.py:219
  108.5 0.7 convert_reduce_fusion
  109.2 1.2 scatter_custom_fusion
  110.4 16.5 %all_to_all.32 = bf16[32,4,384]{2,1,0:T(4,128)(2,1)S(1)} all-to-all(bf16[32,4,384]{2,1,0:T(4,128)(2,1)S(1)} %reshape.74), channel_id=1, replica_groups=mesh['req'=2,'seq'=16,'tp'=8] {'req','seq'}, dimensions={0} | all-to-all | bytes 196608 | tf_op jit(solution)/shard_map/all_to_all | solution.py:235
  126.9 0.6 copy.31
  (4 shorter events, 0.0 us)
Async XLA Ops:
  0.0 88.9 %copy-start = (bf16[512,3072]{1,0:T(8,128)(2,1)S(1)}, bf16[512,3072]{1,0:T(8,128)(2,1)}, u32[]{:S(2)}) copy-start(bf16[512,3072]{1,0:T(8,128)(2,1)} %param.18) | copy-start | bytes 9437188
  1.9 20.9 %all-to-all-start = ((bf16[16,2,32,384]{3,2,1,0:T(8,128)(2,1)}), bf16[16,2,32,384]{3,2,1,0:T(8,128)(2,1)}, u32[]{:S(2)}, u32[]{:S(2)}) async-start(bf16[16,2,32,384]{3,2,1,0:T(8,128)(2,1)} %broadcast_in_dim.5), calls=%async_computation | async-start | bytes 1572864 | tf_op jit(solution)/shard_map/all_to_all | solution.py:191
  9.6 4.0 %copy-start.3 = (bf16[2,32,2,384]{3,2,1,0:T(2,128)(2,1)S(1)}, bf16[2,32,2,384]{3,2,1,0:T(2,128)(2,1)}, u32[]{:S(2)}) copy-start(bf16[2,32,2,384]{3,2,1,0:T(2,128)(2,1)} %param.11) | copy-start | bytes 294916
  9.6 4.7 %copy-start.7 = (s32[2]{0:T(128)S(1)}, s32[2]{0:T(128)}, u32[]{:S(2)}) copy-start(s32[2]{0:T(128)} %param.13) | copy-start | bytes 28
  44.2 17.8 %all-to-all-start.1 = ((bf16[16,2,32,384]{3,2,1,0:T(8,128)(2,1)}), bf16[16,2,32,384]{3,2,1,0:T(8,128)(2,1)}, u32[]{:S(2)}, u32[]{:S(2)}) async-start(bf16[16,2,32,384]{3,2,1,0:T(8,128)(2,1)} %get-tuple-element.9), calls=%async_computation.1 | async-start | bytes 1572864 | tf_op jit(solution)/shard_map/all_to_all | solution.py:195
  48.5 39.1 %copy-start.4 = (f32[3072]{0:T(1024)S(1)}, f32[3072]{0:T(1024)}, u32[]{:S(2)}) copy-start(f32[3072]{0:T(1024)} %param.15) | copy-start | bytes 36868
  66.4 21.2 %copy-start.2 = (bf16[3072,512]{1,0:T(8,128)(2,1)S(1)}, bf16[3072,512]{1,0:T(8,128)(2,1)}, u32[]{:S(2)}) copy-start(bf16[3072,512]{1,0:T(8,128)(2,1)} %param.16) | copy-start | bytes 9437188
  86.7 0.9 copy-start.1
  86.9 0.7 copy-start.6
  88.9 8.2 %copy-start.5 = (s32[1,64,1]{1,2,0:T(1,128)S(1)}, s32[1,64,1]{1,2,0:T(1,128)}, u32[]{:S(2)}) copy-start(s32[1,64,1]{1,2,0:T(1,128)} %param.19) | copy-start | bytes 772
  93.2 15.2 %all-to-all-start.4 = ((bf16[8,64,384]{2,1,0:T(8,128)(2,1)}), bf16[8,64,384]{2,1,0:T(8,128)(2,1)S(1)}, u32[]{:S(2)}, u32[]{:S(2)}) async-start(bf16[8,64,384]{2,1,0:T(8,128)(2,1)} %bitcast.42), calls=%async_computation.4 | async-start | bytes 786432 | tf_op jit(solution)/shard_map/all_to_all | solution.py:219

commit v11 on v9

--- a/solution.py
+++ b/solution.py
@@ -163,6 +163,19 @@
     )(source_sum, source_stats, residual_rows)
 
 
+def copies_kernel(x_ref, out_ref):
+    x = x_ref[...]
+    for k in range(out_ref.shape[0]):
+        out_ref[k] = x
+
+
+def replicate(x, copies):
+    return pl.pallas_call(
+        copies_kernel,
+        out_shape=jax.ShapeDtypeStruct((copies,) + x.shape, x.dtype),
+    )(x)
+
+
 def normalize(features, norm_gain):
     values = features.astype(jnp.float32)
     mean_square = jnp.mean(values * values, axis=-1, keepdims=True)
@@ -176,9 +189,7 @@
     head_count = width_local // HEAD
     seq_index = lax.axis_index("seq")
     seq_count = lax.axis_size("seq")
-    all_queries = lax.all_to_all(
-        jnp.broadcast_to(queries[None], (seq_count,) + queries.shape), "seq", 0, 0, tiled=True
-    )
+    all_queries = lax.all_to_all(replicate(queries, seq_count), "seq", 0, 0, tiled=True)
     partial_sum, partial_stats = local_attention(all_queries, cache_kv, new_kv, cached_len, seq_index)
     source_sum = lax.all_to_all(partial_sum, "seq", 0, 0, tiled=True)
     source_stats = lax.all_to_all(partial_stats, "seq", 0, 0, tiled=True)

time: 123 us -> 123 us (level); the launches traced: 123 us -> 121 us
  Pallas kernels: 12.2 us -> 14.2 us
  local copies, waits for them, and re-layouts: 11.8 us -> 9.84 us
  blocking collectives: 48.4 us -> 46.7 us
    broadcast_in_dim x1 -> x0, local copies, waits for them, and re-layouts: 1.93 us -> none  [per_device(): jnp.broadcast_to(queries[None], (seq_count,) + queries.shape)]
    pallas_call x0 -> x1, Pallas kernels: none -> 1.93 us  [replicate(): pl.pallas_call(copies_kernel, out_shape=jax.ShapeDtypeStruct((copies,) +...]
    all_to_all x1, blocking collectives: 20.3 us -> 18.4 us  [per_device(): lax.all_to_all(outgoing.reshape(owner_count, slot_cap, width_local), ('re...]
where the time goes in v11:
time: 123 us; the launch traced here: 121 us
  blocking collectives  46.7 us (38%)
  waiting for transfers between devices  23.6 us (19%)
  starting transfers between devices  15.4 us (13%)
  Pallas kernels  14.2 us (12%)
  local copies, waits for them, and re-layouts  9.84 us (8%)
  other arithmetic  6.55 us (5%)
  matrix products  4.84 us (4%)
    all_to_all x1, blocking collectives, per_device(): lax.all_to_all(row_copies, 'tp', 0, 0, tiled=True).transpose(1, 0, 2)  19.3 us
    all_to_all x1, blocking collectives, per_device(): lax.all_to_all(outgoing.reshape(owner_count, slot_cap, width_local), ('re...  18.4 us
    all_to_all x1, blocking collectives, per_device(): source_stats = lax.all_to_all(partial_stats, 'seq', 0, 0, tiled=True)  9 us
    pallas_call x1, Pallas kernels, local_attention(): pl.pallas_call(kernel, grid_spec=grid_spec, out_shape=[jax.ShapeDtypeStru...  8.73 us
    all_to_all x1, waiting for transfers between devices, per_device(): source_sum = lax.all_to_all(partial_sum, 'seq', 0, 0, tiled=True)  8.08 us
    all_to_all x1, waiting for transfers between devices, per_device(): lax.all_to_all(replicate(queries, seq_count), 'seq', 0, 0, tiled=True)  7.99 us
    all_to_all x1, starting transfers between devices, per_device(): lax.all_to_all(replicate(queries, seq_count), 'seq', 0, 0, tiled=True)  7.62 us
    all_to_all x1, waiting for transfers between devices, per_device(): lax.all_to_all(pieces, 'tp', 0, 0, tiled=True).astype(jnp.float32)  7.56 us
  transfers between devices with their start and end apart: 3, of which 3 were waited for; matrix products, arithmetic and copies ran while one was open for 9% of the time, Pallas kernels for 0%

profile of v11, /device:TPU:1, one launch (start us, length us, event | category | flops | bytes accessed | tf_op | source)
XLA Modules:
  0.0 121.2 jit_solution(18275559729563237055)
XLA Ops:
  0.0 0.0 copy-start
  0.0 1.9 %shard_map.100 = bf16[16,2,32,384]{3,2,1,0:T(8,128)(2,1)} custom-call(bf16[2,32,384]{2,1,0:T(8,128)(2,1)} %x_ref.1), custom_call_target="tpu_custom_call" | custom-call | tf_op jit(solution)/shard_map/pallas_call | solution.py:173
  1.9 7.6 %all-to-all-start = ((bf16[16,2,32,384]{3,2,1,0:T(8,128)(2,1)}), bf16[16,2,32,384]{3,2,1,0:T(8,128)(2,1)}, u32[]{:S(2)}, u32[]{:S(2)}) async-start(bf16[16,2,32,384]{3,2,1,0:T(8,128)(2,1)} %shard_map.100), calls=%async_computation | async-start | bytes 1572864 | tf_op jit(solution)/shard_map/all_to_all | solution.py:192
  9.6 0.0 copy-start.3
  9.6 0.0 copy-start.7
  9.6 4.0 %copy.27 = bf16[2,1024,2,384]{3,1,2,0:T(8,128)(2,1)} copy(bf16[2,1024,2,384]{3,2,1,0:T(2,128)(2,1)} %param.12) | data formatting | bytes 6291456 | tf_op args[2]
  13.6 0.0 copy-done.3
  13.6 0.7 copy.29
  14.2 0.0 copy-done.7
  14.2 0.6 pad_add_fusion.meta_ref
  14.9 8.0 %all-to-all-done.q_ref = bf16[16,2,32,384]{3,2,1,0:T(8,128)(2,1)} async-done(((bf16[16,2,32,384]{3,2,1,0:T(8,128)(2,1)}), bf16[16,2,32,384]{3,2,1,0:T(8,128)(2,1)}, u32[]{:S(2)}, u32[]{:S(2)}) %all-to-all-start) | async-done | bytes 786464 | tf_op jit(solution)/shard_map/all_to_all | solution.py:192
  22.8 8.7 %shard_map.101 = (bf16[16,2,32,384]{3,2,1,0:T(8,128)(2,1)}, f32[16,2,32,8]{3,2,1,0:T(8,128)}) custom-call(s32[3]{0:T(128)} %pad_add_fusion.meta_ref, bf16[16,2,32,384]{3,2,1,0:T(8,128)(2,1)} %all-to-all-done.q_ref, bf16[2,2,1024,384]{3,2,1,0:T(8,128)(2,1)} %bitcast.36, bf16[2,2,1024,384]{3,2,1,0:T(8,128)(2,1)} %bitcast.37, bf16[2,2,32,384]{3,2,1,0:T(8,128)(2,1)} %bitcast.43, ...), custom_call_target="tpu_custom_call" | custom-call | tf_op jit(solution)/shard_map/pallas_call | solution.py:119
  31.6 1.2 %copy.18 = f32[16,2,32,8]{2,3,1,0:T(8,128)S(1)} copy(f32[16,2,32,8]{3,2,1,0:T(8,128)} %get-tuple-element.10) | data formatting | bytes 65536 | tf_op jit(solution)/shard_map/pallas_call | solution.py:119
  32.8 0.1 reshape.86
  32.9 9.0 %all_to_all.30 = f32[16,1,512]{2,1,0:T(1,128)S(1)} all-to-all(f32[16,1,512]{2,1,0:T(1,128)S(1)} %reshape.86), channel_id=1, replica_groups=mesh['req'=2,'seq'=16,'tp'=8] {'seq'}, dimensions={0} | all-to-all | bytes 65536 | tf_op jit(solution)/shard_map/all_to_all | solution.py:195
  41.9 4.3 %all-to-all-start.1 = ((bf16[16,2,32,384]{3,2,1,0:T(8,128)(2,1)}), bf16[16,2,32,384]{3,2,1,0:T(8,128)(2,1)}, u32[]{:S(2)}, u32[]{:S(2)}) async-start(bf16[16,2,32,384]{3,2,1,0:T(8,128)(2,1)} %get-tuple-element.9), calls=%async_computation.1 | async-start | bytes 1572864 | tf_op jit(solution)/shard_map/all_to_all | solution.py:194
  46.2 0.0 copy-start.4
  46.2 0.5 broadcast.56
  46.8 0.7 reduce.2
  47.5 0.1 reshape.87
  47.6 1.0 copy.19
  48.6 8.1 %all-to-all-done.1 = bf16[16,2,32,384]{3,2,1,0:T(8,128)(2,1)} async-done(((bf16[16,2,32,384]{3,2,1,0:T(8,128)(2,1)}), bf16[16,2,32,384]{3,2,1,0:T(8,128)(2,1)}, u32[]{:S(2)}, u32[]{:S(2)}) %all-to-all-start.1) | async-done | bytes 786464 | tf_op jit(solution)/shard_map/all_to_all | solution.py:194
  56.7 3.5 %shard_map.102 = (bf16[64,384]{1,0:T(8,128)(2,1)}, bf16[8,64,384]{2,1,0:T(8,128)(2,1)}) custom-call(bf16[16,64,384]{2,1,0:T(8,128)(2,1)} %bitcast.7.sum_ref, f32[16,64,8]{2,1,0:T(8,128)} %bitcast.40, bf16[64,384]{1,0:T(8,128)(2,1)} %bitcast.48), custom_call_target="tpu_custom_call" | custom-call | tf_op jit(solution)/shard_map/pallas_call | solution.py:157
  60.2 0.0 copy-start.2
  60.2 19.3 %all_to_all.31 = bf16[8,64,384]{2,1,0:T(8,128)(2,1)S(1)} all-to-all(bf16[8,64,384]{2,1,0:T(8,128)(2,1)} %get-tuple-element.12), channel_id=1, replica_groups=mesh['req'=2,'seq'=16,'tp'=8] {'tp'}, dimensions={0} | all-to-all | bytes 786432 | tf_op jit(solution)/shard_map/all_to_all | solution.py:205
  79.5 0.1 convert_bitcast_fusion
  79.5 0.1 copy.23
  79.6 0.0 copy-start.1
  79.6 0.2 fusion.1
  79.8 0.0 copy-start.6
  79.8 0.7 copy-done.1
  80.5 0.0 copy-done.6
  80.5 0.0 copy-done.4
  80.5 0.0 copy-done.2
  80.5 1.4 %fusion.13 = f32[64,512]{1,0:T(8,128)} fusion(bf16[3072,512]{1,0:T(8,128)(2,1)S(1)} %copy-done.2, f32[64,3072]{1,0:T(8,128)S(1)} %bitcast.38, f32[3072]{0:T(1024)S(1)} %copy-done.4, f32[64]{0:T(128)S(1)} %add_rsqrt_fusion), kind=kOutput, calls=%fused_computation.30 | convolution fusion | flops 201916416 | bytes 4075776 | tf_op jit(solution)/shard_map/dot_general | solution.py:212
  81.8 0.0 copy-done
  81.8 3.5 %convolution_convert_fusion = bf16[64,3072]{1,0:T(8,128)(2,1)S(1)} fusion(bf16[512,3072]{1,0:T(8,128)(2,1)S(1)} %copy-done, bf16[3072,512]{1,0:T(8,128)(2,1)} %param.17, f32[64,512]{1,0:T(8,128)} %fusion.13, f32[64,3072]{1,0:T(8,128)} %bitcast.39, f32[3072]{0:T(1024)S(1)} %copy-done.4, f32[64]{0:T(128)} %copy-done.6), kind=kOutput, calls=%fused_computation.1 | convolution fusion | flops 403636224 | bytes 7614720 | tf_op jit(solution)/shard_map/dot_general | solution.py:215
  85.3 0.8 copy.28
  86.1 3.5 %all-to-all-start.4 = ((bf16[8,64,384]{2,1,0:T(8,128)(2,1)}), bf16[8,64,384]{2,1,0:T(8,128)(2,1)S(1)}, u32[]{:S(2)}, u32[]{:S(2)}) async-start(bf16[8,64,384]{2,1,0:T(8,128)(2,1)} %bitcast.42), calls=%async_computation.4 | async-start | bytes 786432 | tf_op jit(solution)/shard_map/all_to_all | solution.py:218
  89.6 0.0 copy-done.5
  89.6 0.7 fusion.10
  90.3 1.4 %reduce_window_sum.11 = s32[64,32]{1,0:T(8,128)} reduce-window(s32[64,32]{1,0:T(8,128)} %fusion.10, s32[]{:T(128)} %constant.13.clone.1), window={size=64x1 pad=63_0x0_0}, to_apply=%region_0.0 | reduce-window | flops 129024 | bytes 16388 | tf_op jit(solution)/shard_map/jit(cumsum)/reduce_window_sum | solution.py:228
  91.7 0.9 select_reduce_fusion
  92.7 7.6 %all-to-all-done.4 = bf16[8,64,384]{2,1,0:T(8,128)(2,1)S(1)} async-done(((bf16[8,64,384]{2,1,0:T(8,128)(2,1)}), bf16[8,64,384]{2,1,0:T(8,128)(2,1)S(1)}, u32[]{:S(2)}, u32[]{:S(2)}) %all-to-all-start.4) | async-done | bytes 393248 | tf_op jit(solution)/shard_map/all_to_all | solution.py:218
  100.2 0.7 convert_reduce_fusion
  100.9 1.2 scatter_custom_fusion
  102.2 18.4 %all_to_all.32 = bf16[32,4,384]{2,1,0:T(4,128)(2,1)S(1)} all-to-all(bf16[32,4,384]{2,1,0:T(4,128)(2,1)S(1)} %reshape.73), channel_id=1, replica_groups=mesh['req'=2,'seq'=16,'tp'=8] {'req','seq'}, dimensions={0} | all-to-all | bytes 196608 | tf_op jit(solution)/shard_map/all_to_all | solution.py:234
  120.6 0.6 copy.31
  (4 shorter events, 0.0 us)
Async XLA Ops:
  0.0 81.8 %copy-start = (bf16[512,3072]{1,0:T(8,128)(2,1)S(1)}, bf16[512,3072]{1,0:T(8,128)(2,1)}, u32[]{:S(2)}) copy-start(bf16[512,3072]{1,0:T(8,128)(2,1)} %param.18) | copy-start | bytes 9437188
  1.9 20.9 %all-to-all-start = ((bf16[16,2,32,384]{3,2,1,0:T(8,128)(2,1)}), bf16[16,2,32,384]{3,2,1,0:T(8,128)(2,1)}, u32[]{:S(2)}, u32[]{:S(2)}) async-start(bf16[16,2,32,384]{3,2,1,0:T(8,128)(2,1)} %shard_map.100), calls=%async_computation | async-start | bytes 1572864 | tf_op jit(solution)/shard_map/all_to_all | solution.py:192
  9.6 4.0 %copy-start.3 = (bf16[2,32,2,384]{3,2,1,0:T(2,128)(2,1)S(1)}, bf16[2,32,2,384]{3,2,1,0:T(2,128)(2,1)}, u32[]{:S(2)}) copy-start(bf16[2,32,2,384]{3,2,1,0:T(2,128)(2,1)} %param.11) | copy-start | bytes 294916
  9.6 4.7 %copy-start.7 = (s32[2]{0:T(128)S(1)}, s32[2]{0:T(128)}, u32[]{:S(2)}) copy-start(s32[2]{0:T(128)} %param.13) | copy-start | bytes 28
  41.9 14.7 %all-to-all-start.1 = ((bf16[16,2,32,384]{3,2,1,0:T(8,128)(2,1)}), bf16[16,2,32,384]{3,2,1,0:T(8,128)(2,1)}, u32[]{:S(2)}, u32[]{:S(2)}) async-start(bf16[16,2,32,384]{3,2,1,0:T(8,128)(2,1)} %get-tuple-element.9), calls=%async_computation.1 | async-start | bytes 1572864 | tf_op jit(solution)/shard_map/all_to_all | solution.py:194
  46.2 34.2 %copy-start.4 = (f32[3072]{0:T(1024)S(1)}, f32[3072]{0:T(1024)}, u32[]{:S(2)}) copy-start(f32[3072]{0:T(1024)} %param.15) | copy-start | bytes 36868
  60.2 20.3 %copy-start.2 = (bf16[3072,512]{1,0:T(8,128)(2,1)S(1)}, bf16[3072,512]{1,0:T(8,128)(2,1)}, u32[]{:S(2)}) copy-start(bf16[3072,512]{1,0:T(8,128)(2,1)} %param.16) | copy-start | bytes 9437188
  79.6 0.9 copy-start.1
  79.8 0.7 copy-start.6
  81.8 7.7 %copy-start.5 = (s32[1,64,1]{1,2,0:T(1,128)S(1)}, s32[1,64,1]{1,2,0:T(1,128)}, u32[]{:S(2)}) copy-start(s32[1,64,1]{1,2,0:T(1,128)} %param.19) | copy-start | bytes 772
  86.1 14.1 %all-to-all-start.4 = ((bf16[8,64,384]{2,1,0:T(8,128)(2,1)}), bf16[8,64,384]{2,1,0:T(8,128)(2,1)S(1)}, u32[]{:S(2)}, u32[]{:S(2)}) async-start(bf16[8,64,384]{2,1,0:T(8,128)(2,1)} %bitcast.42), calls=%async_computation.4 | async-start | bytes 786432 | tf_op jit(solution)/shard_map/all_to_all | solution.py:218

commit v12 on v9

--- a/solution.py
+++ b/solution.py
@@ -131,13 +131,14 @@
     width = sum_ref.shape[-1]
     lane = lax.broadcasted_iota(jnp.int32, (1, width), 1)
     tiles = [jnp.zeros((sum_ref.shape[1], LANE), jnp.float32) for _ in range(width // LANE)]
+    peaks = stats[:, :, :heads]
+    scales = jnp.exp(peaks - jnp.max(peaks, axis=0)[None])
+    totals = jnp.sum(stats[:, :, heads:] * scales, axis=0)
     for h in range(heads):
         lo = h * HEAD // LANE * LANE
         hi = -(-(h + 1) * HEAD // LANE) * LANE
-        peak = stats[:, :, h:h + 1]
-        joint_peak = jnp.max(peak, axis=0)
-        scale = jnp.exp(peak - joint_peak[None])
-        total = jnp.sum(stats[:, :, heads + h:heads + h + 1] * scale, axis=0)
+        scale = scales[:, :, h:h + 1]
+        total = totals[:, h:h + 1]
         head_sum = jnp.sum(sum_ref[:, :, lo:hi].astype(jnp.float32) * scale, axis=0)
         value = head_sum / total
         for j in range(lo // LANE, hi // LANE):

time: 123 us -> 124 us (level)
  blocking collectives: 48.4 us -> 44.8 us
  Pallas kernels: 12.2 us -> 14.9 us
  waiting for transfers between devices: 23.6 us -> 25.1 us
    all_to_all x1, blocking collectives: 20.3 us -> 16.6 us  [per_device(): lax.all_to_all(outgoing.reshape(owner_count, slot_cap, width_local), ('re...]
    pallas_call x1, Pallas kernels: 8.73 us -> 11.9 us  [local_attention(): pl.pallas_call(kernel, grid_spec=grid_spec, out_shape=[jax.ShapeDtypeStru...]
    all_to_all x1, waiting for transfers between devices: 8.08 us -> 9.46 us  [per_device(): source_sum = lax.all_to_all(partial_sum, 'seq', 0, 0, tiled=True)]
where the time goes in v12:
time: 124 us; the launch traced here: 123 us
  blocking collectives  44.8 us (36%)
  waiting for transfers between devices  25.1 us (20%)
  starting transfers between devices  15.4 us (12%)
  Pallas kernels  14.9 us (12%)
  local copies, waits for them, and re-layouts  11.8 us (10%)
  other arithmetic  6.55 us (5%)
  matrix products  4.84 us (4%)
    all_to_all x1, blocking collectives, per_device(): lax.all_to_all(row_copies, 'tp', 0, 0, tiled=True).transpose(1, 0, 2)  19.1 us
    all_to_all x1, blocking collectives, per_device(): lax.all_to_all(outgoing.reshape(owner_count, slot_cap, width_local), ('re...  16.6 us
    pallas_call x1, Pallas kernels, local_attention(): pl.pallas_call(kernel, grid_spec=grid_spec, out_shape=[jax.ShapeDtypeStru...  11.9 us
    all_to_all x1, waiting for transfers between devices, per_device(): source_sum = lax.all_to_all(partial_sum, 'seq', 0, 0, tiled=True)  9.46 us
    all_to_all x1, blocking collectives, per_device(): source_stats = lax.all_to_all(partial_stats, 'seq', 0, 0, tiled=True)  9 us
    all_to_all x1, waiting for transfers between devices, per_device(): lax.all_to_all(jnp.broadcast_to(queries[None], (seq_count,) + queries.sha...  7.99 us
    all_to_all x1, waiting for transfers between devices, per_device(): lax.all_to_all(pieces, 'tp', 0, 0, tiled=True).astype(jnp.float32)  7.67 us
    all_to_all x1, starting transfers between devices, per_device(): lax.all_to_all(jnp.broadcast_to(queries[None], (seq_count,) + queries.sha...  7.62 us
  transfers between devices with their start and end apart: 3, of which 3 were waited for; matrix products, arithmetic and copies ran while one was open for 9% of the time, Pallas kernels for 0%

profile of v12, /device:TPU:1, one launch (start us, length us, event | category | flops | bytes accessed | tf_op | source)
XLA Modules:
  0.0 123.4 jit_solution(17528089524417868824)
XLA Ops:
  0.0 0.0 copy-start
  0.0 1.9 %broadcast_in_dim.5 = bf16[16,2,32,384]{3,2,1,0:T(8,128)(2,1)} broadcast(bf16[2,32,384]{2,1,0:T(8,128)(2,1)} %param.10), dimensions={1,2,3} | broadcast | bytes 835584 | tf_op jit(solution)/shard_map/broadcast_in_dim | solution.py:181
  1.9 7.6 %all-to-all-start = ((bf16[16,2,32,384]{3,2,1,0:T(8,128)(2,1)}), bf16[16,2,32,384]{3,2,1,0:T(8,128)(2,1)}, u32[]{:S(2)}, u32[]{:S(2)}) async-start(bf16[16,2,32,384]{3,2,1,0:T(8,128)(2,1)} %broadcast_in_dim.5), calls=%async_computation | async-start | bytes 1572864 | tf_op jit(solution)/shard_map/all_to_all | solution.py:180
  9.6 0.0 copy-start.3
  9.6 0.0 copy-start.7
  9.6 4.0 %copy.27 = bf16[2,1024,2,384]{3,1,2,0:T(8,128)(2,1)} copy(bf16[2,1024,2,384]{3,2,1,0:T(2,128)(2,1)} %param.12) | data formatting | bytes 6291456 | tf_op args[2]
  13.6 0.0 copy-done.3
  13.6 0.7 copy.29
  14.2 0.0 copy-done.7
  14.3 0.6 pad_add_fusion.meta_ref
  14.9 8.0 %all-to-all-done.q_ref = bf16[16,2,32,384]{3,2,1,0:T(8,128)(2,1)} async-done(((bf16[16,2,32,384]{3,2,1,0:T(8,128)(2,1)}), bf16[16,2,32,384]{3,2,1,0:T(8,128)(2,1)}, u32[]{:S(2)}, u32[]{:S(2)}) %all-to-all-start) | async-done | bytes 786464 | tf_op jit(solution)/shard_map/all_to_all | solution.py:180
  22.9 11.9 %shard_map.100 = (bf16[16,2,32,384]{3,2,1,0:T(8,128)(2,1)}, f32[16,2,32,8]{3,2,1,0:T(8,128)}) custom-call(s32[3]{0:T(128)} %pad_add_fusion.meta_ref, bf16[16,2,32,384]{3,2,1,0:T(8,128)(2,1)} %all-to-all-done.q_ref, bf16[2,2,1024,384]{3,2,1,0:T(8,128)(2,1)} %bitcast.36, bf16[2,2,1024,384]{3,2,1,0:T(8,128)(2,1)} %bitcast.37, bf16[2,2,32,384]{3,2,1,0:T(8,128)(2,1)} %bitcast.43, ...), custom_call_target="tpu_custom_call" | custom-call | tf_op jit(solution)/shard_map/pallas_call | solution.py:119
  34.8 1.2 copy.18
  36.0 0.1 reshape.87
  36.1 9.0 %all_to_all.30 = f32[16,1,512]{2,1,0:T(1,128)S(1)} all-to-all(f32[16,1,512]{2,1,0:T(1,128)S(1)} %reshape.87), channel_id=1, replica_groups=mesh['req'=2,'seq'=16,'tp'=8] {'seq'}, dimensions={0} | all-to-all | bytes 65536 | tf_op jit(solution)/shard_map/all_to_all | solution.py:185
  45.1 4.3 %all-to-all-start.1 = ((bf16[16,2,32,384]{3,2,1,0:T(8,128)(2,1)}), bf16[16,2,32,384]{3,2,1,0:T(8,128)(2,1)}, u32[]{:S(2)}, u32[]{:S(2)}) async-start(bf16[16,2,32,384]{3,2,1,0:T(8,128)(2,1)} %get-tuple-element.9), calls=%async_computation.1 | async-start | bytes 1572864 | tf_op jit(solution)/shard_map/all_to_all | solution.py:184
  49.4 0.0 copy-start.4
  49.4 0.5 broadcast.57
  49.9 0.7 reduce.2
  50.7 0.1 reshape.88
  50.8 1.0 copy.19
  51.8 9.5 %all-to-all-done.1 = bf16[16,2,32,384]{3,2,1,0:T(8,128)(2,1)} async-done(((bf16[16,2,32,384]{3,2,1,0:T(8,128)(2,1)}), bf16[16,2,32,384]{3,2,1,0:T(8,128)(2,1)}, u32[]{:S(2)}, u32[]{:S(2)}) %all-to-all-start.1) | async-done | bytes 786464 | tf_op jit(solution)/shard_map/all_to_all | solution.py:184
  61.2 3.0 %shard_map.101 = (bf16[64,384]{1,0:T(8,128)(2,1)}, bf16[8,64,384]{2,1,0:T(8,128)(2,1)}) custom-call(bf16[16,64,384]{2,1,0:T(8,128)(2,1)} %bitcast.7.sum_ref, f32[16,64,8]{2,1,0:T(8,128)} %bitcast.40, bf16[64,384]{1,0:T(8,128)(2,1)} %bitcast.48), custom_call_target="tpu_custom_call" | custom-call | tf_op jit(solution)/shard_map/pallas_call | solution.py:158
  64.2 0.0 copy-start.2
  64.2 19.1 %all_to_all.31 = bf16[8,64,384]{2,1,0:T(8,128)(2,1)S(1)} all-to-all(bf16[8,64,384]{2,1,0:T(8,128)(2,1)} %get-tuple-element.12), channel_id=1, replica_groups=mesh['req'=2,'seq'=16,'tp'=8] {'tp'}, dimensions={0} | all-to-all | bytes 786432 | tf_op jit(solution)/shard_map/all_to_all | solution.py:195
  83.3 0.1 convert_bitcast_fusion
  83.4 0.1 copy.23
  83.5 0.0 copy-start.1
  83.5 0.2 fusion.1
  83.7 0.7 copy-done.1
  84.3 0.0 copy-done.6
  84.3 0.0 copy-done.4
  84.3 0.0 copy-done.2
  84.3 1.4 %fusion.13 = f32[64,512]{1,0:T(8,128)} fusion(bf16[3072,512]{1,0:T(8,128)(2,1)S(1)} %copy-done.2, f32[64,3072]{1,0:T(8,128)S(1)} %bitcast.38, f32[3072]{0:T(1024)S(1)} %copy-done.4, f32[64]{0:T(128)S(1)} %add_rsqrt_fusion), kind=kOutput, calls=%fused_computation.30 | convolution fusion | flops 201916416 | bytes 4075776 | tf_op jit(solution)/shard_map/dot_general | solution.py:202
  85.7 0.0 copy-done
  85.7 0.0 copy-start.5
  85.7 3.5 %convolution_convert_fusion = bf16[64,3072]{1,0:T(8,128)(2,1)S(1)} fusion(bf16[512,3072]{1,0:T(8,128)(2,1)S(1)} %copy-done, bf16[3072,512]{1,0:T(8,128)(2,1)} %param.17, f32[64,512]{1,0:T(8,128)} %fusion.13, f32[64,3072]{1,0:T(8,128)} %bitcast.39, f32[3072]{0:T(1024)S(1)} %copy-done.4, f32[64]{0:T(128)} %copy-done.6), kind=kOutput, calls=%fused_computation.1 | convolution fusion | flops 403636224 | bytes 7614720 | tf_op jit(solution)/shard_map/dot_general | solution.py:205
  89.2 0.8 copy.28
  90.0 3.5 %all-to-all-start.4 = ((bf16[8,64,384]{2,1,0:T(8,128)(2,1)}), bf16[8,64,384]{2,1,0:T(8,128)(2,1)S(1)}, u32[]{:S(2)}, u32[]{:S(2)}) async-start(bf16[8,64,384]{2,1,0:T(8,128)(2,1)} %bitcast.42), calls=%async_computation.4 | async-start | bytes 786432 | tf_op jit(solution)/shard_map/all_to_all | solution.py:208
  93.4 0.0 copy-done.5
  93.5 0.7 fusion.10
  94.1 1.4 %reduce_window_sum.11 = s32[64,32]{1,0:T(8,128)} reduce-window(s32[64,32]{1,0:T(8,128)} %fusion.10, s32[]{:T(128)} %constant.13.clone.1), window={size=64x1 pad=63_0x0_0}, to_apply=%region_0.0 | reduce-window | flops 129024 | bytes 16388 | tf_op jit(solution)/shard_map/jit(cumsum)/reduce_window_sum | solution.py:218
  95.6 0.9 select_reduce_fusion
  96.5 7.7 %all-to-all-done.4 = bf16[8,64,384]{2,1,0:T(8,128)(2,1)S(1)} async-done(((bf16[8,64,384]{2,1,0:T(8,128)(2,1)}), bf16[8,64,384]{2,1,0:T(8,128)(2,1)S(1)}, u32[]{:S(2)}, u32[]{:S(2)}) %all-to-all-start.4) | async-done | bytes 393248 | tf_op jit(solution)/shard_map/all_to_all | solution.py:208
  104.2 0.7 convert_reduce_fusion
  104.9 1.2 scatter_custom_fusion
  106.1 16.6 %all_to_all.32 = bf16[32,4,384]{2,1,0:T(4,128)(2,1)S(1)} all-to-all(bf16[32,4,384]{2,1,0:T(4,128)(2,1)S(1)} %reshape.74), channel_id=1, replica_groups=mesh['req'=2,'seq'=16,'tp'=8] {'req','seq'}, dimensions={0} | all-to-all | bytes 196608 | tf_op jit(solution)/shard_map/all_to_all | solution.py:224
  122.8 0.6 copy.31
  (4 shorter events, 0.0 us)
Async XLA Ops:
  0.0 85.7 %copy-start = (bf16[512,3072]{1,0:T(8,128)(2,1)S(1)}, bf16[512,3072]{1,0:T(8,128)(2,1)}, u32[]{:S(2)}) copy-start(bf16[512,3072]{1,0:T(8,128)(2,1)} %param.18) | copy-start | bytes 9437188
  1.9 20.9 %all-to-all-start = ((bf16[16,2,32,384]{3,2,1,0:T(8,128)(2,1)}), bf16[16,2,32,384]{3,2,1,0:T(8,128)(2,1)}, u32[]{:S(2)}, u32[]{:S(2)}) async-start(bf16[16,2,32,384]{3,2,1,0:T(8,128)(2,1)} %broadcast_in_dim.5), calls=%async_computation | async-start | bytes 1572864 | tf_op jit(solution)/shard_map/all_to_all | solution.py:180
  9.6 4.0 %copy-start.3 = (bf16[2,32,2,384]{3,2,1,0:T(2,128)(2,1)S(1)}, bf16[2,32,2,384]{3,2,1,0:T(2,128)(2,1)}, u32[]{:S(2)}) copy-start(bf16[2,32,2,384]{3,2,1,0:T(2,128)(2,1)} %param.11) | copy-start | bytes 294916
  9.6 4.7 %copy-start.7 = (s32[2]{0:T(128)S(1)}, s32[2]{0:T(128)}, u32[]{:S(2)}) copy-start(s32[2]{0:T(128)} %param.13) | copy-start | bytes 28
  45.1 16.1 %all-to-all-start.1 = ((bf16[16,2,32,384]{3,2,1,0:T(8,128)(2,1)}), bf16[16,2,32,384]{3,2,1,0:T(8,128)(2,1)}, u32[]{:S(2)}, u32[]{:S(2)}) async-start(bf16[16,2,32,384]{3,2,1,0:T(8,128)(2,1)} %get-tuple-element.9), calls=%async_computation.1 | async-start | bytes 1572864 | tf_op jit(solution)/shard_map/all_to_all | solution.py:184
  49.4 34.9 %copy-start.4 = (f32[3072]{0:T(1024)S(1)}, f32[3072]{0:T(1024)}, u32[]{:S(2)}) copy-start(f32[3072]{0:T(1024)} %param.15) | copy-start | bytes 36868
  64.2 20.1 %copy-start.2 = (bf16[3072,512]{1,0:T(8,128)(2,1)S(1)}, bf16[3072,512]{1,0:T(8,128)(2,1)}, u32[]{:S(2)}) copy-start(bf16[3072,512]{1,0:T(8,128)(2,1)} %param.16) | copy-start | bytes 9437188
  83.5 0.9 copy-start.1
  83.7 0.7 copy-start.6
  85.7 7.7 %copy-start.5 = (s32[1,64,1]{1,2,0:T(1,128)S(1)}, s32[1,64,1]{1,2,0:T(1,128)}, u32[]{:S(2)}) copy-start(s32[1,64,1]{1,2,0:T(1,128)} %param.19) | copy-start | bytes 772
  90.0 14.2 %all-to-all-start.4 = ((bf16[8,64,384]{2,1,0:T(8,128)(2,1)}), bf16[8,64,384]{2,1,0:T(8,128)(2,1)S(1)}, u32[]{:S(2)}, u32[]{:S(2)}) async-start(bf16[8,64,384]{2,1,0:T(8,128)(2,1)} %bitcast.42), calls=%async_computation.4 | async-start | bytes 786432 | tf_op jit(solution)/shard_map/all_to_all | solution.py:208
